TPU v7x, 32 devices: a whole 2x2x4 slice. The times are simulated.
32 devices in a mesh: group: 2 (over y), head: 4 (over x, core), seq: 4 (over z).
Axes of the slice: x: 2, y: 2, z: 4, core: 2. Of those that a mesh axis runs over, the one named last changes fastest.
Arguments:
- new_queries: bfloat16 [512, 4096], P(('group', 'seq'), 'head'), parts along dimension 0, may hold values from -80 to 80
- new_keys: bfloat16 [512, 1024], P(('group', 'seq'), 'head'), parts along dimension 0, may hold values from -6 to 6
- new_values: bfloat16 [512, 1024], P(('group', 'seq'), 'head'), parts along dimension 0, may hold values from -6 to 6
- cache_keys: bfloat16 [8192, 1024], P(('group', 'seq'), 'head'), parts along dimension 0, may hold values from -5 to 5
- cache_values: bfloat16 [8192, 1024], P(('group', 'seq'), 'head'), parts along dimension 0, may hold values from -6 to 6
- segment_ids: int32 [512], P('group'), parts along dimension 0, may hold values from 0 to 7, as said below
- cache_length: int32 [2], P('group'), parts along dimension 0, may hold values from 512 to 4096
Outputs:
- attended: bfloat16 [512, 4096], P(('group', 'seq'), 'head'), parts along dimension 0
There are 2 independent parts, one for each index of `group`. A program takes and returns all parts, laid end to end along the dimension named above; each array names one. Nothing has to cross between parts.
Inputs may be any that keep to these rules, and one draw needn't show every extreme that they name: `segment_ids`: Non-decreasing along the positions; every number of 0 to 7 appears.
All inputs are finite; a program needn't handle non-finite values.
Results may differ from a plain program's by a relative error of at most 0.0024.
Values may be sent and summed in bfloat16 or wider, within the bound.
No kernel may reach another device: no remote copies, remote signals or barrier semaphores. Data moves between devices by JAX's collectives and lax.ppermute only.
A program may use at most 64 MiB of HBM per device.

v0:
```python
import jax
import jax.numpy as jnp
from jax import lax
from jax.sharding import PartitionSpec as P

HEAD_DIM = 128


NEG_FILL = -1e30


def on_device(
    new_queries, new_keys, new_values, cache_keys, cache_values, segment_ids, cache_length
):
    head_size = HEAD_DIM
    own_count = new_queries.shape[0]
    join_rows = segment_ids.shape[0]
    cache_rows = cache_keys.shape[0]
    heads_kv = cache_keys.shape[1] // head_size
    heads_q = new_queries.shape[1] // head_size
    group_size = heads_q // heads_kv
    seq_count = lax.axis_size("seq")
    seq_rank = lax.axis_index("seq")
    score_scale = head_size ** (-0.5)
    cache_limit = cache_length[0]
    all_queries, all_keys, all_values = (
        lax.all_gather(new_queries, "seq", axis=0, tiled=True),
        lax.all_gather(new_keys, "seq", axis=0, tiled=True),
        lax.all_gather(new_values, "seq", axis=0, tiled=True),
    )
    keys_here, values_here = (cache_keys, cache_values)
    live_rows = jnp.clip(cache_limit - seq_rank * cache_rows, 0, cache_rows)
    tile_width = min(cache_rows // seq_count, 256)
    block_rows = min(256, cache_rows)
    tiles_per_block = block_rows // tile_width
    block_total = (live_rows + block_rows - 1) // block_rows
    keys_tiled = keys_here.reshape(cache_rows, heads_kv, head_size)
    values_tiled = values_here.reshape(cache_rows, heads_kv, head_size)
    query_block = min(64, join_rows)
    grouped = all_queries.reshape(
        join_rows // query_block, query_block, heads_kv, group_size, head_size
    )

    def one_block(block_queries):

        def step_pass(block_index, running):
            best, numer_acc, denom_acc = running
            start = block_index * block_rows
            key_tile = lax.dynamic_slice_in_dim(keys_tiled, start, block_rows, 0)
            scores = (
                jnp.einsum(
                    "cgrd,tgd->cgrt", block_queries, key_tile, preferred_element_type=jnp.float32
                )
                * score_scale
            )
            usable = (start + jnp.arange(block_rows, dtype=jnp.int32) < live_rows).reshape(
                tiles_per_block, tile_width
            )
            split = scores.reshape(query_block, heads_kv, group_size, tiles_per_block, tile_width)
            tile_max = jnp.max(jnp.where(usable, split, NEG_FILL), axis=-1)
            weights = jnp.exp(jnp.where(usable, split - tile_max[..., None], NEG_FILL)).astype(
                jnp.bfloat16
            )
            value_tile = lax.dynamic_slice_in_dim(values_tiled, start, block_rows, 0).reshape(
                tiles_per_block, tile_width, heads_kv, head_size
            )
            tile_numer = jnp.einsum(
                "cgrbt,btgd->cgrbd", weights, value_tile, preferred_element_type=jnp.float32
            )
            tile_denom = jnp.sum(weights.astype(jnp.float32), axis=-1)
            new_best = jnp.maximum(best, jnp.max(tile_max, axis=-1))
            keep = jnp.exp(best - new_best)
            factor = jnp.exp(tile_max - new_best[..., None])
            numer_acc = numer_acc * keep[..., None] + jnp.sum(
                tile_numer * factor[..., None], axis=3
            )
            denom_acc = denom_acc * keep + jnp.sum(tile_denom * factor, axis=-1)
            return (new_best, numer_acc, denom_acc)

        start_state = (
            jnp.full((query_block, heads_kv, group_size), NEG_FILL, jnp.float32),
            jnp.zeros((query_block, heads_kv, group_size, head_size), jnp.float32),
            jnp.zeros((query_block, heads_kv, group_size), jnp.float32),
        )
        return lax.fori_loop(0, block_total, step_pass, start_state)

    block_best, block_numer, block_denom = lax.map(one_block, grouped)
    cache_max = block_best.reshape(join_rows, heads_kv, group_size)
    cache_numer = block_numer.reshape(join_rows, heads_kv, group_size, head_size)
    cache_denom = block_denom.reshape(join_rows, heads_kv, group_size)
    own_queries = new_queries.reshape(own_count, heads_kv, group_size, head_size)
    fresh_scores = (
        jnp.einsum(
            "cgrd,tgd->cgrt",
            own_queries,
            all_keys.reshape(join_rows, heads_kv, head_size),
            preferred_element_type=jnp.float32,
        )
        * score_scale
    )
    start_row = seq_rank * own_count
    own_positions = start_row + jnp.arange(own_count, dtype=jnp.int32)
    own_segments = lax.dynamic_slice_in_dim(segment_ids, start_row, own_count, 0)
    key_positions = jnp.arange(join_rows, dtype=jnp.int32)
    allowed = (key_positions[None, :] <= own_positions[:, None]) & (
        segment_ids[None, :] == own_segments[:, None]
    )
    allowed = allowed[:, None, None, :]
    fresh_max = jnp.max(jnp.where(allowed, fresh_scores, NEG_FILL), axis=-1)
    zero_index = jnp.zeros((), jnp.int32)
    merged = lax.dynamic_update_slice(
        cache_max,
        jnp.maximum(lax.dynamic_slice_in_dim(cache_max, start_row, own_count, 0), fresh_max),
        (start_row, zero_index, zero_index),
    )
    row_max = (
        lax.pmax(merged.reshape(join_rows, heads_q).astype(jnp.bfloat16), "seq")
        .astype(jnp.float32)
        .reshape(join_rows, heads_kv, group_size)
    )
    rescale = jnp.exp(cache_max - row_max)
    scaled_numer = (cache_numer * rescale[..., None]).reshape(join_rows, heads_q * head_size)
    scaled_denom = (cache_denom * rescale).reshape(join_rows, heads_q)
    own_numer, own_denom = (
        lax.psum_scatter(scaled_numer, "seq", scatter_dimension=0, tiled=True),
        lax.psum_scatter(scaled_denom, "seq", scatter_dimension=0, tiled=True),
    )
    own_max = lax.dynamic_slice_in_dim(row_max, start_row, own_count, 0)
    fresh_weights = jnp.exp(
        jnp.where(allowed, fresh_scores - fresh_max[..., None], NEG_FILL)
    ).astype(jnp.bfloat16)
    fresh_factor = jnp.exp(fresh_max - own_max)
    fresh_numer = (
        jnp.einsum(
            "cgrt,tgd->cgrd",
            fresh_weights,
            all_values.reshape(join_rows, heads_kv, head_size),
            preferred_element_type=jnp.float32,
        )
        * fresh_factor[..., None]
    )
    fresh_denom = jnp.sum(fresh_weights.astype(jnp.float32), axis=-1) * fresh_factor
    total_numer = own_numer + fresh_numer.reshape(own_count, heads_q * head_size)
    total_denom = own_denom + fresh_denom.reshape(own_count, heads_q)
    attended = total_numer.reshape(own_count, heads_q, head_size) / total_denom[..., None]
    return attended.reshape(own_count, heads_q * head_size).astype(jnp.bfloat16)


def solution(mesh):
    placed = (
        P(("group", "seq"), "head"),
        P(("group", "seq"), "head"),
        P(("group", "seq"), "head"),
        P(("group", "seq"), "head"),
        P(("group", "seq"), "head"),
        P("group"),
        P("group"),
    )
    return jax.shard_map(
        on_device,
        mesh=mesh,
        in_specs=placed,
        out_specs=P(("group", "seq"), "head"),
        check_vma=False,
    )
```

profile of v0, /device:TPU:0, one launch (start us, length us, event | category | flops | bytes accessed | tf_op | source)
XLA Modules:
  0.0 125.5 jit_solution(12809682222911493052)
XLA Ops:
  7.2 17.6 %all_gather.9 = bf16[256,1024]{1,0:T(8,128)(2,1)S(1)} all-gather(bf16[64,1024]{1,0:T(8,128)(2,1)} %param.11), channel_id=1, replica_groups=mesh['group'=2,'head'=4,'seq'=4] {'seq'}, dimensions={0}, use_global_device_ids=true | all-gather | bytes 655360 | tf_op jit(solution)/shard_map/all_gather | solution.py:27
  24.8 0.4 reshape.144
  25.2 0.7 copy-done.1
  26.3 1.3 copy.30
  27.9 18.3 %while.29 = (s32[]{:T(128)}, f32[4,64,2,4]{1,0,3,2:T(4,128)S(1)}, f32[4,64,2,4,128]{4,3,2,1,0:T(4,128)S(1)}, f32[4,64,2,4]{1,0,3,2:T(4,128)S(1)}, bf16[4,64,2,4,...) while((s32[]{:T(128)}, f32[4,64,2,4]{1,0,3,2:T(4,128)S(1)}, ...), condition=%wide.region_5.6_spmd, body=%wide.region_0.5_spmd.sunk | while | flops 68749824 | bytes 3850228 | solution.py:87
  28.0 4.1 %while.30 = (s32[]{:T(128)}, f32[64,2,4]{0,2,1:T(4,128)S(1)}, f32[64,2,4,128]{3,0,2,1:T(8,128)S(1)}, f32[64,2,4]{0,2,1:T(4,128)S(1)}, s32[]{:T(128)}, /*index=5*...) while((s32[]{:T(128)}, f32[64,2,4]{0,2,1:T(4,128)S(1)}, ...), condition=%wide.region_4.4_spmd, body=%wide.region_1.3_spmd.sunk | while | flops 68749824 | bytes 2526915 | solution.py:85
  28.1 0.3 select_reduce_fusion.3
  28.4 0.3 convert_reduce_fusion.3
  28.7 0.3 fusion.26
  29.1 0.3 select_reduce_fusion.3
  29.4 0.3 convert_reduce_fusion.3
  29.7 0.4 fusion.26
  30.1 0.3 select_reduce_fusion.3
  30.4 0.3 convert_reduce_fusion.3
  30.7 0.3 fusion.26
  31.1 0.3 select_reduce_fusion.3
  31.5 0.3 convert_reduce_fusion.3
  31.8 0.4 fusion.26
  32.6 4.1 %while.30 = (s32[]{:T(128)}, f32[64,2,4]{0,2,1:T(4,128)S(1)}, f32[64,2,4,128]{3,0,2,1:T(8,128)S(1)}, f32[64,2,4]{0,2,1:T(4,128)S(1)}, s32[]{:T(128)}, /*index=5*...) while((s32[]{:T(128)}, f32[64,2,4]{0,2,1:T(4,128)S(1)}, ...), condition=%wide.region_4.4_spmd, body=%wide.region_1.3_spmd.sunk | while | flops 68749824 | bytes 2526915 | solution.py:85
  32.6 0.3 select_reduce_fusion.3
  32.9 0.3 convert_reduce_fusion.3
  33.3 0.4 fusion.26
  33.6 0.3 select_reduce_fusion.3
  34.3 0.3 fusion.26
  34.7 0.3 select_reduce_fusion.3
  35.3 0.4 fusion.26
  35.7 0.3 select_reduce_fusion.3
  36.3 0.3 fusion.26
  37.1 4.1 %while.30 = (s32[]{:T(128)}, f32[64,2,4]{0,2,1:T(4,128)S(1)}, f32[64,2,4,128]{3,0,2,1:T(8,128)S(1)}, f32[64,2,4]{0,2,1:T(4,128)S(1)}, s32[]{:T(128)}, /*index=5*...) while((s32[]{:T(128)}, f32[64,2,4]{0,2,1:T(4,128)S(1)}, ...), condition=%wide.region_4.4_spmd, body=%wide.region_1.3_spmd.sunk | while | flops 68749824 | bytes 2526915 | solution.py:85
  37.2 0.3 select_reduce_fusion.3
  37.5 0.3 convert_reduce_fusion.3
  37.8 0.4 fusion.26
  38.2 0.3 select_reduce_fusion.3
  38.8 0.3 fusion.26
  39.2 0.3 select_reduce_fusion.3
  39.9 0.4 fusion.26
  40.3 0.3 select_reduce_fusion.3
  40.9 0.3 fusion.26
  41.7 4.1 %while.30 = (s32[]{:T(128)}, f32[64,2,4]{0,2,1:T(4,128)S(1)}, f32[64,2,4,128]{3,0,2,1:T(8,128)S(1)}, f32[64,2,4]{0,2,1:T(4,128)S(1)}, s32[]{:T(128)}, /*index=5*...) while((s32[]{:T(128)}, f32[64,2,4]{0,2,1:T(4,128)S(1)}, ...), condition=%wide.region_4.4_spmd, body=%wide.region_1.3_spmd.sunk | while | flops 68749824 | bytes 2526915 | solution.py:85
  41.7 0.3 select_reduce_fusion.3
  42.4 0.4 fusion.26
  42.8 0.3 select_reduce_fusion.3
  43.4 0.3 fusion.26
  43.8 0.3 select_reduce_fusion.3
  44.4 0.4 fusion.26
  44.8 0.3 select_reduce_fusion.3
  45.5 0.3 fusion.26
  46.5 0.7 copy-done.3
  47.1 13.3 %all_gather.10 = bf16[256,256]{1,0:T(8,128)(2,1)S(1)} all-gather(bf16[64,256]{1,0:T(8,128)(2,1)S(1)} %copy-done.3), channel_id=1, replica_groups=mesh['group'=2,'head'=4,'seq'=4] {'seq'}, dimensions={0}, use_global_device_ids=true | all-gather | bytes 163840 | tf_op jit(solution)/shard_map/all_gather | solution.py:28
  60.6 0.7 copy-done.5
  61.4 0.3 select_reduce_fusion.1
  62.0 8.7 %pmax.7 = bf16[256,8]{0,1:T(8,128)(2,1)S(1)} all-reduce(bf16[256,8]{0,1:T(8,128)(2,1)S(1)} %convert_element_type.27), channel_id=1, replica_groups=mesh['group'=2,'head'=4,'seq'=4] {'seq'}, use_global_device_ids=true, to_apply=%region_7.8 | all-reduce | flops 2048 | bytes 8192 | tf_op jit(solution)/shard_map/pmax | solution.py:117
  70.7 0.8 copy.54
  71.6 0.4 reshape.147
  72.2 1.6 %mul.74 = f32[256,2,4,128]{3,2,1,0:T(4,128)} broadcast(f32[256,2,4]{2,1,0:T(2,128)S(1)} %copy.39), dimensions={0,1,2} | broadcast | bytes 1056768 | tf_op jit(solution)/shard_map/mul | solution.py:122
  73.8 1.6 %mul.75 = f32[256,1024]{1,0:T(8,128)S(1)} reshape(f32[256,2,4,128]{3,2,1,0:T(4,128)} %mul.74) | data formatting | bytes 2097152 | tf_op jit(solution)/shard_map/mul | solution.py:122
  75.4 1.2 mul.76
  76.6 0.7 copy-done.4
  77.3 13.4 %all_gather.11 = bf16[256,256]{1,0:T(8,128)(2,1)S(1)} all-gather(bf16[64,256]{1,0:T(8,128)(2,1)S(1)} %copy-done.4), channel_id=1, replica_groups=mesh['group'=2,'head'=4,'seq'=4] {'seq'}, dimensions={0}, use_global_device_ids=true | all-gather | bytes 163840 | tf_op jit(solution)/shard_map/all_gather | solution.py:29
  91.2 0.3 fusion.12
  91.9 0.8 copy.55
  92.8 24.2 %reduce-scatter.5.cloned.1.call-done = f32[64,1024]{1,0:T(8,128)} async-done(((f32[256,1024]{1,0:T(8,128)}), f32[64,1024]{1,0:T(8,128)}) %reduce-scatter.5.cloned.1.call-update) | async-done | bytes 262160 | tf_op jit(solution)/shard_map/reduce_scatter | solution.py:125
  117.1 0.8 copy-done.2
  118.0 0.7 fusion.13
  (117 shorter events, 7.5 us)
Async XLA Ops:
  6.5 85.3 %reduce-scatter.7.cloned.1.call-start = ((), (), s32[]{:S(2)}) async-start(), calls=%async_computation.3 | async-start | bytes 163840
  24.8 1.0 copy-start.1
  27.9 18.4 %copy-start = (bf16[64,1024]{1,0:T(8,128)(2,1)S(1)}, bf16[64,1024]{1,0:T(8,128)(2,1)}, u32[]{:S(2)}) copy-start(bf16[64,1024]{1,0:T(8,128)(2,1)} %param.11) | copy-start | bytes 393220
  46.4 0.8 copy-start.3
  60.6 0.7 copy-start.5
  71.5 45.5 %reduce-scatter.5.cloned.1.call-start = ((), (), s32[]{:S(2)}) async-start(), calls=%async_computation.2 | async-start | bytes 1310720 | tf_op jit(solution)/shard_map/reduce_scatter | solution.py:125
  76.6 0.8 copy-start.4
  117.0 0.9 copy-start.2
Sparse Core Ops, SparseCore 0:
  71.6 17.5 reduce-scatter.6
  91.6 25.3 reduce-scatter.4
where the time goes:
time: 128 us; the launch traced here: 126 us
  blocking collectives  53 us (41%)
  waiting for transfers between devices  24.3 us (19%)
  between operations  14.3 us (11%)
  local copies, waits for them, and re-layouts  14.1 us (11%)
  matrix products  11.4 us (9%)
  other arithmetic  7.33 us (6%)
    reduce_scatter x1, waiting for transfers between devices, on_device(): lax.psum_scatter(scaled_numer, 'seq', scatter_dimension=0, tiled=True)  24.2 us
    all_gather x1, blocking collectives, on_device(): lax.all_gather(new_queries, 'seq', axis=0, tiled=True)  17.6 us
    all_gather x1, blocking collectives, on_device(): lax.all_gather(new_values, 'seq', axis=0, tiled=True)  13.4 us
    all_gather x1, blocking collectives, on_device(): lax.all_gather(new_keys, 'seq', axis=0, tiled=True)  13.3 us
    pmax x1, blocking collectives, on_device(): lax.pmax(merged.reshape(join_rows, heads_q).astype(jnp.bfloat16), 'seq')  8.67 us
    unnamed x17, local copies, waits for them, and re-layouts  6.63 us
    dot_general x16, matrix products, step_pass(): jnp.einsum('cgrbt,btgd->cgrbd', weights, value_tile, preferred_element_ty...  5.59 us
    dot_general x16, matrix products, step_pass(): jnp.einsum('cgrd,tgd->cgrt', block_queries, key_tile, preferred_element_t...  5.24 us
  transfers between devices with their start and end apart: 2, of which 1 were waited for; matrix products, arithmetic and copies ran while one was open for 6% of the time, Pallas kernels for 0%

commit v1 on v0

v1 whole, which is shorter than its diff:
```python
import functools

import jax
import jax.numpy as jnp
from jax import lax
from jax.experimental import pallas as pl
from jax.experimental.pallas import tpu as pltpu
from jax.sharding import PartitionSpec as P

HEAD_DIM = 128
SUB = 256
NEG_FILL = -1e30


def cache_kernel(live_ref, q_ref, k_ref, v_ref, out_ref):
    live = live_ref[0]
    rows = q_ref.shape[0]
    heads_q = q_ref.shape[1] // HEAD_DIM
    heads_kv = k_ref.shape[1] // HEAD_DIM
    group = heads_q // heads_kv
    tiles = k_ref.shape[0] // SUB
    scale = HEAD_DIM ** (-0.5)
    col = lax.broadcasted_iota(jnp.int32, (rows, SUB), 1)
    lane = lax.broadcasted_iota(jnp.int32, (rows, 128), 1)
    extra = jnp.zeros((rows, 128), jnp.float32)
    for h in range(heads_q):
        g = h // group
        qh = q_ref[:, h * HEAD_DIM:(h + 1) * HEAD_DIM]
        maxes, numers, denoms = [], [], []
        for b in range(tiles):
            kb = k_ref[b * SUB:(b + 1) * SUB, g * HEAD_DIM:(g + 1) * HEAD_DIM]
            s = lax.dot_general(
                qh, kb, (((1,), (1,)), ((), ())), preferred_element_type=jnp.float32
            ) * scale
            ok = (col + b * SUB) < live
            tm = jnp.max(jnp.where(ok, s, NEG_FILL), axis=1, keepdims=True)
            w = jnp.exp(jnp.where(ok, s - tm, NEG_FILL)).astype(jnp.bfloat16)
            vb = v_ref[b * SUB:(b + 1) * SUB, g * HEAD_DIM:(g + 1) * HEAD_DIM]
            numers.append(jnp.dot(w, vb, preferred_element_type=jnp.float32))
            denoms.append(jnp.sum(w.astype(jnp.float32), axis=1, keepdims=True))
            maxes.append(tm)
        m = maxes[0]
        for tm in maxes[1:]:
            m = jnp.maximum(m, tm)
        numer = jnp.zeros((rows, HEAD_DIM), jnp.float32)
        denom = jnp.zeros((rows, 1), jnp.float32)
        for tm, nb, db in zip(maxes, numers, denoms):
            f = jnp.exp(tm - m)
            numer = numer + nb * f
            denom = denom + db * f
        out_ref[:, h * HEAD_DIM:(h + 1) * HEAD_DIM] = numer
        extra = jnp.where(lane == h, denom, extra)
        extra = jnp.where(lane == heads_q + h, m, extra)
    out_ref[:, heads_q * HEAD_DIM:] = extra


def cache_partials(live, queries, keys, values):
    rows, qcols = queries.shape
    cache_rows, kcols = keys.shape
    block = min(rows, 256)
    out_cols = qcols + 128
    heads_q = qcols // HEAD_DIM
    flops = 4 * rows * cache_rows * qcols
    return pl.pallas_call(
        cache_kernel,
        grid=(rows // block,),
        in_specs=[
            pl.BlockSpec(memory_space=pltpu.SMEM),
            pl.BlockSpec((block, qcols), lambda i: (i, 0)),
            pl.BlockSpec((cache_rows, kcols), lambda i: (0, 0)),
            pl.BlockSpec((cache_rows, kcols), lambda i: (0, 0)),
        ],
        out_specs=pl.BlockSpec((block, out_cols), lambda i: (i, 0)),
        out_shape=jax.ShapeDtypeStruct((rows, out_cols), jnp.float32),
        cost_estimate=pl.CostEstimate(
            flops=flops,
            transcendentals=rows * cache_rows * heads_q,
            bytes_accessed=2 * (rows * qcols + 2 * cache_rows * kcols) + 4 * rows * out_cols,
        ),
    )(live, queries, keys, values)


def on_device(
    new_queries, new_keys, new_values, cache_keys, cache_values, segment_ids, cache_length
):
    head_size = HEAD_DIM
    own_count = new_queries.shape[0]
    join_rows = segment_ids.shape[0]
    cache_rows = cache_keys.shape[0]
    heads_kv = cache_keys.shape[1] // head_size
    heads_q = new_queries.shape[1] // head_size
    group_size = heads_q // heads_kv
    qcols = heads_q * head_size
    kcols = heads_kv * head_size
    seq_count = lax.axis_size("seq")
    seq_rank = lax.axis_index("seq")
    score_scale = head_size ** (-0.5)

    packed = jnp.concatenate([new_queries, new_keys, new_values], axis=1)
    gathered = lax.all_gather(packed, "seq", axis=0, tiled=True)
    all_queries = gathered[:, :qcols]
    all_keys = gathered[:, qcols:qcols + kcols]
    all_values = gathered[:, qcols + kcols:]

    live_rows = jnp.clip(cache_length[0] - seq_rank * cache_rows, 0, cache_rows)
    partial = cache_partials(
        live_rows.reshape(1).astype(jnp.int32), all_queries, cache_keys, cache_values
    )

    if seq_count <= 8:
        chunks = partial.reshape(seq_count, own_count, qcols + 128)
        received = [lax.dynamic_index_in_dim(chunks, seq_rank, 0, keepdims=False)]
        for shift in range(1, seq_count):
            src = lax.rem(seq_rank + shift, seq_count)
            send = lax.dynamic_index_in_dim(chunks, src, 0, keepdims=False)
            received.append(
                lax.ppermute(
                    send, "seq", [(i, (i + shift) % seq_count) for i in range(seq_count)]
                )
            )
        recv = jnp.stack(received, axis=0)
    else:
        recv = lax.all_to_all(partial, "seq", 0, 0, tiled=True).reshape(
            seq_count, own_count, qcols + 128
        )
    part_numer = recv[:, :, :qcols].reshape(seq_count, own_count, heads_q, head_size)
    part_denom = recv[:, :, qcols:qcols + heads_q]
    part_max = recv[:, :, qcols + heads_q:qcols + 2 * heads_q]

    own_queries = new_queries.reshape(own_count, heads_kv, group_size, head_size)
    fresh_scores = (
        jnp.einsum(
            "cgrd,tgd->cgrt",
            own_queries,
            all_keys.reshape(join_rows, heads_kv, head_size),
            preferred_element_type=jnp.float32,
        )
        * score_scale
    )
    start_row = seq_rank * own_count
    own_positions = start_row + jnp.arange(own_count, dtype=jnp.int32)
    own_segments = lax.dynamic_slice_in_dim(segment_ids, start_row, own_count, 0)
    key_positions = jnp.arange(join_rows, dtype=jnp.int32)
    allowed = (key_positions[None, :] <= own_positions[:, None]) & (
        segment_ids[None, :] == own_segments[:, None]
    )
    allowed = allowed[:, None, None, :]
    fresh_max = jnp.max(jnp.where(allowed, fresh_scores, NEG_FILL), axis=-1)
    fresh_weights = jnp.exp(
        jnp.where(allowed, fresh_scores - fresh_max[..., None], NEG_FILL)
    ).astype(jnp.bfloat16)
    fresh_numer = jnp.einsum(
        "cgrt,tgd->cgrd",
        fresh_weights,
        all_values.reshape(join_rows, heads_kv, head_size),
        preferred_element_type=jnp.float32,
    ).reshape(own_count, heads_q, head_size)
    fresh_denom = jnp.sum(fresh_weights.astype(jnp.float32), axis=-1).reshape(own_count, heads_q)
    fresh_max = fresh_max.reshape(own_count, heads_q)

    row_max = jnp.maximum(fresh_max, jnp.max(part_max, axis=0))
    fresh_factor = jnp.exp(fresh_max - row_max)
    part_factor = jnp.exp(part_max - row_max[None])
    total_numer = fresh_numer * fresh_factor[..., None] + jnp.sum(
        part_numer * part_factor[..., None], axis=0
    )
    total_denom = fresh_denom * fresh_factor + jnp.sum(part_denom * part_factor, axis=0)
    attended = total_numer / total_denom[..., None]
    return attended.reshape(own_count, qcols).astype(jnp.bfloat16)


def solution(mesh):
    placed = (
        P(("group", "seq"), "head"),
        P(("group", "seq"), "head"),
        P(("group", "seq"), "head"),
        P(("group", "seq"), "head"),
        P(("group", "seq"), "head"),
        P("group"),
        P("group"),
    )
    return jax.shard_map(
        on_device,
        mesh=mesh,
        in_specs=placed,
        out_specs=P(("group", "seq"), "head"),
        check_vma=False,
    )
```

time: 128 us -> 61.7 us (0.48)
  the two profiles are of different devices: /device:TPU:0 before, /device:TPU:14 now
where the time goes in v1:
time: 61.7 us; the launch traced here: 61.5 us
  waiting for transfers between devices  20.9 us (34%)
  blocking collectives  17.9 us (29%)
  Pallas kernels  7.4 us (12%)
  local copies, waits for them, and re-layouts  6.83 us (11%)
  starting transfers between devices  4.65 us (8%)
  other arithmetic  2.45 us (4%)
  between operations  0.77 us (1%)
    ppermute x3, waiting for transfers between devices, on_device(): lax.ppermute(send, 'seq', [(i, (i + shift) % seq_count) for i in range(se...  20.9 us
    all_gather x1, blocking collectives, on_device(): gathered = lax.all_gather(packed, 'seq', axis=0, tiled=True)  17.9 us
    pallas_call x1, Pallas kernels, cache_partials(): pl.pallas_call(cache_kernel, grid=(rows // block,), in_specs=[pl.BlockSpe...  7.4 us
    ppermute x3, starting transfers between devices, on_device(): lax.ppermute(send, 'seq', [(i, (i + shift) % seq_count) for i in range(se...  4.65 us
    mul x2, local copies, waits for them, and re-layouts, on_device(): part_numer * part_factor[..., None]  2.71 us
    dynamic_slice x1, local copies, waits for them, and re-layouts, on_device(): received = [lax.dynamic_index_in_dim(chunks, seq_rank, 0, keepdims=False)]  2.07 us
  transfers between devices with their start and end apart: 3, of which 2 were waited for; matrix products, arithmetic and copies ran while one was open for 2% of the time, Pallas kernels for 0%

profile of v1, /device:TPU:14, one launch (start us, length us, event | category | flops | bytes accessed | tf_op | source)
XLA Modules:
  0.0 61.5 jit_solution(2008557348027171463)
XLA Ops:
  0.7 1.0 %pad_maximum_fusion.1 = bf16[64,1536]{1,0:T(8,128)(2,1)S(1)} fusion(bf16[64,256]{1,0:T(8,128)(2,1)} %param.9, bf16[64,256]{1,0:T(8,128)(2,1)} %param.8, bf16[64,1024]{1,0:T(8,128)(2,1)} %param.7), kind=kLoop, calls=%fused_computation.16 | loop fusion | flops 589824 | bytes 393216 | tf_op jit(solution)/shard_map/concatenate | solution.py:99
  1.6 17.9 %all_gather.3 = bf16[256,1536]{1,0:T(8,128)(2,1)S(1)} all-gather(bf16[64,1536]{1,0:T(8,128)(2,1)S(1)} %pad_maximum_fusion.1), channel_id=1, replica_groups=mesh['group'=2,'head'=4,'seq'=4] {'seq'}, dimensions={0}, use_global_device_ids=true | all-gather | bytes 983040 | tf_op jit(solution)/shard_map/all_gather | solution.py:100
  19.5 0.9 %slice.26.q_ref = bf16[256,1024]{1,0:T(8,128)(2,1)} slice(bf16[256,1536]{1,0:T(8,128)(2,1)S(1)} %all_gather.3), slice={[0:256], [0:1024]} | slice | bytes 1048576 | tf_op jit(solution)/shard_map/slice | solution.py:101
  20.4 7.4 %shard_map.73 = f32[256,1152]{1,0:T(8,128)} custom-call(s32[1]{0:T(128)} %bitcast.6.live_ref, bf16[256,1024]{1,0:T(8,128)(2,1)} %slice.26.q_ref, bf16[1024,256]{1,0:T(8,128)(2,1)} %k_ref.1, bf16[1024,256]{1,0:T(8,128)(2,1)} %v_ref.1), custom_call_target="tpu_custom_call" | custom-call | flops 1073741824 | bytes 2752512 | tf_op jit(solution)/shard_map/pallas_call | solution.py:64
  27.8 0.0 copy-start
  27.8 2.1 %constant_dynamic-slice_fusion = (f32[1,64,1152]{2,1,0:T(8,128)S(1)}, f32[64,1152]{1,0:T(8,128)S(1)}, f32[64,1152]{1,0:T(8,128)}, f32[64,1152]{1,0:T(8,128)S(1)}) fusion(f32[4,64,1152]{2,1,0:T(8,128)} %bitcast.44, s32[]{:T(128)S(6)} %select_n.26, s32[]{:T(128)S(6)} %select_n.29, s32[]{:T(128)S(6)} %select_n.28, s32[]{:T(128)S(6)} %select_n.27), kind=kLoop, calls=%fused_computation.28 | loop fusion | bytes 2359312 | tf_op jit(solution)/shard_map/jit(dynamic_index_in_dim)/dynamic_slice | solution.py:112
  29.9 0.0 copy-start.1
  29.9 2.6 %collective-permute-start.1 = (f32[64,1152]{1,0:T(8,128)}, f32[64,1152]{1,0:T(8,128)S(1)}, u32[]{:S(2)}, u32[]{:S(2)}) collective-permute-start(f32[64,1152]{1,0:T(8,128)} %get-tuple-element.11), channel_id=1, source_target_pairs={{0,2},{1,3},{2,0},{3,1},{4,6},{5,7},{6,4},{7,5},{8,10},{9,11},{10,... | collective-permute-start | bytes 884744 | tf_op jit(solution)/shard_map/ppermute | solution.py:117
  32.5 0.6 collective-permute-start.2
  33.1 1.4 %collective-permute-start = (f32[64,1152]{1,0:T(8,128)S(1)}, f32[64,1152]{1,0:T(8,128)S(1)}, u32[]{:S(2)}, u32[]{:S(2)}) collective-permute-start(f32[64,1152]{1,0:T(8,128)S(1)} %get-tuple-element.12), channel_id=1, source_target_pairs={{0,1},{1,2},{2,3},{3,0},{4,5},{5,6},{6,7},{7,4},{8,9},{9,10},{10,1... | collective-permute-start | bytes 884744 | tf_op jit(solution)/shard_map/ppermute | solution.py:117
  34.6 0.0 copy-done
  34.6 0.1 reshape.116
  34.7 0.0 copy-done.1
  34.7 0.1 dynamic_slice.16
  34.8 0.1 fusion.8
  34.9 0.3 select_reduce_fusion
  35.2 0.3 convolution_bitcast_fusion
  35.5 0.2 copy.36
  35.7 0.1 reshape.117
  35.8 0.3 convert_reduce_fusion
  36.1 13.4 %collective-permute-done.1 = f32[64,1152]{1,0:T(8,128)S(1)} collective-permute-done((f32[64,1152]{1,0:T(8,128)}, f32[64,1152]{1,0:T(8,128)S(1)}, u32[]{:S(2)}, u32[]{:S(2)}) %collective-permute-start.1) | collective-permute-done | bytes 294944 | tf_op jit(solution)/shard_map/ppermute | solution.py:117
  49.5 7.5 %collective-permute-done.2 = f32[64,1152]{1,0:T(8,128)S(1)} collective-permute-done((f32[64,1152]{1,0:T(8,128)S(1)}, f32[64,1152]{1,0:T(8,128)S(1)}, u32[]{:S(2)}, u32[]{:S(2)}) %collective-permute-start.2) | collective-permute-done | bytes 294944 | tf_op jit(solution)/shard_map/ppermute | solution.py:117
  57.0 0.0 collective-permute-done
  57.0 0.1 pad_maximum_fusion
  57.1 0.1 fusion.10
  57.2 0.1 copy.37
  57.2 0.1 copy.39
  57.4 1.3 %mul.55 = f32[4,64,8,128]{3,2,1,0:T(8,128)} broadcast(f32[4,64,8]{2,1,0:T(8,128)S(1)} %get-tuple-element.15), dimensions={0,1,2} | broadcast | bytes 1056768 | tf_op jit(solution)/shard_map/mul | solution.py:165
  58.7 1.4 %mul.56 = f32[4,64,1024]{2,1,0:T(8,128)S(1)} reshape(f32[4,64,8,128]{3,2,1,0:T(8,128)} %mul.55) | data formatting | bytes 2097152 | tf_op jit(solution)/shard_map/mul | solution.py:165
  60.1 0.1 copy.40
  60.2 0.1 copy.38
  60.2 0.1 copy.41
  60.3 0.1 fusion.1
  60.5 0.1 mul.52
  60.6 0.1 div.11
  60.7 0.8 %fusion.2 = bf16[64,1024]{1,0:T(8,128)(2,1)} fusion(f32[8,8,8,128]{3,2,1,0:T(8,128)S(1)} %bitcast.46, f32[64,1024]{1,0:T(8,128)S(1)} %fusion.1, f32[64,1024]{1,0:T(8,128)S(1)} %reshape.117, f32[8,8,8,128]{3,2,1,0:T(8,128)S(1)} %bitcast.45), kind=kLoop, calls=%fused_computation.13 | loop fusion | flops 262144 | bytes 1179648 | tf_op jit(solution)/shard_map/convert_element_type | solution.py:169
  (7 shorter events, 0.2 us)
Async XLA Ops:
  27.8 6.8 %copy-start = (bf16[64,1024]{1,0:T(8,128)(2,1)S(1)}, bf16[64,1024]{1,0:T(8,128)(2,1)}, u32[]{:S(2)}) copy-start(bf16[64,1024]{1,0:T(8,128)(2,1)} %param.7) | copy-start | bytes 393220
  29.9 4.8 %copy-start.1 = (s32[256]{0:T(256)S(1)}, s32[256]{0:T(256)}, u32[]{:S(2)}) copy-start(s32[256]{0:T(256)} %param.12) | copy-start | bytes 3076
  29.9 19.6 %collective-permute-start.1 = (f32[64,1152]{1,0:T(8,128)}, f32[64,1152]{1,0:T(8,128)S(1)}, u32[]{:S(2)}, u32[]{:S(2)}) collective-permute-start(f32[64,1152]{1,0:T(8,128)} %get-tuple-element.11), channel_id=1, source_target_pairs={{0,2},{1,3},{2,0},{3,1},{4,6},{5,7},{6,4},{7,5},{8,10},{9,11},{10,... | collective-permute-start | bytes 884744 | tf_op jit(solution)/shard_map/ppermute | solution.py:117
  32.5 24.5 %collective-permute-start.2 = (f32[64,1152]{1,0:T(8,128)S(1)}, f32[64,1152]{1,0:T(8,128)S(1)}, u32[]{:S(2)}, u32[]{:S(2)}) collective-permute-start(f32[64,1152]{1,0:T(8,128)S(1)} %get-tuple-element.10), channel_id=1, source_target_pairs={{0,3},{1,0},{2,1},{3,2},{4,7},{5,4},{6,5},{7,6},{8,11},{9,8},{10,9... | collective-permute-start | bytes 884744 | tf_op jit(solution)/shard_map/ppermute | solution.py:117
  33.1 23.9 %collective-permute-start = (f32[64,1152]{1,0:T(8,128)S(1)}, f32[64,1152]{1,0:T(8,128)S(1)}, u32[]{:S(2)}, u32[]{:S(2)}) collective-permute-start(f32[64,1152]{1,0:T(8,128)S(1)} %get-tuple-element.12), channel_id=1, source_target_pairs={{0,1},{1,2},{2,3},{3,0},{4,5},{5,6},{6,7},{7,4},{8,9},{9,10},{10,1... | collective-permute-start | bytes 884744 | tf_op jit(solution)/shard_map/ppermute | solution.py:117

commit v2 on v1

--- a/solution.py
+++ b/solution.py
@@ -15,7 +15,7 @@
 def cache_kernel(live_ref, q_ref, k_ref, v_ref, out_ref):
     live = live_ref[0]
     rows = q_ref.shape[0]
-    heads_q = q_ref.shape[1] // HEAD_DIM
+    heads_q = (out_ref.shape[1] - 128) // HEAD_DIM
     heads_kv = k_ref.shape[1] // HEAD_DIM
     group = heads_q // heads_kv
     tiles = k_ref.shape[0] // SUB
@@ -54,30 +54,37 @@
     out_ref[:, heads_q * HEAD_DIM:] = extra
 
 
-def cache_partials(live, queries, keys, values):
-    rows, qcols = queries.shape
+def cache_partials(scalars, gathered, keys, values, block, chunked, qcols):
+    rows, gcols = gathered.shape
+    if chunked:
+        rows = block
     cache_rows, kcols = keys.shape
-    block = min(rows, 256)
     out_cols = qcols + 128
     heads_q = qcols // HEAD_DIM
     flops = 4 * rows * cache_rows * qcols
+    if chunked:
+        q_map = lambda i, s: (s[1], 0)
+    else:
+        q_map = lambda i, s: (i, 0)
     return pl.pallas_call(
         cache_kernel,
-        grid=(rows // block,),
-        in_specs=[
-            pl.BlockSpec(memory_space=pltpu.SMEM),
-            pl.BlockSpec((block, qcols), lambda i: (i, 0)),
-            pl.BlockSpec((cache_rows, kcols), lambda i: (0, 0)),
-            pl.BlockSpec((cache_rows, kcols), lambda i: (0, 0)),
-        ],
-        out_specs=pl.BlockSpec((block, out_cols), lambda i: (i, 0)),
+        grid_spec=pltpu.PrefetchScalarGridSpec(
+            num_scalar_prefetch=1,
+            grid=(rows // block,),
+            in_specs=[
+                pl.BlockSpec((block, gcols), q_map),
+                pl.BlockSpec((cache_rows, kcols), lambda i, s: (0, 0)),
+                pl.BlockSpec((cache_rows, kcols), lambda i, s: (0, 0)),
+            ],
+            out_specs=pl.BlockSpec((block, out_cols), lambda i, s: (i, 0)),
+        ),
         out_shape=jax.ShapeDtypeStruct((rows, out_cols), jnp.float32),
         cost_estimate=pl.CostEstimate(
             flops=flops,
             transcendentals=rows * cache_rows * heads_q,
-            bytes_accessed=2 * (rows * qcols + 2 * cache_rows * kcols) + 4 * rows * out_cols,
+            bytes_accessed=2 * (rows * gcols + 2 * cache_rows * kcols) + 4 * rows * out_cols,
         ),
-    )(live, queries, keys, values)
+    )(scalars, gathered, keys, values)
 
 
 def on_device(
@@ -98,34 +105,35 @@
 
     packed = jnp.concatenate([new_queries, new_keys, new_values], axis=1)
     gathered = lax.all_gather(packed, "seq", axis=0, tiled=True)
-    all_queries = gathered[:, :qcols]
     all_keys = gathered[:, qcols:qcols + kcols]
     all_values = gathered[:, qcols + kcols:]
 
     live_rows = jnp.clip(cache_length[0] - seq_rank * cache_rows, 0, cache_rows)
-    partial = cache_partials(
-        live_rows.reshape(1).astype(jnp.int32), all_queries, cache_keys, cache_values
-    )
+    live_rows = live_rows.astype(jnp.int32)
 
     if seq_count <= 8:
-        chunks = partial.reshape(seq_count, own_count, qcols + 128)
-        received = [lax.dynamic_index_in_dim(chunks, seq_rank, 0, keepdims=False)]
-        for shift in range(1, seq_count):
-            src = lax.rem(seq_rank + shift, seq_count)
-            send = lax.dynamic_index_in_dim(chunks, src, 0, keepdims=False)
-            received.append(
-                lax.ppermute(
-                    send, "seq", [(i, (i + shift) % seq_count) for i in range(seq_count)]
+        parts = []
+        for shift in list(range(1, seq_count)) + [0]:
+            chunk = lax.rem(seq_rank + shift, seq_count)
+            scalars = jnp.stack([live_rows, chunk.astype(jnp.int32)])
+            part = cache_partials(
+                scalars, gathered, cache_keys, cache_values, own_count, True, qcols
+            )
+            if shift:
+                part = lax.ppermute(
+                    part, "seq", [(i, (i + shift) % seq_count) for i in range(seq_count)]
                 )
-            )
-        recv = jnp.stack(received, axis=0)
+            parts.append(part)
     else:
-        recv = lax.all_to_all(partial, "seq", 0, 0, tiled=True).reshape(
-            seq_count, own_count, qcols + 128
+        scalars = jnp.stack([live_rows, jnp.zeros((), jnp.int32)])
+        partial = cache_partials(
+            scalars, gathered, cache_keys, cache_values, min(join_rows, 256), False, qcols
         )
-    part_numer = recv[:, :, :qcols].reshape(seq_count, own_count, heads_q, head_size)
-    part_denom = recv[:, :, qcols:qcols + heads_q]
-    part_max = recv[:, :, qcols + heads_q:qcols + 2 * heads_q]
+        recv = lax.all_to_all(partial, "seq", 0, 0, tiled=True)
+        parts = [recv[j * own_count:(j + 1) * own_count] for j in range(seq_count)]
+    part_numer = [p[:, :qcols].reshape(own_count, heads_q, head_size) for p in parts]
+    part_denom = [p[:, qcols:qcols + heads_q] for p in parts]
+    part_max = [p[:, qcols + heads_q:qcols + 2 * heads_q] for p in parts]
 
     own_queries = new_queries.reshape(own_count, heads_kv, group_size, head_size)
     fresh_scores = (
@@ -158,13 +166,16 @@
     fresh_denom = jnp.sum(fresh_weights.astype(jnp.float32), axis=-1).reshape(own_count, heads_q)
     fresh_max = fresh_max.reshape(own_count, heads_q)
 
-    row_max = jnp.maximum(fresh_max, jnp.max(part_max, axis=0))
+    row_max = fresh_max
+    for m in part_max:
+        row_max = jnp.maximum(row_max, m)
     fresh_factor = jnp.exp(fresh_max - row_max)
-    part_factor = jnp.exp(part_max - row_max[None])
-    total_numer = fresh_numer * fresh_factor[..., None] + jnp.sum(
-        part_numer * part_factor[..., None], axis=0
-    )
-    total_denom = fresh_denom * fresh_factor + jnp.sum(part_denom * part_factor, axis=0)
+    total_numer = fresh_numer * fresh_factor[..., None]
+    total_denom = fresh_denom * fresh_factor
+    for n_j, d_j, m_j in zip(part_numer, part_denom, part_max):
+        f_j = jnp.exp(m_j - row_max)
+        total_numer = total_numer + n_j * f_j[..., None]
+        total_denom = total_denom + d_j * f_j
     attended = total_numer / total_denom[..., None]
     return attended.reshape(own_count, qcols).astype(jnp.bfloat16)
 

time: 61.7 us -> 78.6 us (1.27)
  the two profiles are of different devices: /device:TPU:14 before, /device:TPU:0 now
where the time goes in v2:
time: 78.6 us; the launch traced here: 78.1 us
  Pallas kernels  41.7 us (53%)
  blocking collectives  21.7 us (28%)
  other arithmetic  5.65 us (7%)
  starting transfers between devices  3.82 us (5%)
  local copies, waits for them, and re-layouts  3.79 us (5%)
    pallas_call x4, Pallas kernels, cache_partials(): pl.pallas_call(cache_kernel, grid_spec=pltpu.PrefetchScalarGridSpec(num_s...  41.7 us
    all_gather x1, blocking collectives, on_device(): gathered = lax.all_gather(packed, 'seq', axis=0, tiled=True)  21.7 us
    ppermute x3, starting transfers between devices, on_device(): lax.ppermute(part, 'seq', [(i, (i + shift) % seq_count) for i in range(se...  3.82 us
    another operation x4, other arithmetic, on_device(): scalars = jnp.stack([live_rows, chunk.astype(jnp.int32)])  2.4 us
  transfers between devices with their start and end apart: 3, of which 0 were waited for; matrix products, arithmetic and copies ran while one was open for 6% of the time, Pallas kernels for 40%

profile of v2, /device:TPU:0, one launch (start us, length us, event | category | flops | bytes accessed | tf_op | source)
XLA Modules:
  0.0 78.1 jit_solution(7920124413463501611)
XLA Ops:
  0.7 1.0 %pad_maximum_fusion = bf16[64,1536]{1,0:T(8,128)(2,1)S(1)} fusion(bf16[64,256]{1,0:T(8,128)(2,1)} %param.9, bf16[64,256]{1,0:T(8,128)(2,1)} %param.8, bf16[64,1024]{1,0:T(8,128)(2,1)} %param.7), kind=kLoop, calls=%fused_computation.17 | loop fusion | flops 589824 | bytes 393216 | tf_op jit(solution)/shard_map/concatenate | solution.py:106
  1.6 21.7 %all_gather.3.q_ref = bf16[256,1536]{1,0:T(8,128)(2,1)} all-gather(bf16[64,1536]{1,0:T(8,128)(2,1)S(1)} %pad_maximum_fusion), channel_id=1, replica_groups=mesh['group'=2,'head'=4,'seq'=4] {'seq'}, dimensions={0}, use_global_device_ids=true | all-gather | bytes 983040 | tf_op jit(solution)/shard_map/all_gather | solution.py:107
  23.3 0.6 pad_add_fusion.live_ref
  23.9 10.4 %shard_map.73 = f32[64,1152]{1,0:T(8,128)} custom-call(s32[2]{0:T(128)} %pad_add_fusion.live_ref, bf16[256,1536]{1,0:T(8,128)(2,1)} %all_gather.3.q_ref, bf16[1024,256]{1,0:T(8,128)(2,1)} %k_ref.7, bf16[1024,256]{1,0:T(8,128)(2,1)} %v_ref.7), custom_call_target="tpu_custom_call" | custom-call | flops 268435456 | bytes 1540096 | tf_op jit(solution)/shard_map/pallas_call | solution.py:69
  34.3 0.0 collective-permute-start
  34.3 0.6 pad_add_fusion.1.live_ref
  34.9 10.4 %shard_map.74 = f32[64,1152]{1,0:T(8,128)} custom-call(s32[2]{0:T(128)} %pad_add_fusion.1.live_ref, bf16[256,1536]{1,0:T(8,128)(2,1)} %all_gather.3.q_ref, bf16[1024,256]{1,0:T(8,128)(2,1)} %k_ref.7, bf16[1024,256]{1,0:T(8,128)(2,1)} %v_ref.7), custom_call_target="tpu_custom_call" | custom-call | flops 268435456 | bytes 1540096 | tf_op jit(solution)/shard_map/pallas_call | solution.py:69
  45.3 2.6 %collective-permute-start.1 = (f32[64,1152]{1,0:T(8,128)}, f32[64,1152]{1,0:T(8,128)S(1)}, u32[]{:S(2)}, u32[]{:S(2)}) collective-permute-start(f32[64,1152]{1,0:T(8,128)} %shard_map.74), channel_id=1, source_target_pairs={{0,2},{1,3},{2,0},{3,1},{4,6},{5,7},{6,4},{7,5},{8,10},{9,11},{10,... | collective-permute-start | bytes 884744 | tf_op jit(solution)/shard_map/ppermute | solution.py:123
  47.9 0.6 pad_add_fusion.2.live_ref
  48.5 0.0 copy-start.1
  48.5 10.5 %shard_map.75 = f32[64,1152]{1,0:T(8,128)} custom-call(s32[2]{0:T(128)} %pad_add_fusion.2.live_ref, bf16[256,1536]{1,0:T(8,128)(2,1)} %all_gather.3.q_ref, bf16[1024,256]{1,0:T(8,128)(2,1)} %k_ref.7, bf16[1024,256]{1,0:T(8,128)(2,1)} %v_ref.7), custom_call_target="tpu_custom_call" | custom-call | flops 268435456 | bytes 1540096 | tf_op jit(solution)/shard_map/pallas_call | solution.py:69
  59.0 1.2 %collective-permute-start.2 = (f32[64,1152]{1,0:T(8,128)}, f32[64,1152]{1,0:T(8,128)S(1)}, u32[]{:S(2)}, u32[]{:S(2)}) collective-permute-start(f32[64,1152]{1,0:T(8,128)} %shard_map.75), channel_id=1, source_target_pairs={{0,3},{1,0},{2,1},{3,2},{4,7},{5,4},{6,5},{7,6},{8,11},{9,8},{10,9... | collective-permute-start | bytes 884744 | tf_op jit(solution)/shard_map/ppermute | solution.py:123
  60.3 0.0 copy-done.1
  60.3 0.1 reshape.84
  60.3 1.0 %fusion.15 = (bf16[256,256]{1,0:T(8,128)(2,1)S(1)}, bf16[256,256]{1,0:T(8,128)(2,1)S(1)}) fusion(bf16[256,1536]{1,0:T(8,128)(2,1)} %all_gather.3.q_ref), kind=kLoop, calls=%fused_computation.43 | loop fusion | bytes 524288 | tf_op jit(solution)/shard_map/slice | solution.py:109
  61.4 0.0 copy-start.2
  61.4 0.7 copy-done.2
  62.1 0.1 dynamic_slice.3
  62.2 0.1 fusion.9
  62.3 0.3 select_reduce_fusion
  62.6 0.3 convolution_bitcast_fusion
  62.9 0.2 copy.23
  63.1 0.1 reshape.85
  63.2 0.3 convert_reduce_fusion
  63.5 0.1 copy.26
  63.5 0.1 copy.25
  63.6 0.7 pad_add_fusion.3.live_ref
  64.3 10.4 %shard_map.76 = f32[64,1152]{1,0:T(8,128)} custom-call(s32[2]{0:T(128)} %pad_add_fusion.3.live_ref, bf16[256,1536]{1,0:T(8,128)(2,1)} %all_gather.3.q_ref, bf16[1024,256]{1,0:T(8,128)(2,1)} %k_ref.7, bf16[1024,256]{1,0:T(8,128)(2,1)} %v_ref.7), custom_call_target="tpu_custom_call" | custom-call | flops 268435456 | bytes 1540096 | tf_op jit(solution)/shard_map/pallas_call | solution.py:69
  74.7 0.0 collective-permute-done
  74.7 0.0 collective-permute-done.1
  74.7 0.0 collective-permute-done.2
  74.7 1.0 %fusion.10 = (f32[64,8]{1,0:T(8,128)S(1)}, f32[64,8]{1,0:T(8,128)S(1)}, f32[64,8]{1,0:T(8,128)S(1)}, f32[64,8]{1,0:T(8,128)S(1)}, f32[64,8]{1,0:T(8,128)S(1)}, /*index=5*/f32[64,8]{1,0:T(8,128)S(1)}) fusion(f32[64,1152]{1,0:T(8,128)} %shard_map.76, f32[64,1152]{1,0:T(8,128)S(1)} %collective-permute-done.2, f32[64,1152]{1,0:T(8,128)S(1)} %collective-permute-done.1, ...), kind=kLoop, calls=%fused_computation.24 | loop fusion | flops 9216 | bytes 32768 | tf_op jit(solution)/shard_map/add | solution.py:178
  75.7 0.1 div.11
  75.8 0.1 mul.90
  75.9 0.1 mul.93
  76.1 0.1 mul.96
  76.2 0.0 copy-start
  76.2 0.1 mul.99
  76.3 0.1 mul.102
  76.5 0.7 copy-done
  77.2 1.0 %fusion.1 = bf16[64,1024]{1,0:T(8,128)(2,1)} fusion(f32[8,8,8,128]{3,2,1,0:T(8,128)S(1)} %bitcast.53, f32[8,8,8,128]{3,2,1,0:T(8,128)S(1)} %bitcast.58, f32[8,8,8,128]{3,2,1,0:T(8,128)S(1)} %bitcast.57, f32[8,8,8,128]{3,2,1,0:T(8,128)S(1)} %bitcast.56, f32[8,8,8,128]{3,2,1,0:T(8,128)S(1)} %bitcast.55, f32[64,1024]{1,0:T(8,128)S(1)} %reshape.85, ...), kind=kLoop, calls=%fused_computation.7 | loop fusion | flops 720896 | bytes 3014656 | tf_op jit(solution)/shard_map/convert_element_type | solution.py:180
  (3 shorter events, 0.1 us)
Async XLA Ops:
  34.3 40.4 %collective-permute-start = (f32[64,1152]{1,0:T(8,128)}, f32[64,1152]{1,0:T(8,128)S(1)}, u32[]{:S(2)}, u32[]{:S(2)}) collective-permute-start(f32[64,1152]{1,0:T(8,128)} %shard_map.73), channel_id=1, source_target_pairs={{0,1},{1,2},{2,3},{3,0},{4,5},{5,6},{6,7},{7,4},{8,9},{9,10},{10,1... | collective-permute-start | bytes 884744 | tf_op jit(solution)/shard_map/ppermute | solution.py:123
  45.3 29.3 %collective-permute-start.1 = (f32[64,1152]{1,0:T(8,128)}, f32[64,1152]{1,0:T(8,128)S(1)}, u32[]{:S(2)}, u32[]{:S(2)}) collective-permute-start(f32[64,1152]{1,0:T(8,128)} %shard_map.74), channel_id=1, source_target_pairs={{0,2},{1,3},{2,0},{3,1},{4,6},{5,7},{6,4},{7,5},{8,10},{9,11},{10,... | collective-permute-start | bytes 884744 | tf_op jit(solution)/shard_map/ppermute | solution.py:123
  48.5 11.8 %copy-start.1 = (bf16[64,1024]{1,0:T(8,128)(2,1)S(1)}, bf16[64,1024]{1,0:T(8,128)(2,1)}, u32[]{:S(2)}) copy-start(bf16[64,1024]{1,0:T(8,128)(2,1)} %param.7) | copy-start | bytes 393220
  59.0 15.7 %collective-permute-start.2 = (f32[64,1152]{1,0:T(8,128)}, f32[64,1152]{1,0:T(8,128)S(1)}, u32[]{:S(2)}, u32[]{:S(2)}) collective-permute-start(f32[64,1152]{1,0:T(8,128)} %shard_map.75), channel_id=1, source_target_pairs={{0,3},{1,0},{2,1},{3,2},{4,7},{5,4},{6,5},{7,6},{8,11},{9,8},{10,9... | collective-permute-start | bytes 884744 | tf_op jit(solution)/shard_map/ppermute | solution.py:123
  61.4 0.7 copy-start.2
  76.2 1.0 %copy-start = (f32[64,1152]{1,0:T(8,128)S(1)}, f32[64,1152]{1,0:T(8,128)}, u32[]{:S(2)}) copy-start(f32[64,1152]{1,0:T(8,128)} %shard_map.76) | copy-start | bytes 884740

commit v3 on v2

--- a/solution.py
+++ b/solution.py
@@ -12,26 +12,26 @@
 NEG_FILL = -1e30
 
 
-def cache_kernel(live_ref, q_ref, k_ref, v_ref, out_ref):
-    live = live_ref[0]
+def cache_kernel(scalar_ref, q_ref, kt_ref, v_ref, out_ref):
+    live = scalar_ref[0]
     rows = q_ref.shape[0]
     heads_q = (out_ref.shape[1] - 128) // HEAD_DIM
-    heads_kv = k_ref.shape[1] // HEAD_DIM
+    heads_kv = kt_ref.shape[0] // HEAD_DIM
     group = heads_q // heads_kv
-    tiles = k_ref.shape[0] // SUB
+    tiles = kt_ref.shape[1] // SUB
     scale = HEAD_DIM ** (-0.5)
-    col = lax.broadcasted_iota(jnp.int32, (rows, SUB), 1)
+    col = lax.broadcasted_iota(jnp.int32, (group * rows, SUB), 1)
     lane = lax.broadcasted_iota(jnp.int32, (rows, 128), 1)
     extra = jnp.zeros((rows, 128), jnp.float32)
-    for h in range(heads_q):
-        g = h // group
-        qh = q_ref[:, h * HEAD_DIM:(h + 1) * HEAD_DIM]
+    for g in range(heads_kv):
+        qg = jnp.concatenate(
+            [q_ref[:, (g * group + r) * HEAD_DIM:(g * group + r + 1) * HEAD_DIM] for r in range(group)],
+            axis=0,
+        )
         maxes, numers, denoms = [], [], []
         for b in range(tiles):
-            kb = k_ref[b * SUB:(b + 1) * SUB, g * HEAD_DIM:(g + 1) * HEAD_DIM]
-            s = lax.dot_general(
-                qh, kb, (((1,), (1,)), ((), ())), preferred_element_type=jnp.float32
-            ) * scale
+            kb = kt_ref[g * HEAD_DIM:(g + 1) * HEAD_DIM, b * SUB:(b + 1) * SUB]
+            s = jnp.dot(qg, kb, preferred_element_type=jnp.float32) * scale
             ok = (col + b * SUB) < live
             tm = jnp.max(jnp.where(ok, s, NEG_FILL), axis=1, keepdims=True)
             w = jnp.exp(jnp.where(ok, s - tm, NEG_FILL)).astype(jnp.bfloat16)
@@ -42,15 +42,17 @@
         m = maxes[0]
         for tm in maxes[1:]:
             m = jnp.maximum(m, tm)
-        numer = jnp.zeros((rows, HEAD_DIM), jnp.float32)
-        denom = jnp.zeros((rows, 1), jnp.float32)
+        numer = jnp.zeros((group * rows, HEAD_DIM), jnp.float32)
+        denom = jnp.zeros((group * rows, 1), jnp.float32)
         for tm, nb, db in zip(maxes, numers, denoms):
             f = jnp.exp(tm - m)
             numer = numer + nb * f
             denom = denom + db * f
-        out_ref[:, h * HEAD_DIM:(h + 1) * HEAD_DIM] = numer
-        extra = jnp.where(lane == h, denom, extra)
-        extra = jnp.where(lane == heads_q + h, m, extra)
+        for r in range(group):
+            h = g * group + r
+            out_ref[:, h * HEAD_DIM:(h + 1) * HEAD_DIM] = numer[r * rows:(r + 1) * rows]
+            extra = jnp.where(lane == h, denom[r * rows:(r + 1) * rows], extra)
+            extra = jnp.where(lane == heads_q + h, m[r * rows:(r + 1) * rows], extra)
     out_ref[:, heads_q * HEAD_DIM:] = extra
 
 
@@ -58,7 +60,7 @@
     rows, gcols = gathered.shape
     if chunked:
         rows = block
-    cache_rows, kcols = keys.shape
+    kcols, cache_rows = keys.shape
     out_cols = qcols + 128
     heads_q = qcols // HEAD_DIM
     flops = 4 * rows * cache_rows * qcols
@@ -73,7 +75,7 @@
             grid=(rows // block,),
             in_specs=[
                 pl.BlockSpec((block, gcols), q_map),
-                pl.BlockSpec((cache_rows, kcols), lambda i, s: (0, 0)),
+                pl.BlockSpec((kcols, cache_rows), lambda i, s: (0, 0)),
                 pl.BlockSpec((cache_rows, kcols), lambda i, s: (0, 0)),
             ],
             out_specs=pl.BlockSpec((block, out_cols), lambda i, s: (i, 0)),
@@ -110,6 +112,7 @@
 
     live_rows = jnp.clip(cache_length[0] - seq_rank * cache_rows, 0, cache_rows)
     live_rows = live_rows.astype(jnp.int32)
+    keys_t = cache_keys.T
 
     if seq_count <= 8:
         parts = []
@@ -117,7 +120,7 @@
             chunk = lax.rem(seq_rank + shift, seq_count)
             scalars = jnp.stack([live_rows, chunk.astype(jnp.int32)])
             part = cache_partials(
-                scalars, gathered, cache_keys, cache_values, own_count, True, qcols
+                scalars, gathered, keys_t, cache_values, own_count, True, qcols
             )
             if shift:
                 part = lax.ppermute(
@@ -127,7 +130,7 @@
     else:
         scalars = jnp.stack([live_rows, jnp.zeros((), jnp.int32)])
         partial = cache_partials(
-            scalars, gathered, cache_keys, cache_values, min(join_rows, 256), False, qcols
+            scalars, gathered, keys_t, cache_values, min(join_rows, 256), False, qcols
         )
         recv = lax.all_to_all(partial, "seq", 0, 0, tiled=True)
         parts = [recv[j * own_count:(j + 1) * own_count] for j in range(seq_count)]

time: 78.6 us -> 58.1 us (0.74)
  the two profiles are of different devices: /device:TPU:0 before, /device:TPU:11 now
where the time goes in v3:
time: 58.1 us; the launch traced here: 57.7 us
  blocking collectives  15.9 us (27%)
  Pallas kernels  15.8 us (27%)
  waiting for transfers between devices  9.97 us (17%)
  local copies, waits for them, and re-layouts  5.87 us (10%)
  other arithmetic  4.64 us (8%)
  starting transfers between devices  4.08 us (7%)
  between operations  0.81 us (1%)
  matrix products  0.61 us (1%)
    all_gather x1, blocking collectives, on_device(): gathered = lax.all_gather(packed, 'seq', axis=0, tiled=True)  15.9 us
    pallas_call x4, Pallas kernels, cache_partials(): pl.pallas_call(cache_kernel, grid_spec=pltpu.PrefetchScalarGridSpec(num_s...  15.8 us
    ppermute x3, waiting for transfers between devices, on_device(): lax.ppermute(part, 'seq', [(i, (i + shift) % seq_count) for i in range(se...  9.97 us
    ppermute x3, starting transfers between devices, on_device(): lax.ppermute(part, 'seq', [(i, (i + shift) % seq_count) for i in range(se...  4.08 us
    unnamed x11, local copies, waits for them, and re-layouts  3.46 us
    another operation x4, other arithmetic, on_device(): scalars = jnp.stack([live_rows, chunk.astype(jnp.int32)])  2.34 us
  transfers between devices with their start and end apart: 3, of which 2 were waited for; matrix products, arithmetic and copies ran while one was open for 8% of the time, Pallas kernels for 21%

profile of v3, /device:TPU:11, one launch (start us, length us, event | category | flops | bytes accessed | tf_op | source)
XLA Modules:
  0.0 57.7 jit_solution(9672204181358952717)
XLA Ops:
  0.7 0.0 copy-start.1
  0.7 0.0 copy-start.2
  0.7 0.0 copy-start.3
  0.7 2.1 %copy.26 = bf16[1024,256]{0,1:T(8,128)(2,1)} copy(bf16[1024,256]{1,0:T(8,128)(2,1)} %param.10) | data formatting | bytes 1048576 | tf_op args[3]
  2.8 0.0 copy-done.1
  2.8 0.0 copy-done.2
  2.8 0.0 copy-done.3
  2.8 15.9 %all_gather.3.q_ref = bf16[256,1536]{1,0:T(8,128)(2,1)} all-gather(bf16[64,1536]{1,0:T(8,128)(2,1)S(1)} %pad_maximum_fusion), channel_id=1, replica_groups=mesh['group'=2,'head'=4,'seq'=4] {'seq'}, dimensions={0}, use_global_device_ids=true | all-gather | bytes 983040 | tf_op jit(solution)/shard_map/all_gather | solution.py:109
  18.7 0.6 %pad_add_fusion.scalar_ref = s32[2]{0:T(128)} fusion(s32[1]{0:T(128)} %bitcast.7, s32[1]{0:T(128)} %bitcast.6), kind=kLoop, calls=%fused_computation.37 | loop fusion | flops 2 | bytes 16 | tf_op jit(solution)/shard_map/stack | solution.py:121
  19.3 3.9 %shard_map.73 = f32[64,1152]{1,0:T(8,128)} custom-call(s32[2]{0:T(128)} %pad_add_fusion.scalar_ref, bf16[256,1536]{1,0:T(8,128)(2,1)} %all_gather.3.q_ref, bf16[256,1024]{1,0:T(8,128)(2,1)} %bitcast.54, bf16[1024,256]{1,0:T(8,128)(2,1)} %v_ref.7), custom_call_target="tpu_custom_call" | custom-call | flops 268435456 | bytes 1540096 | tf_op jit(solution)/shard_map/pallas_call | solution.py:71
  23.3 1.5 %collective-permute-start = (f32[64,1152]{1,0:T(8,128)}, f32[64,1152]{1,0:T(8,128)S(1)}, u32[]{:S(2)}, u32[]{:S(2)}) collective-permute-start(f32[64,1152]{1,0:T(8,128)} %shard_map.73), channel_id=1, source_target_pairs={{0,1},{1,2},{2,3},{3,0},{4,5},{5,6},{6,7},{7,4},{8,9},{9,10},{10,1... | collective-permute-start | bytes 884744 | tf_op jit(solution)/shard_map/ppermute | solution.py:126
  24.8 0.6 %pad_add_fusion.1.scalar_ref = s32[2]{0:T(128)} fusion(s32[1]{0:T(128)} %bitcast.9, s32[1]{0:T(128)} %bitcast.6), kind=kLoop, calls=%fused_computation.38 | loop fusion | flops 2 | bytes 16 | tf_op jit(solution)/shard_map/stack | solution.py:121
  25.4 3.9 %shard_map.74 = f32[64,1152]{1,0:T(8,128)} custom-call(s32[2]{0:T(128)} %pad_add_fusion.1.scalar_ref, bf16[256,1536]{1,0:T(8,128)(2,1)} %all_gather.3.q_ref, bf16[256,1024]{1,0:T(8,128)(2,1)} %bitcast.55, bf16[1024,256]{1,0:T(8,128)(2,1)} %v_ref.7), custom_call_target="tpu_custom_call" | custom-call | flops 268435456 | bytes 1540096 | tf_op jit(solution)/shard_map/pallas_call | solution.py:71
  29.3 2.4 %collective-permute-start.1 = (f32[64,1152]{1,0:T(8,128)}, f32[64,1152]{1,0:T(8,128)S(1)}, u32[]{:S(2)}, u32[]{:S(2)}) collective-permute-start(f32[64,1152]{1,0:T(8,128)} %shard_map.74), channel_id=1, source_target_pairs={{0,2},{1,3},{2,0},{3,1},{4,6},{5,7},{6,4},{7,5},{8,10},{9,11},{10,... | collective-permute-start | bytes 884744 | tf_op jit(solution)/shard_map/ppermute | solution.py:126
  31.8 0.6 pad_add_fusion.2.scalar_ref
  32.3 4.0 %shard_map.75 = f32[64,1152]{1,0:T(8,128)} custom-call(s32[2]{0:T(128)} %pad_add_fusion.2.scalar_ref, bf16[256,1536]{1,0:T(8,128)(2,1)} %all_gather.3.q_ref, bf16[256,1024]{1,0:T(8,128)(2,1)} %bitcast.56, bf16[1024,256]{1,0:T(8,128)(2,1)} %v_ref.7), custom_call_target="tpu_custom_call" | custom-call | flops 268435456 | bytes 1540096 | tf_op jit(solution)/shard_map/pallas_call | solution.py:71
  36.3 0.1 collective-permute-start.2
  36.4 0.1 reshape.84
  36.5 1.0 %fusion.15 = (bf16[256,256]{1,0:T(8,128)(2,1)S(1)}, bf16[256,256]{1,0:T(8,128)(2,1)S(1)}) fusion(bf16[256,1536]{1,0:T(8,128)(2,1)} %all_gather.3.q_ref), kind=kLoop, calls=%fused_computation.43 | loop fusion | bytes 524288 | tf_op jit(solution)/shard_map/slice | solution.py:111
  37.6 0.0 copy-start.4
  37.6 0.7 %copy-done.4 = s32[256]{0:T(256)S(1)} copy-done((s32[256]{0:T(256)S(1)}, s32[256]{0:T(256)}, u32[]{:S(2)}) %copy-start.4) | copy-done | bytes 1048
  38.3 0.1 dynamic_slice.3
  38.3 0.1 fusion.9
  38.4 0.3 select_reduce_fusion
  38.7 0.3 convolution_bitcast_fusion
  39.0 0.2 copy.25
  39.2 0.1 reshape.85
  39.3 0.3 convert_reduce_fusion
  39.6 0.1 copy.29
  39.7 0.1 copy.28
  39.8 0.6 %pad_add_fusion.3.scalar_ref = s32[2]{0:T(128)} fusion(s32[1]{0:T(128)} %bitcast.11, s32[1]{0:T(128)} %bitcast.6), kind=kLoop, calls=%fused_computation.40 | loop fusion | flops 2 | bytes 16 | tf_op jit(solution)/shard_map/stack | solution.py:121
  40.4 3.9 %shard_map.76 = f32[64,1152]{1,0:T(8,128)} custom-call(s32[2]{0:T(128)} %pad_add_fusion.3.scalar_ref, bf16[256,1536]{1,0:T(8,128)(2,1)} %all_gather.3.q_ref, bf16[256,1024]{1,0:T(8,128)(2,1)} %bitcast.57, bf16[1024,256]{1,0:T(8,128)(2,1)} %v_ref.7), custom_call_target="tpu_custom_call" | custom-call | flops 268435456 | bytes 1540096 | tf_op jit(solution)/shard_map/pallas_call | solution.py:71
  44.3 0.0 collective-permute-done
  44.3 6.2 %collective-permute-done.1 = f32[64,1152]{1,0:T(8,128)S(1)} collective-permute-done((f32[64,1152]{1,0:T(8,128)}, f32[64,1152]{1,0:T(8,128)S(1)}, u32[]{:S(2)}, u32[]{:S(2)}) %collective-permute-start.1) | collective-permute-done | bytes 294944 | tf_op jit(solution)/shard_map/ppermute | solution.py:126
  50.5 3.8 %collective-permute-done.2 = f32[64,1152]{1,0:T(8,128)S(1)} collective-permute-done((f32[64,1152]{1,0:T(8,128)}, f32[64,1152]{1,0:T(8,128)S(1)}, u32[]{:S(2)}, u32[]{:S(2)}) %collective-permute-start.2) | collective-permute-done | bytes 294944 | tf_op jit(solution)/shard_map/ppermute | solution.py:126
  54.3 1.0 %fusion.10 = (f32[64,8]{1,0:T(8,128)S(1)}, f32[64,8]{1,0:T(8,128)S(1)}, f32[64,8]{1,0:T(8,128)S(1)}, f32[64,8]{1,0:T(8,128)S(1)}, f32[64,8]{1,0:T(8,128)S(1)}, /*index=5*/f32[64,8]{1,0:T(8,128)S(1)}) fusion(f32[64,1152]{1,0:T(8,128)} %shard_map.76, f32[64,1152]{1,0:T(8,128)S(1)} %collective-permute-done.2, f32[64,1152]{1,0:T(8,128)S(1)} %collective-permute-done.1, ...), kind=kLoop, calls=%fused_computation.24 | loop fusion | flops 9216 | bytes 32768 | tf_op jit(solution)/shard_map/add | solution.py:181
  55.2 0.1 div.11
  55.4 0.1 mul.90
  55.5 0.1 mul.93
  55.6 0.1 mul.96
  55.8 0.0 copy-start
  55.8 0.1 mul.99
  55.9 0.1 mul.102
  56.1 0.7 %copy-done = f32[64,1152]{1,0:T(8,128)S(1)} copy-done((f32[64,1152]{1,0:T(8,128)S(1)}, f32[64,1152]{1,0:T(8,128)}, u32[]{:S(2)}) %copy-start) | copy-done | bytes 294936
  56.8 1.0 %fusion.1 = bf16[64,1024]{1,0:T(8,128)(2,1)} fusion(f32[8,8,8,128]{3,2,1,0:T(8,128)S(1)} %bitcast.58, f32[8,8,8,128]{3,2,1,0:T(8,128)S(1)} %bitcast.63, f32[8,8,8,128]{3,2,1,0:T(8,128)S(1)} %bitcast.62, f32[8,8,8,128]{3,2,1,0:T(8,128)S(1)} %bitcast.61, f32[8,8,8,128]{3,2,1,0:T(8,128)S(1)} %bitcast.60, f32[64,1024]{1,0:T(8,128)S(1)} %reshape.85, ...), kind=kLoop, calls=%fused_computation.7 | loop fusion | flops 720896 | bytes 3014656 | tf_op jit(solution)/shard_map/convert_element_type | solution.py:183
  (4 shorter events, 0.1 us)
Async XLA Ops:
  0.7 2.1 %copy-start.1 = (bf16[64,1024]{1,0:T(8,128)(2,1)S(1)}, bf16[64,1024]{1,0:T(8,128)(2,1)}, u32[]{:S(2)}) copy-start(bf16[64,1024]{1,0:T(8,128)(2,1)} %param.7) | copy-start | bytes 393220
  0.7 2.1 %copy-start.2 = (bf16[64,256]{1,0:T(8,128)(2,1)S(1)}, bf16[64,256]{1,0:T(8,128)(2,1)}, u32[]{:S(2)}) copy-start(bf16[64,256]{1,0:T(8,128)(2,1)} %param.9) | copy-start | bytes 98308
  0.7 2.1 %copy-start.3 = (bf16[64,256]{1,0:T(8,128)(2,1)S(1)}, bf16[64,256]{1,0:T(8,128)(2,1)}, u32[]{:S(2)}) copy-start(bf16[64,256]{1,0:T(8,128)(2,1)} %param.8) | copy-start | bytes 98308
  23.3 21.1 %collective-permute-start = (f32[64,1152]{1,0:T(8,128)}, f32[64,1152]{1,0:T(8,128)S(1)}, u32[]{:S(2)}, u32[]{:S(2)}) collective-permute-start(f32[64,1152]{1,0:T(8,128)} %shard_map.73), channel_id=1, source_target_pairs={{0,1},{1,2},{2,3},{3,0},{4,5},{5,6},{6,7},{7,4},{8,9},{9,10},{10,1... | collective-permute-start | bytes 884744 | tf_op jit(solution)/shard_map/ppermute | solution.py:126
  29.3 21.2 %collective-permute-start.1 = (f32[64,1152]{1,0:T(8,128)}, f32[64,1152]{1,0:T(8,128)S(1)}, u32[]{:S(2)}, u32[]{:S(2)}) collective-permute-start(f32[64,1152]{1,0:T(8,128)} %shard_map.74), channel_id=1, source_target_pairs={{0,2},{1,3},{2,0},{3,1},{4,6},{5,7},{6,4},{7,5},{8,10},{9,11},{10,... | collective-permute-start | bytes 884744 | tf_op jit(solution)/shard_map/ppermute | solution.py:126
  36.3 18.0 %collective-permute-start.2 = (f32[64,1152]{1,0:T(8,128)}, f32[64,1152]{1,0:T(8,128)S(1)}, u32[]{:S(2)}, u32[]{:S(2)}) collective-permute-start(f32[64,1152]{1,0:T(8,128)} %shard_map.75), channel_id=1, source_target_pairs={{0,3},{1,0},{2,1},{3,2},{4,7},{5,4},{6,5},{7,6},{8,11},{9,8},{10,9... | collective-permute-start | bytes 884744 | tf_op jit(solution)/shard_map/ppermute | solution.py:126
  37.6 0.7 %copy-start.4 = (s32[256]{0:T(256)S(1)}, s32[256]{0:T(256)}, u32[]{:S(2)}) copy-start(s32[256]{0:T(256)} %param.12) | copy-start | bytes 3076
  55.8 1.0 %copy-start = (f32[64,1152]{1,0:T(8,128)S(1)}, f32[64,1152]{1,0:T(8,128)}, u32[]{:S(2)}) copy-start(f32[64,1152]{1,0:T(8,128)} %shard_map.76) | copy-start | bytes 884740

commit v4 on v3

--- a/solution.py
+++ b/solution.py
@@ -48,15 +48,32 @@
             f = jnp.exp(tm - m)
             numer = numer + nb * f
             denom = denom + db * f
+        top = jnp.floor(jnp.maximum(m, -60000.0) * 0.25 + 0.5) * 4.0
+        f = jnp.exp(m - top)
+        numer = numer * f
+        denom = denom * f
+        mean = numer / jnp.where(denom > 0, denom, 1.0)
         for r in range(group):
             h = g * group + r
-            out_ref[:, h * HEAD_DIM:(h + 1) * HEAD_DIM] = numer[r * rows:(r + 1) * rows]
-            extra = jnp.where(lane == h, denom[r * rows:(r + 1) * rows], extra)
-            extra = jnp.where(lane == heads_q + h, m[r * rows:(r + 1) * rows], extra)
+            rs = slice(r * rows, (r + 1) * rows)
+            out_ref[:, h * HEAD_DIM:(h + 1) * HEAD_DIM] = mean[rs]
+            extra = jnp.where((lane == h) | (lane == heads_q + h), denom[rs], extra)
+            extra = jnp.where(lane == 2 * heads_q + h, top[rs], extra)
     out_ref[:, heads_q * HEAD_DIM:] = extra
 
 
-def cache_partials(scalars, gathered, keys, values, block, chunked, qcols):
+def to_half(part, qcols, heads_q):
+    extra = part[:, qcols:]
+    rounded = extra.astype(jnp.float16)
+    rest = (extra - rounded.astype(jnp.float32)).astype(jnp.float16)
+    lane = lax.broadcasted_iota(jnp.int32, extra.shape, 1)
+    second = (lane >= heads_q) & (lane < 2 * heads_q)
+    return jnp.concatenate(
+        [part[:, :qcols].astype(jnp.float16), jnp.where(second, rest, rounded)], axis=1
+    )
+
+
+def cache_partials(scalars, gathered, keys, values, block, chunked, qcols, slot):
     rows, gcols = gathered.shape
     if chunked:
         rows = block
@@ -65,7 +82,7 @@
     heads_q = qcols // HEAD_DIM
     flops = 4 * rows * cache_rows * qcols
     if chunked:
-        q_map = lambda i, s: (s[1], 0)
+        q_map = lambda i, s: (s[slot], 0)
     else:
         q_map = lambda i, s: (i, 0)
     return pl.pallas_call(
@@ -115,13 +132,16 @@
     keys_t = cache_keys.T
 
     if seq_count <= 8:
+        shifts = list(range(1, seq_count)) + [0]
+        scalars = jnp.stack(
+            [live_rows] + [lax.rem(seq_rank + s, seq_count).astype(jnp.int32) for s in shifts]
+        )
         parts = []
-        for shift in list(range(1, seq_count)) + [0]:
-            chunk = lax.rem(seq_rank + shift, seq_count)
-            scalars = jnp.stack([live_rows, chunk.astype(jnp.int32)])
+        for slot, shift in enumerate(shifts):
             part = cache_partials(
-                scalars, gathered, keys_t, cache_values, own_count, True, qcols
+                scalars, gathered, keys_t, cache_values, own_count, True, qcols, slot + 1
             )
+            part = to_half(part, qcols, heads_q)
             if shift:
                 part = lax.ppermute(
                     part, "seq", [(i, (i + shift) % seq_count) for i in range(seq_count)]
@@ -130,13 +150,16 @@
     else:
         scalars = jnp.stack([live_rows, jnp.zeros((), jnp.int32)])
         partial = cache_partials(
-            scalars, gathered, keys_t, cache_values, min(join_rows, 256), False, qcols
-        )
-        recv = lax.all_to_all(partial, "seq", 0, 0, tiled=True)
+            scalars, gathered, keys_t, cache_values, min(join_rows, 256), False, qcols, 1
+        )
+        recv = lax.all_to_all(to_half(partial, qcols, heads_q), "seq", 0, 0, tiled=True)
         parts = [recv[j * own_count:(j + 1) * own_count] for j in range(seq_count)]
-    part_numer = [p[:, :qcols].reshape(own_count, heads_q, head_size) for p in parts]
-    part_denom = [p[:, qcols:qcols + heads_q] for p in parts]
-    part_max = [p[:, qcols + heads_q:qcols + 2 * heads_q] for p in parts]
+    parts = [p.astype(jnp.float32) for p in parts]
+    part_mean = [p[:, :qcols].reshape(own_count, heads_q, head_size) for p in parts]
+    part_denom = [
+        p[:, qcols:qcols + heads_q] + p[:, qcols + heads_q:qcols + 2 * heads_q] for p in parts
+    ]
+    part_max = [p[:, qcols + 2 * heads_q:qcols + 3 * heads_q] for p in parts]
 
     own_queries = new_queries.reshape(own_count, heads_kv, group_size, head_size)
     fresh_scores = (
@@ -175,10 +198,10 @@
     fresh_factor = jnp.exp(fresh_max - row_max)
     total_numer = fresh_numer * fresh_factor[..., None]
     total_denom = fresh_denom * fresh_factor
-    for n_j, d_j, m_j in zip(part_numer, part_denom, part_max):
-        f_j = jnp.exp(m_j - row_max)
-        total_numer = total_numer + n_j * f_j[..., None]
-        total_denom = total_denom + d_j * f_j
+    for o_j, d_j, m_j in zip(part_mean, part_denom, part_max):
+        w_j = jnp.exp(m_j - row_max) * d_j
+        total_numer = total_numer + o_j * w_j[..., None]
+        total_denom = total_denom + w_j
     attended = total_numer / total_denom[..., None]
     return attended.reshape(own_count, qcols).astype(jnp.bfloat16)
 

time: 58.1 us -> 58.5 us (level)
  the two profiles are of different devices: /device:TPU:11 before, /device:TPU:0 now
where the time goes in v4:
time: 58.5 us; the launch traced here: 58.2 us
  blocking collectives  21.7 us (37%)
  Pallas kernels  16.3 us (28%)
  local copies, waits for them, and re-layouts  6.74 us (12%)
  waiting for transfers between devices  6.09 us (10%)
  starting transfers between devices  3.99 us (7%)
  other arithmetic  1.8 us (3%)
  between operations  0.92 us (2%)
  matrix products  0.62 us (1%)
    all_gather x1, blocking collectives, on_device(): gathered = lax.all_gather(packed, 'seq', axis=0, tiled=True)  21.7 us
    pallas_call x4, Pallas kernels, cache_partials(): pl.pallas_call(cache_kernel, grid_spec=pltpu.PrefetchScalarGridSpec(num_s...  16.3 us
    ppermute x3, waiting for transfers between devices, on_device(): lax.ppermute(part, 'seq', [(i, (i + shift) % seq_count) for i in range(se...  6.09 us
    ppermute x3, starting transfers between devices, on_device(): lax.ppermute(part, 'seq', [(i, (i + shift) % seq_count) for i in range(se...  3.99 us
    unnamed x17, local copies, waits for them, and re-layouts  3.73 us
  transfers between devices with their start and end apart: 3, of which 2 were waited for; matrix products, arithmetic and copies ran while one was open for 5% of the time, Pallas kernels for 0%

profile of v4, /device:TPU:0, one launch (start us, length us, event | category | flops | bytes accessed | tf_op | source)
XLA Modules:
  0.0 58.2 jit_solution(9991288970400376865)
XLA Ops:
  0.7 0.0 copy-start.4
  0.7 0.0 copy-start.5
  0.7 0.0 copy-start.6
  0.7 2.1 %copy.26 = bf16[1024,256]{0,1:T(8,128)(2,1)} copy(bf16[1024,256]{1,0:T(8,128)(2,1)} %param.10) | data formatting | bytes 1048576 | tf_op args[3]
  2.8 0.0 copy-done.4
  2.8 0.0 copy-done.5
  2.8 0.0 copy-done.6
  2.8 21.7 %all_gather.3.q_ref = bf16[256,1536]{1,0:T(8,128)(2,1)} all-gather(bf16[64,1536]{1,0:T(8,128)(2,1)S(1)} %pad_maximum_fusion), channel_id=1, replica_groups=mesh['group'=2,'head'=4,'seq'=4] {'seq'}, dimensions={0}, use_global_device_ids=true | all-gather | bytes 983040 | tf_op jit(solution)/shard_map/all_gather | solution.py:126
  24.5 0.6 %stack.23.scalar_ref = s32[5]{0:T(128)} concatenate(s32[1]{0:T(128)} %bitcast.6, s32[1]{0:T(128)} %bitcast.7, s32[1]{0:T(128)} %bitcast.8, s32[1]{0:T(128)} %bitcast.9, s32[1]{0:T(128)} %bitcast.10), dimensions={0} | concatenate | bytes 40 | tf_op jit(solution)/shard_map/stack | solution.py:136
  25.1 4.0 %shard_map.75 = f32[64,1152]{1,0:T(8,128)} custom-call(s32[5]{0:T(128)} %stack.23.scalar_ref, bf16[256,1536]{1,0:T(8,128)(2,1)} %all_gather.3.q_ref, bf16[256,1024]{1,0:T(8,128)(2,1)} %bitcast.54, bf16[1024,256]{1,0:T(8,128)(2,1)} %v_ref.7), custom_call_target="tpu_custom_call" | custom-call | flops 268435456 | bytes 1540096 | tf_op jit(solution)/shard_map/pallas_call | solution.py:88
  29.2 4.1 %shard_map.74 = f32[64,1152]{1,0:T(8,128)} custom-call(s32[5]{0:T(128)} %stack.23.scalar_ref, bf16[256,1536]{1,0:T(8,128)(2,1)} %all_gather.3.q_ref, bf16[256,1024]{1,0:T(8,128)(2,1)} %bitcast.55, bf16[1024,256]{1,0:T(8,128)(2,1)} %v_ref.7), custom_call_target="tpu_custom_call" | custom-call | flops 268435456 | bytes 1540096 | tf_op jit(solution)/shard_map/pallas_call | solution.py:88
  33.2 4.0 %shard_map.73 = f32[64,1152]{1,0:T(8,128)} custom-call(s32[5]{0:T(128)} %stack.23.scalar_ref, bf16[256,1536]{1,0:T(8,128)(2,1)} %all_gather.3.q_ref, bf16[256,1024]{1,0:T(8,128)(2,1)} %bitcast.56, bf16[1024,256]{1,0:T(8,128)(2,1)} %v_ref.7), custom_call_target="tpu_custom_call" | custom-call | flops 268435456 | bytes 1540096 | tf_op jit(solution)/shard_map/pallas_call | solution.py:88
  37.3 0.0 copy-start.3
  37.3 0.0 copy-start.1
  37.3 0.0 copy-start.2
  37.3 4.2 %shard_map.76 = f32[64,1152]{1,0:T(8,128)} custom-call(s32[5]{0:T(128)} %stack.23.scalar_ref, bf16[256,1536]{1,0:T(8,128)(2,1)} %all_gather.3.q_ref, bf16[256,1024]{1,0:T(8,128)(2,1)} %bitcast.57, bf16[1024,256]{1,0:T(8,128)(2,1)} %v_ref.7), custom_call_target="tpu_custom_call" | custom-call | flops 268435456 | bytes 1540096 | tf_op jit(solution)/shard_map/pallas_call | solution.py:88
  41.5 0.0 copy-done.3
  41.5 0.0 copy-start
  41.5 0.0 copy-done.1
  41.5 0.0 copy-done.2
  41.5 0.9 %copy-done = f32[64,1152]{1,0:T(8,128)S(1)} copy-done((f32[64,1152]{1,0:T(8,128)S(1)}, f32[64,1152]{1,0:T(8,128)}, u32[]{:S(2)}) %copy-start) | copy-done | bytes 294936
  42.5 0.1 collective-permute-start
  42.6 3.9 %collective-permute-start.2 = (f16[64,1152]{1,0:T(8,128)(2,1)S(1)}, f16[64,1152]{1,0:T(8,128)(2,1)S(1)}, u32[]{:S(2)}, u32[]{:S(2)}) collective-permute-start(f16[64,1152]{1,0:T(8,128)(2,1)S(1)} %pad_maximum_fusion.3), channel_id=1, source_target_pairs={{0,3},{1,0},{2,1},{3,2},{4,7},{5,4},{6,5},{7,6},{8,11},{9,8},{10,9... | collective-permute-start | bytes 442376 | tf_op jit(solution)/shard_map/ppermute | solution.py:146
  46.6 0.1 collective-permute-start.1
  46.7 0.1 reshape.84
  46.7 1.0 %fusion.24 = (bf16[256,256]{1,0:T(8,128)(2,1)S(1)}, bf16[256,256]{1,0:T(8,128)(2,1)S(1)}) fusion(bf16[256,1536]{1,0:T(8,128)(2,1)} %all_gather.3.q_ref), kind=kLoop, calls=%fused_computation.60 | loop fusion | bytes 524288 | tf_op jit(solution)/shard_map/slice | solution.py:128
  47.8 0.0 copy-start.7
  47.8 0.7 %copy-done.7 = s32[256]{0:T(256)S(1)} copy-done((s32[256]{0:T(256)S(1)}, s32[256]{0:T(256)}, u32[]{:S(2)}) %copy-start.7) | copy-done | bytes 1048
  48.5 0.1 dynamic_slice.3
  48.6 0.1 fusion.9
  48.7 0.3 select_reduce_fusion
  49.0 0.3 convert_reduce_fusion
  49.3 0.3 convolution_bitcast_fusion
  49.6 0.2 copy.25
  49.8 0.1 reshape.85
  49.9 0.1 copy.29
  50.0 0.1 copy.28
  50.1 0.5 collective-permute-done
  50.6 0.0 collective-permute-done.2
  50.7 5.6 %collective-permute-done.1 = f16[64,1152]{1,0:T(8,128)(2,1)S(1)} collective-permute-done((f16[64,1152]{1,0:T(8,128)(2,1)S(1)}, f16[64,1152]{1,0:T(8,128)(2,1)S(1)}, u32[]{:S(2)}, u32[]{:S(2)}) %collective-permute-start.1) | collective-permute-done | bytes 147488 | tf_op jit(solution)/shard_map/ppermute | solution.py:146
  56.3 0.1 add_add_fusion
  56.4 0.1 div.11
  56.5 0.1 mul.90
  56.7 0.1 mul.94
  56.8 0.1 mul.98
  56.9 0.1 mul.102
  57.1 0.1 mul.106
  57.2 1.0 %fusion.1 = bf16[64,1024]{1,0:T(8,128)(2,1)} fusion(f32[8,8,8,128]{3,2,1,0:T(8,128)S(1)} %bitcast.58, f32[8,8,8,128]{3,2,1,0:T(8,128)S(1)} %bitcast.63, f32[8,8,8,128]{3,2,1,0:T(8,128)S(1)} %bitcast.62, f32[8,8,8,128]{3,2,1,0:T(8,128)S(1)} %bitcast.61, f32[8,8,8,128]{3,2,1,0:T(8,128)S(1)} %bitcast.60, f32[64,1024]{1,0:T(8,128)S(1)} %reshape.85, ...), kind=kLoop, calls=%fused_computation.7 | loop fusion | flops 720896 | bytes 3014656 | tf_op jit(solution)/shard_map/convert_element_type | solution.py:206
  (17 shorter events, 0.4 us)
Async XLA Ops:
  0.7 2.1 %copy-start.4 = (bf16[64,1024]{1,0:T(8,128)(2,1)S(1)}, bf16[64,1024]{1,0:T(8,128)(2,1)}, u32[]{:S(2)}) copy-start(bf16[64,1024]{1,0:T(8,128)(2,1)} %param.7) | copy-start | bytes 393220
  0.7 2.1 %copy-start.5 = (bf16[64,256]{1,0:T(8,128)(2,1)S(1)}, bf16[64,256]{1,0:T(8,128)(2,1)}, u32[]{:S(2)}) copy-start(bf16[64,256]{1,0:T(8,128)(2,1)} %param.9) | copy-start | bytes 98308
  0.7 2.1 %copy-start.6 = (bf16[64,256]{1,0:T(8,128)(2,1)S(1)}, bf16[64,256]{1,0:T(8,128)(2,1)}, u32[]{:S(2)}) copy-start(bf16[64,256]{1,0:T(8,128)(2,1)} %param.8) | copy-start | bytes 98308
  37.3 4.2 %copy-start.3 = (f32[64,1152]{1,0:T(8,128)S(1)}, f32[64,1152]{1,0:T(8,128)}, u32[]{:S(2)}) copy-start(f32[64,1152]{1,0:T(8,128)} %shard_map.73) | copy-start | bytes 884740
  37.3 4.2 %copy-start.1 = (f32[64,1152]{1,0:T(8,128)S(1)}, f32[64,1152]{1,0:T(8,128)}, u32[]{:S(2)}) copy-start(f32[64,1152]{1,0:T(8,128)} %shard_map.74) | copy-start | bytes 884740
  37.3 4.2 %copy-start.2 = (f32[64,1152]{1,0:T(8,128)S(1)}, f32[64,1152]{1,0:T(8,128)}, u32[]{:S(2)}) copy-start(f32[64,1152]{1,0:T(8,128)} %shard_map.75) | copy-start | bytes 884740
  41.5 1.0 %copy-start = (f32[64,1152]{1,0:T(8,128)S(1)}, f32[64,1152]{1,0:T(8,128)}, u32[]{:S(2)}) copy-start(f32[64,1152]{1,0:T(8,128)} %shard_map.76) | copy-start | bytes 884740
  42.5 8.1 %collective-permute-start = (f16[64,1152]{1,0:T(8,128)(2,1)S(1)}, f16[64,1152]{1,0:T(8,128)(2,1)S(1)}, u32[]{:S(2)}, u32[]{:S(2)}) collective-permute-start(f16[64,1152]{1,0:T(8,128)(2,1)S(1)} %pad_maximum_fusion.1), channel_id=1, source_target_pairs={{0,1},{1,2},{2,3},{3,0},{4,5},{5,6},{6,7},{7,4},{8,9},{9,10},{10,1... | collective-permute-start | bytes 442376 | tf_op jit(solution)/shard_map/ppermute | solution.py:146
  42.6 8.0 %collective-permute-start.2 = (f16[64,1152]{1,0:T(8,128)(2,1)S(1)}, f16[64,1152]{1,0:T(8,128)(2,1)S(1)}, u32[]{:S(2)}, u32[]{:S(2)}) collective-permute-start(f16[64,1152]{1,0:T(8,128)(2,1)S(1)} %pad_maximum_fusion.3), channel_id=1, source_target_pairs={{0,3},{1,0},{2,1},{3,2},{4,7},{5,4},{6,5},{7,6},{8,11},{9,8},{10,9... | collective-permute-start | bytes 442376 | tf_op jit(solution)/shard_map/ppermute | solution.py:146
  46.6 9.7 %collective-permute-start.1 = (f16[64,1152]{1,0:T(8,128)(2,1)S(1)}, f16[64,1152]{1,0:T(8,128)(2,1)S(1)}, u32[]{:S(2)}, u32[]{:S(2)}) collective-permute-start(f16[64,1152]{1,0:T(8,128)(2,1)S(1)} %pad_maximum_fusion.2), channel_id=1, source_target_pairs={{0,2},{1,3},{2,0},{3,1},{4,6},{5,7},{6,4},{7,5},{8,10},{9,11},{10,... | collective-permute-start | bytes 442376 | tf_op jit(solution)/shard_map/ppermute | solution.py:146
  47.8 0.7 %copy-start.7 = (s32[256]{0:T(256)S(1)}, s32[256]{0:T(256)}, u32[]{:S(2)}) copy-start(s32[256]{0:T(256)} %param.12) | copy-start | bytes 3076

commit v5 on v4

--- a/solution.py
+++ b/solution.py
@@ -12,13 +12,14 @@
 NEG_FILL = -1e30
 
 
-def cache_kernel(scalar_ref, q_ref, kt_ref, v_ref, out_ref):
+def cache_kernel(scalar_ref, q_ref, k_ref, v_ref, out_ref):
     live = scalar_ref[0]
     rows = q_ref.shape[0]
     heads_q = (out_ref.shape[1] - 128) // HEAD_DIM
-    heads_kv = kt_ref.shape[0] // HEAD_DIM
+    heads_kv = k_ref.shape[1] // HEAD_DIM
     group = heads_q // heads_kv
-    tiles = kt_ref.shape[1] // SUB
+    tiles = k_ref.shape[0] // SUB
+    ones = jnp.ones((SUB, 128), jnp.bfloat16)
     scale = HEAD_DIM ** (-0.5)
     col = lax.broadcasted_iota(jnp.int32, (group * rows, SUB), 1)
     lane = lax.broadcasted_iota(jnp.int32, (rows, 128), 1)
@@ -30,14 +31,16 @@
         )
         maxes, numers, denoms = [], [], []
         for b in range(tiles):
-            kb = kt_ref[g * HEAD_DIM:(g + 1) * HEAD_DIM, b * SUB:(b + 1) * SUB]
-            s = jnp.dot(qg, kb, preferred_element_type=jnp.float32) * scale
+            kb = k_ref[b * SUB:(b + 1) * SUB, g * HEAD_DIM:(g + 1) * HEAD_DIM]
+            s = lax.dot_general(
+                qg, kb, (((1,), (1,)), ((), ())), preferred_element_type=jnp.float32
+            ) * scale
             ok = (col + b * SUB) < live
             tm = jnp.max(jnp.where(ok, s, NEG_FILL), axis=1, keepdims=True)
             w = jnp.exp(jnp.where(ok, s - tm, NEG_FILL)).astype(jnp.bfloat16)
             vb = v_ref[b * SUB:(b + 1) * SUB, g * HEAD_DIM:(g + 1) * HEAD_DIM]
             numers.append(jnp.dot(w, vb, preferred_element_type=jnp.float32))
-            denoms.append(jnp.sum(w.astype(jnp.float32), axis=1, keepdims=True))
+            denoms.append(jnp.dot(w, ones, preferred_element_type=jnp.float32)[:, :1])
             maxes.append(tm)
         m = maxes[0]
         for tm in maxes[1:]:
@@ -73,26 +76,21 @@
     )
 
 
-def cache_partials(scalars, gathered, keys, values, block, chunked, qcols, slot):
-    rows, gcols = gathered.shape
-    if chunked:
-        rows = block
-    kcols, cache_rows = keys.shape
+def cache_partials(scalars, gathered, keys, values, block, first_slot, count, qcols):
+    gcols = gathered.shape[1]
+    rows = block * count
+    cache_rows, kcols = keys.shape
     out_cols = qcols + 128
     heads_q = qcols // HEAD_DIM
-    flops = 4 * rows * cache_rows * qcols
-    if chunked:
-        q_map = lambda i, s: (s[slot], 0)
-    else:
-        q_map = lambda i, s: (i, 0)
+    flops = 4 * rows * cache_rows * qcols + 2 * rows * cache_rows * 128 * (qcols // HEAD_DIM)
     return pl.pallas_call(
         cache_kernel,
         grid_spec=pltpu.PrefetchScalarGridSpec(
             num_scalar_prefetch=1,
-            grid=(rows // block,),
+            grid=(count,),
             in_specs=[
-                pl.BlockSpec((block, gcols), q_map),
-                pl.BlockSpec((kcols, cache_rows), lambda i, s: (0, 0)),
+                pl.BlockSpec((block, gcols), lambda i, s: (s[first_slot + i], 0)),
+                pl.BlockSpec((cache_rows, kcols), lambda i, s: (0, 0)),
                 pl.BlockSpec((cache_rows, kcols), lambda i, s: (0, 0)),
             ],
             out_specs=pl.BlockSpec((block, out_cols), lambda i, s: (i, 0)),
@@ -129,28 +127,33 @@
 
     live_rows = jnp.clip(cache_length[0] - seq_rank * cache_rows, 0, cache_rows)
     live_rows = live_rows.astype(jnp.int32)
-    keys_t = cache_keys.T
 
     if seq_count <= 8:
-        shifts = list(range(1, seq_count)) + [0]
+        shifts = list(range(1, seq_count))
         scalars = jnp.stack(
-            [live_rows] + [lax.rem(seq_rank + s, seq_count).astype(jnp.int32) for s in shifts]
+            [live_rows]
+            + [lax.rem(seq_rank + s, seq_count).astype(jnp.int32) for s in shifts]
+            + [seq_rank.astype(jnp.int32)]
+        )
+        remote = cache_partials(
+            scalars, gathered, cache_keys, cache_values, own_count, 1, seq_count - 1, qcols
         )
         parts = []
-        for slot, shift in enumerate(shifts):
-            part = cache_partials(
-                scalars, gathered, keys_t, cache_values, own_count, True, qcols, slot + 1
-            )
-            part = to_half(part, qcols, heads_q)
-            if shift:
-                part = lax.ppermute(
+        for k, shift in enumerate(shifts):
+            part = to_half(remote[k * own_count:(k + 1) * own_count], qcols, heads_q)
+            parts.append(
+                lax.ppermute(
                     part, "seq", [(i, (i + shift) % seq_count) for i in range(seq_count)]
                 )
-            parts.append(part)
+            )
+        own = cache_partials(
+            scalars, gathered, cache_keys, cache_values, own_count, seq_count, 1, qcols
+        )
+        parts.append(to_half(own, qcols, heads_q))
     else:
-        scalars = jnp.stack([live_rows, jnp.zeros((), jnp.int32)])
+        scalars = jnp.stack([live_rows] + [jnp.int32(j) for j in range(join_rows // 256)])
         partial = cache_partials(
-            scalars, gathered, keys_t, cache_values, min(join_rows, 256), False, qcols, 1
+            scalars, gathered, cache_keys, cache_values, 256, 1, join_rows // 256, qcols
         )
         recv = lax.all_to_all(to_half(partial, qcols, heads_q), "seq", 0, 0, tiled=True)
         parts = [recv[j * own_count:(j + 1) * own_count] for j in range(seq_count)]

time: 58.5 us -> 56.5 us (0.966)
  other arithmetic: 1.8 us -> 4.67 us
  local copies, waits for them, and re-layouts: 6.74 us -> 5.01 us
  waiting for transfers between devices: 6.09 us -> 4.61 us
  starting transfers between devices: 3.99 us -> 3.02 us
  Pallas kernels: 16.3 us -> 15.5 us
    unnamed x17 -> x8, local copies, waits for them, and re-layouts: 3.73 us -> 1.92 us
    ppermute x3, waiting for transfers between devices: 6.09 us -> 4.61 us  [on_device(): lax.ppermute(part, 'seq', [(i, (i + shift) % seq_count) for i in range(se...]
    another operation x4 -> x2, other arithmetic: 0.07 us -> 1.23 us
    ppermute x3, starting transfers between devices: 3.99 us -> 3.02 us  [on_device(): lax.ppermute(part, 'seq', [(i, (i + shift) % seq_count) for i in range(se...]
    concatenate x1, other arithmetic: 0.02 us -> 0.94 us  [on_device(): packed = jnp.concatenate([new_queries, new_keys, new_values], axis=1)]
    pallas_call x4 -> x2, Pallas kernels: 16.3 us -> 15.5 us  [cache_partials(): pl.pallas_call(cache_kernel, grid_spec=pltpu.PrefetchScalarGridSpec(num_s...]
    select_n x1, other arithmetic: 0.02 us -> 0.81 us  [to_half(): jnp.where(second, rest, rounded)]
  transfers between devices with their start and end apart: 3 -> 3, of which waited for: 2 -> 1; matrix products, arithmetic and copies ran while one was open for 5% -> 5% of each run, Pallas kernels for 0% -> 0%
where the time goes in v5:
time: 56.5 us; the launch traced here: 56 us
  blocking collectives  21.7 us (38%)
  Pallas kernels  15.5 us (27%)
  local copies, waits for them, and re-layouts  5.01 us (9%)
  other arithmetic  4.67 us (8%)
  waiting for transfers between devices  4.61 us (8%)
  starting transfers between devices  3.02 us (5%)
  between operations  0.86 us (2%)
  matrix products  0.62 us (1%)
    all_gather x1, blocking collectives, on_device(): gathered = lax.all_gather(packed, 'seq', axis=0, tiled=True)  21.7 us
    pallas_call x2, Pallas kernels, cache_partials(): pl.pallas_call(cache_kernel, grid_spec=pltpu.PrefetchScalarGridSpec(num_s...  15.5 us
    ppermute x3, waiting for transfers between devices, on_device(): lax.ppermute(part, 'seq', [(i, (i + shift) % seq_count) for i in range(se...  4.61 us
    ppermute x3, starting transfers between devices, on_device(): lax.ppermute(part, 'seq', [(i, (i + shift) % seq_count) for i in range(se...  3.02 us
    unnamed x8, local copies, waits for them, and re-layouts  1.92 us
    another operation x2, other arithmetic  1.23 us
  transfers between devices with their start and end apart: 3, of which 1 were waited for; matrix products, arithmetic and copies ran while one was open for 5% of the time, Pallas kernels for 0%

profile of v5, /device:TPU:0, one launch (start us, length us, event | category | flops | bytes accessed | tf_op | source)
XLA Modules:
  0.0 56.0 jit_solution(13300215711775477190)
XLA Ops:
  0.0 0.0 copy-start.2
  0.7 0.1 copy-done.2
  0.8 0.9 %pad_maximum_fusion = bf16[64,1536]{1,0:T(8,128)(2,1)S(1)} fusion(bf16[64,256]{1,0:T(8,128)(2,1)S(1)} %copy-done.2, bf16[64,256]{1,0:T(8,128)(2,1)} %param.8, bf16[64,1024]{1,0:T(8,128)(2,1)} %param.7), kind=kLoop, calls=%fused_computation.18 | loop fusion | flops 589824 | bytes 393216 | tf_op jit(solution)/shard_map/concatenate | solution.py:123
  1.7 21.7 %all_gather.3.q_ref = bf16[256,1536]{1,0:T(8,128)(2,1)} all-gather(bf16[64,1536]{1,0:T(8,128)(2,1)S(1)} %pad_maximum_fusion), channel_id=1, replica_groups=mesh['group'=2,'head'=4,'seq'=4] {'seq'}, dimensions={0}, use_global_device_ids=true | all-gather | bytes 983040 | tf_op jit(solution)/shard_map/all_gather | solution.py:124
  23.4 0.6 %stack.23.scalar_ref = s32[5]{0:T(128)} concatenate(s32[1]{0:T(128)} %bitcast.6, s32[1]{0:T(128)} %bitcast.7, s32[1]{0:T(128)} %bitcast.8, s32[1]{0:T(128)} %bitcast.9, s32[1]{0:T(128)} %bitcast.10), dimensions={0} | concatenate | bytes 40 | tf_op jit(solution)/shard_map/stack | solution.py:133
  24.0 5.2 %shard_map.74 = f32[64,1152]{1,0:T(8,128)} custom-call(s32[5]{0:T(128)} %stack.23.scalar_ref, bf16[256,1536]{1,0:T(8,128)(2,1)} %all_gather.3.q_ref, bf16[1024,256]{1,0:T(8,128)(2,1)} %k_ref.3, bf16[1024,256]{1,0:T(8,128)(2,1)} %v_ref.3), custom_call_target="tpu_custom_call" | custom-call | flops 402653184 | bytes 1540096 | tf_op jit(solution)/shard_map/pallas_call | solution.py:86
  29.2 10.3 %shard_map.73 = f32[192,1152]{1,0:T(8,128)} custom-call(s32[5]{0:T(128)} %stack.23.scalar_ref, bf16[256,1536]{1,0:T(8,128)(2,1)} %all_gather.3.q_ref, bf16[1024,256]{1,0:T(8,128)(2,1)} %k_ref.3, bf16[1024,256]{1,0:T(8,128)(2,1)} %v_ref.3), custom_call_target="tpu_custom_call" | custom-call | flops 1207959552 | bytes 2523136 | tf_op jit(solution)/shard_map/pallas_call | solution.py:86
  39.5 1.2 %convert.8 = f16[192,1152]{1,0:T(8,128)(2,1)S(1)} convert(f32[192,1152]{1,0:T(8,128)} %shard_map.73) | non-fusion elementwise | flops 221184 | bytes 1327104 | tf_op jit(solution)/shard_map/convert.3
  40.7 0.0 copy-start
  40.7 0.1 fusion.25
  40.8 0.9 %copy-done = f32[64,1152]{1,0:T(8,128)S(1)} copy-done((f32[64,1152]{1,0:T(8,128)S(1)}, f32[64,1152]{1,0:T(8,128)}, u32[]{:S(2)}) %copy-start) | copy-done | bytes 294936
  41.7 0.8 %fusion.15 = (f16[64,128]{1,0:T(8,128)(2,1)S(1)}, f16[64,128]{1,0:T(8,128)(2,1)S(1)}, f16[64,128]{1,0:T(8,128)(2,1)S(1)}, f16[64,128]{1,0:T(8,128)(2,1)S(1)}) fusion(f32[192,1152]{1,0:T(8,128)} %shard_map.73, pred[128]{0:T(512)(128)(4,1)S(1)} %compare_and_fusion, f32[64,1152]{1,0:T(8,128)S(1)} %copy-done), kind=kLoop, calls=%fused_computation.49 | loop fusion | flops 163840 | bytes 196736 | tf_op jit(solution)/shard_map/jit(_where)/select_n | solution.py:75
  42.5 0.9 %collective-permute-start.1 = (f16[64,1152]{1,0:T(8,128)(2,1)S(1)}, f16[64,1152]{1,0:T(8,128)(2,1)S(1)}, u32[]{:S(2)}, u32[]{:S(2)}) collective-permute-start(f16[64,1152]{1,0:T(8,128)(2,1)S(1)} %pad_maximum_fusion.2), channel_id=1, source_target_pairs={{0,2},{1,3},{2,0},{3,1},{4,6},{5,7},{6,4},{7,5},{8,10},{9,11},{10,... | collective-permute-start | bytes 442376 | tf_op jit(solution)/shard_map/ppermute | solution.py:145
  43.5 1.6 %collective-permute-start.2 = (f16[64,1152]{1,0:T(8,128)(2,1)S(1)}, f16[64,1152]{1,0:T(8,128)(2,1)S(1)}, u32[]{:S(2)}, u32[]{:S(2)}) collective-permute-start(f16[64,1152]{1,0:T(8,128)(2,1)S(1)} %pad_maximum_fusion.3), channel_id=1, source_target_pairs={{0,3},{1,0},{2,1},{3,2},{4,7},{5,4},{6,5},{7,6},{8,11},{9,8},{10,9... | collective-permute-start | bytes 442376 | tf_op jit(solution)/shard_map/ppermute | solution.py:145
  45.0 0.0 copy-start.1
  45.1 0.6 %collective-permute-start = (f16[64,1152]{1,0:T(8,128)(2,1)S(1)}, f16[64,1152]{1,0:T(8,128)(2,1)S(1)}, u32[]{:S(2)}, u32[]{:S(2)}) collective-permute-start(f16[64,1152]{1,0:T(8,128)(2,1)S(1)} %pad_maximum_fusion.1), channel_id=1, source_target_pairs={{0,1},{1,2},{2,3},{3,0},{4,5},{5,6},{6,7},{7,4},{8,9},{9,10},{10,1... | collective-permute-start | bytes 442376 | tf_op jit(solution)/shard_map/ppermute | solution.py:145
  45.6 0.3 copy-done.1
  45.9 0.1 reshape.84
  46.0 1.0 %fusion.24 = (bf16[256,256]{1,0:T(8,128)(2,1)S(1)}, bf16[256,256]{1,0:T(8,128)(2,1)S(1)}) fusion(bf16[256,1536]{1,0:T(8,128)(2,1)} %all_gather.3.q_ref), kind=kLoop, calls=%fused_computation.57 | loop fusion | bytes 524288 | tf_op jit(solution)/shard_map/slice | solution.py:126
  47.1 0.0 copy-start.3
  47.1 0.7 %copy-done.3 = s32[256]{0:T(256)S(1)} copy-done((s32[256]{0:T(256)S(1)}, s32[256]{0:T(256)}, u32[]{:S(2)}) %copy-start.3) | copy-done | bytes 1048
  47.8 0.1 dynamic_slice.3
  47.9 0.1 fusion.9
  48.0 0.3 select_reduce_fusion
  48.3 0.3 convert_reduce_fusion
  48.6 0.3 convolution_bitcast_fusion
  48.9 0.2 copy.23
  49.0 0.1 reshape.85
  49.2 0.1 copy.26
  49.2 0.1 copy.25
  49.4 4.6 %collective-permute-done.1 = f16[64,1152]{1,0:T(8,128)(2,1)S(1)} collective-permute-done((f16[64,1152]{1,0:T(8,128)(2,1)S(1)}, f16[64,1152]{1,0:T(8,128)(2,1)S(1)}, u32[]{:S(2)}, u32[]{:S(2)}) %collective-permute-start.1) | collective-permute-done | bytes 147488 | tf_op jit(solution)/shard_map/ppermute | solution.py:145
  54.0 0.0 collective-permute-done.2
  54.0 0.0 collective-permute-done
  54.1 0.1 add_add_fusion
  54.2 0.1 div.11
  54.3 0.1 mul.90
  54.5 0.1 mul.94
  54.6 0.1 mul.98
  54.8 0.1 mul.102
  54.9 0.1 mul.106
  55.0 1.0 %fusion.1 = bf16[64,1024]{1,0:T(8,128)(2,1)} fusion(f32[8,8,8,128]{3,2,1,0:T(8,128)S(1)} %bitcast.53, f32[8,8,8,128]{3,2,1,0:T(8,128)S(1)} %bitcast.58, f32[8,8,8,128]{3,2,1,0:T(8,128)S(1)} %bitcast.57, f32[8,8,8,128]{3,2,1,0:T(8,128)S(1)} %bitcast.56, f32[8,8,8,128]{3,2,1,0:T(8,128)S(1)} %bitcast.55, f32[64,1024]{1,0:T(8,128)S(1)} %reshape.85, ...), kind=kLoop, calls=%fused_computation.7 | loop fusion | flops 720896 | bytes 3014656 | tf_op jit(solution)/shard_map/convert_element_type | solution.py:209
  (12 shorter events, 0.3 us)
Async XLA Ops:
  0.0 0.8 %copy-start.2 = (bf16[64,256]{1,0:T(8,128)(2,1)S(1)}, bf16[64,256]{1,0:T(8,128)(2,1)}, u32[]{:S(2)}) copy-start(bf16[64,256]{1,0:T(8,128)(2,1)} %param.9) | copy-start | bytes 98308
  40.7 1.0 %copy-start = (f32[64,1152]{1,0:T(8,128)S(1)}, f32[64,1152]{1,0:T(8,128)}, u32[]{:S(2)}) copy-start(f32[64,1152]{1,0:T(8,128)} %shard_map.74) | copy-start | bytes 884740
  42.5 11.4 %collective-permute-start.1 = (f16[64,1152]{1,0:T(8,128)(2,1)S(1)}, f16[64,1152]{1,0:T(8,128)(2,1)S(1)}, u32[]{:S(2)}, u32[]{:S(2)}) collective-permute-start(f16[64,1152]{1,0:T(8,128)(2,1)S(1)} %pad_maximum_fusion.2), channel_id=1, source_target_pairs={{0,2},{1,3},{2,0},{3,1},{4,6},{5,7},{6,4},{7,5},{8,10},{9,11},{10,... | collective-permute-start | bytes 442376 | tf_op jit(solution)/shard_map/ppermute | solution.py:145
  43.5 10.5 %collective-permute-start.2 = (f16[64,1152]{1,0:T(8,128)(2,1)S(1)}, f16[64,1152]{1,0:T(8,128)(2,1)S(1)}, u32[]{:S(2)}, u32[]{:S(2)}) collective-permute-start(f16[64,1152]{1,0:T(8,128)(2,1)S(1)} %pad_maximum_fusion.3), channel_id=1, source_target_pairs={{0,3},{1,0},{2,1},{3,2},{4,7},{5,4},{6,5},{7,6},{8,11},{9,8},{10,9... | collective-permute-start | bytes 442376 | tf_op jit(solution)/shard_map/ppermute | solution.py:145
  45.0 0.9 %copy-start.1 = (bf16[64,1024]{1,0:T(8,128)(2,1)S(1)}, bf16[64,1024]{1,0:T(8,128)(2,1)}, u32[]{:S(2)}) copy-start(bf16[64,1024]{1,0:T(8,128)(2,1)} %param.7) | copy-start | bytes 393220
  45.1 9.0 %collective-permute-start = (f16[64,1152]{1,0:T(8,128)(2,1)S(1)}, f16[64,1152]{1,0:T(8,128)(2,1)S(1)}, u32[]{:S(2)}, u32[]{:S(2)}) collective-permute-start(f16[64,1152]{1,0:T(8,128)(2,1)S(1)} %pad_maximum_fusion.1), channel_id=1, source_target_pairs={{0,1},{1,2},{2,3},{3,0},{4,5},{5,6},{6,7},{7,4},{8,9},{9,10},{10,1... | collective-permute-start | bytes 442376 | tf_op jit(solution)/shard_map/ppermute | solution.py:145
  47.1 0.7 %copy-start.3 = (s32[256]{0:T(256)S(1)}, s32[256]{0:T(256)}, u32[]{:S(2)}) copy-start(s32[256]{0:T(256)} %param.12) | copy-start | bytes 3076

commit v6 on v5

--- a/solution.py
+++ b/solution.py
@@ -12,41 +12,49 @@
 NEG_FILL = -1e30
 
 
-def cache_kernel(scalar_ref, q_ref, k_ref, v_ref, out_ref):
+def cache_kernel(pieces, scalar_ref, q_ref, k_ref, v_ref, out_ref):
     live = scalar_ref[0]
-    rows = q_ref.shape[0]
+    rows = out_ref.shape[0]
+    piece = rows // pieces
     heads_q = (out_ref.shape[1] - 128) // HEAD_DIM
     heads_kv = k_ref.shape[1] // HEAD_DIM
     group = heads_q // heads_kv
     tiles = k_ref.shape[0] // SUB
-    ones = jnp.ones((SUB, 128), jnp.bfloat16)
     scale = HEAD_DIM ** (-0.5)
-    col = lax.broadcasted_iota(jnp.int32, (group * rows, SUB), 1)
+    col = lax.broadcasted_iota(jnp.int32, (rows, SUB), 1)
     lane = lax.broadcasted_iota(jnp.int32, (rows, 128), 1)
     extra = jnp.zeros((rows, 128), jnp.float32)
-    for g in range(heads_kv):
-        qg = jnp.concatenate(
-            [q_ref[:, (g * group + r) * HEAD_DIM:(g * group + r + 1) * HEAD_DIM] for r in range(group)],
-            axis=0,
-        )
+    for h in range(heads_q):
+        g = h // group
+        cols = slice(h * HEAD_DIM, (h + 1) * HEAD_DIM)
+        if pieces > 1:
+            qh = jnp.concatenate(
+                [
+                    q_ref[pl.ds(pl.multiple_of(scalar_ref[1 + p] * piece, piece), piece), cols]
+                    for p in range(pieces)
+                ],
+                axis=0,
+            )
+        else:
+            qh = q_ref[:, cols]
         maxes, numers, denoms = [], [], []
         for b in range(tiles):
             kb = k_ref[b * SUB:(b + 1) * SUB, g * HEAD_DIM:(g + 1) * HEAD_DIM]
             s = lax.dot_general(
-                qg, kb, (((1,), (1,)), ((), ())), preferred_element_type=jnp.float32
+                qh, kb, (((1,), (1,)), ((), ())), preferred_element_type=jnp.float32
             ) * scale
             ok = (col + b * SUB) < live
             tm = jnp.max(jnp.where(ok, s, NEG_FILL), axis=1, keepdims=True)
             w = jnp.exp(jnp.where(ok, s - tm, NEG_FILL)).astype(jnp.bfloat16)
             vb = v_ref[b * SUB:(b + 1) * SUB, g * HEAD_DIM:(g + 1) * HEAD_DIM]
             numers.append(jnp.dot(w, vb, preferred_element_type=jnp.float32))
-            denoms.append(jnp.dot(w, ones, preferred_element_type=jnp.float32)[:, :1])
+            denoms.append(jnp.sum(w.astype(jnp.float32), axis=1, keepdims=True))
             maxes.append(tm)
         m = maxes[0]
         for tm in maxes[1:]:
             m = jnp.maximum(m, tm)
-        numer = jnp.zeros((group * rows, HEAD_DIM), jnp.float32)
-        denom = jnp.zeros((group * rows, 1), jnp.float32)
+        numer = jnp.zeros((rows, HEAD_DIM), jnp.float32)
+        denom = jnp.zeros((rows, 1), jnp.float32)
         for tm, nb, db in zip(maxes, numers, denoms):
             f = jnp.exp(tm - m)
             numer = numer + nb * f
@@ -55,13 +63,9 @@
         f = jnp.exp(m - top)
         numer = numer * f
         denom = denom * f
-        mean = numer / jnp.where(denom > 0, denom, 1.0)
-        for r in range(group):
-            h = g * group + r
-            rs = slice(r * rows, (r + 1) * rows)
-            out_ref[:, h * HEAD_DIM:(h + 1) * HEAD_DIM] = mean[rs]
-            extra = jnp.where((lane == h) | (lane == heads_q + h), denom[rs], extra)
-            extra = jnp.where(lane == 2 * heads_q + h, top[rs], extra)
+        out_ref[:, cols] = numer / jnp.where(denom > 0, denom, 1.0)
+        extra = jnp.where((lane == h) | (lane == heads_q + h), denom, extra)
+        extra = jnp.where(lane == 2 * heads_q + h, top, extra)
     out_ref[:, heads_q * HEAD_DIM:] = extra
 
 
@@ -76,20 +80,22 @@
     )
 
 
-def cache_partials(scalars, gathered, keys, values, block, first_slot, count, qcols):
-    gcols = gathered.shape[1]
-    rows = block * count
+def cache_partials(scalars, gathered, keys, values, block, pieces, qcols):
+    rows, gcols = gathered.shape
     cache_rows, kcols = keys.shape
     out_cols = qcols + 128
     heads_q = qcols // HEAD_DIM
-    flops = 4 * rows * cache_rows * qcols + 2 * rows * cache_rows * 128 * (qcols // HEAD_DIM)
+    if pieces > 1:
+        q_spec = pl.BlockSpec((rows, gcols), lambda i, s: (0, 0))
+    else:
+        q_spec = pl.BlockSpec((block, gcols), lambda i, s: (i, 0))
     return pl.pallas_call(
-        cache_kernel,
+        functools.partial(cache_kernel, pieces),
         grid_spec=pltpu.PrefetchScalarGridSpec(
             num_scalar_prefetch=1,
-            grid=(count,),
+            grid=(rows // block,),
             in_specs=[
-                pl.BlockSpec((block, gcols), lambda i, s: (s[first_slot + i], 0)),
+                q_spec,
                 pl.BlockSpec((cache_rows, kcols), lambda i, s: (0, 0)),
                 pl.BlockSpec((cache_rows, kcols), lambda i, s: (0, 0)),
             ],
@@ -97,7 +103,7 @@
         ),
         out_shape=jax.ShapeDtypeStruct((rows, out_cols), jnp.float32),
         cost_estimate=pl.CostEstimate(
-            flops=flops,
+            flops=4 * rows * cache_rows * qcols,
             transcendentals=rows * cache_rows * heads_q,
             bytes_accessed=2 * (rows * gcols + 2 * cache_rows * kcols) + 4 * rows * out_cols,
         ),
@@ -129,31 +135,25 @@
     live_rows = live_rows.astype(jnp.int32)
 
     if seq_count <= 8:
-        shifts = list(range(1, seq_count))
         scalars = jnp.stack(
             [live_rows]
-            + [lax.rem(seq_rank + s, seq_count).astype(jnp.int32) for s in shifts]
-            + [seq_rank.astype(jnp.int32)]
-        )
-        remote = cache_partials(
-            scalars, gathered, cache_keys, cache_values, own_count, 1, seq_count - 1, qcols
-        )
-        parts = []
-        for k, shift in enumerate(shifts):
-            part = to_half(remote[k * own_count:(k + 1) * own_count], qcols, heads_q)
+            + [lax.rem(seq_rank + s, seq_count).astype(jnp.int32) for s in range(seq_count)]
+        )
+        partial = cache_partials(
+            scalars, gathered, cache_keys, cache_values, join_rows, seq_count, qcols
+        )
+        parts = [to_half(partial[:own_count], qcols, heads_q)]
+        for shift in range(1, seq_count):
+            part = to_half(partial[shift * own_count:(shift + 1) * own_count], qcols, heads_q)
             parts.append(
                 lax.ppermute(
                     part, "seq", [(i, (i + shift) % seq_count) for i in range(seq_count)]
                 )
             )
-        own = cache_partials(
-            scalars, gathered, cache_keys, cache_values, own_count, seq_count, 1, qcols
-        )
-        parts.append(to_half(own, qcols, heads_q))
     else:
-        scalars = jnp.stack([live_rows] + [jnp.int32(j) for j in range(join_rows // 256)])
+        scalars = jnp.stack([live_rows, jnp.zeros((), jnp.int32)])
         partial = cache_partials(
-            scalars, gathered, cache_keys, cache_values, 256, 1, join_rows // 256, qcols
+            scalars, gathered, cache_keys, cache_values, min(join_rows, 256), 1, qcols
         )
         recv = lax.all_to_all(to_half(partial, qcols, heads_q), "seq", 0, 0, tiled=True)
         parts = [recv[j * own_count:(j + 1) * own_count] for j in range(seq_count)]

time: 56.5 us -> 48.3 us (0.85)
  Pallas kernels: 15.5 us -> 8.47 us
  local copies, waits for them, and re-layouts: 5.01 us -> 3.09 us
  starting transfers between devices: 3.02 us -> 4 us
    pallas_call x2 -> x1, Pallas kernels: 15.5 us -> 8.47 us  [cache_partials(): pl.pallas_call(functools.partial(cache_kernel, pieces), grid_spec=pltpu.P...]
    unnamed x8 -> x4, local copies, waits for them, and re-layouts: 1.92 us -> 0.01 us
    ppermute x3, starting transfers between devices: 3.02 us -> 4 us  [on_device(): lax.ppermute(part, 'seq', [(i, (i + shift) % seq_count) for i in range(se...]
    another operation x2 -> x1, other arithmetic: 1.23 us -> 1.33 us
  transfers between devices with their start and end apart: 3 -> 3, of which waited for: 1 -> 2; matrix products, arithmetic and copies ran while one was open for 5% -> 6% of each run, Pallas kernels for 0% -> 0%
where the time goes in v6:
time: 48.3 us; the launch traced here: 48 us
  blocking collectives  21.7 us (45%)
  Pallas kernels  8.47 us (18%)
  other arithmetic  4.85 us (10%)
  waiting for transfers between devices  4.42 us (9%)
  starting transfers between devices  4 us (8%)
  local copies, waits for them, and re-layouts  3.09 us (6%)
  between operations  0.85 us (2%)
  matrix products  0.61 us (1%)
    all_gather x1, blocking collectives, on_device(): gathered = lax.all_gather(packed, 'seq', axis=0, tiled=True)  21.7 us
    pallas_call x1, Pallas kernels, cache_partials(): pl.pallas_call(functools.partial(cache_kernel, pieces), grid_spec=pltpu.P...  8.47 us
    ppermute x3, waiting for transfers between devices, on_device(): lax.ppermute(part, 'seq', [(i, (i + shift) % seq_count) for i in range(se...  4.42 us
    ppermute x3, starting transfers between devices, on_device(): lax.ppermute(part, 'seq', [(i, (i + shift) % seq_count) for i in range(se...  4 us
    another operation x1, other arithmetic  1.33 us
    slice x1, local copies, waits for them, and re-layouts, on_device(): all_values = gathered[:, qcols + kcols:]  0.99 us
  transfers between devices with their start and end apart: 3, of which 2 were waited for; matrix products, arithmetic and copies ran while one was open for 6% of the time, Pallas kernels for 0%

profile of v6, /device:TPU:0, one launch (start us, length us, event | category | flops | bytes accessed | tf_op | source)
XLA Modules:
  0.0 48.0 jit_solution(8837654423067858851)
XLA Ops:
  0.7 1.0 %pad_maximum_fusion = bf16[64,1536]{1,0:T(8,128)(2,1)S(1)} fusion(bf16[64,256]{1,0:T(8,128)(2,1)} %param.9, bf16[64,256]{1,0:T(8,128)(2,1)} %param.8, bf16[64,1024]{1,0:T(8,128)(2,1)} %param.7), kind=kLoop, calls=%fused_computation.17 | loop fusion | flops 589824 | bytes 393216 | tf_op jit(solution)/shard_map/concatenate | solution.py:129
  1.6 21.7 %all_gather.3.q_ref = bf16[256,1536]{1,0:T(8,128)(2,1)} all-gather(bf16[64,1536]{1,0:T(8,128)(2,1)S(1)} %pad_maximum_fusion), channel_id=1, replica_groups=mesh['group'=2,'head'=4,'seq'=4] {'seq'}, dimensions={0}, use_global_device_ids=true | all-gather | bytes 983040 | tf_op jit(solution)/shard_map/all_gather | solution.py:130
  23.3 0.6 %stack.23.scalar_ref = s32[5]{0:T(128)} concatenate(s32[1]{0:T(128)} %bitcast.6, s32[1]{0:T(128)} %bitcast.7, s32[1]{0:T(128)} %bitcast.8, s32[1]{0:T(128)} %bitcast.9, s32[1]{0:T(128)} %bitcast.10), dimensions={0} | concatenate | bytes 40 | tf_op jit(solution)/shard_map/stack | solution.py:138
  23.9 8.5 %shard_map.73 = f32[256,1152]{1,0:T(8,128)} custom-call(s32[5]{0:T(128)} %stack.23.scalar_ref, bf16[256,1536]{1,0:T(8,128)(2,1)} %all_gather.3.q_ref, bf16[1024,256]{1,0:T(8,128)(2,1)} %k_ref.1, bf16[1024,256]{1,0:T(8,128)(2,1)} %v_ref.1), custom_call_target="tpu_custom_call" | custom-call | flops 1073741824 | bytes 3014656 | tf_op jit(solution)/shard_map/pallas_call | solution.py:92
  32.4 1.3 %convert.6 = f16[256,1152]{1,0:T(8,128)(2,1)S(1)} convert(f32[256,1152]{1,0:T(8,128)} %shard_map.73) | non-fusion elementwise | flops 294912 | bytes 1769472 | tf_op jit(solution)/shard_map/convert.3
  33.7 0.0 copy-start
  33.7 0.9 %fusion.18 = (f16[64,128]{1,0:T(8,128)(2,1)S(1)}, f16[64,128]{1,0:T(8,128)(2,1)S(1)}, f16[64,128]{1,0:T(8,128)(2,1)S(1)}, f16[64,128]{1,0:T(8,128)(2,1)S(1)}) fusion(f32[256,1152]{1,0:T(8,128)} %shard_map.73, pred[128]{0:T(512)(128)(4,1)S(1)} %compare_and_fusion), kind=kLoop, calls=%fused_computation.51 | loop fusion | flops 163840 | bytes 196736 | tf_op jit(solution)/shard_map/jit(_where)/select_n | solution.py:79
  34.6 0.1 fusion.28
  34.7 0.0 copy-start.1
  34.8 0.1 collective-permute-start
  34.9 2.6 %collective-permute-start.1 = (f16[64,1152]{1,0:T(8,128)(2,1)S(1)}, f16[64,1152]{1,0:T(8,128)(2,1)S(1)}, u32[]{:S(2)}, u32[]{:S(2)}) collective-permute-start(f16[64,1152]{1,0:T(8,128)(2,1)S(1)} %pad_maximum_fusion.2), channel_id=1, source_target_pairs={{0,2},{1,3},{2,0},{3,1},{4,6},{5,7},{6,4},{7,5},{8,10},{9,11},{10,... | collective-permute-start | bytes 442376 | tf_op jit(solution)/shard_map/ppermute | solution.py:149
  37.6 1.3 %collective-permute-start.2 = (f16[64,1152]{1,0:T(8,128)(2,1)S(1)}, f16[64,1152]{1,0:T(8,128)(2,1)S(1)}, u32[]{:S(2)}, u32[]{:S(2)}) collective-permute-start(f16[64,1152]{1,0:T(8,128)(2,1)S(1)} %pad_maximum_fusion.3), channel_id=1, source_target_pairs={{0,3},{1,0},{2,1},{3,2},{4,7},{5,4},{6,5},{7,6},{8,11},{9,8},{10,9... | collective-permute-start | bytes 442376 | tf_op jit(solution)/shard_map/ppermute | solution.py:149
  38.9 0.0 copy-done
  38.9 0.1 reshape.84
  38.9 1.0 %fusion.27 = (bf16[256,256]{1,0:T(8,128)(2,1)S(1)}, bf16[256,256]{1,0:T(8,128)(2,1)S(1)}) fusion(bf16[256,1536]{1,0:T(8,128)(2,1)} %all_gather.3.q_ref), kind=kLoop, calls=%fused_computation.59 | loop fusion | bytes 524288 | tf_op jit(solution)/shard_map/slice | solution.py:132
  40.0 0.0 copy-done.1
  40.0 0.1 dynamic_slice.3
  40.1 0.1 fusion.9
  40.2 0.3 select_reduce_fusion
  40.5 0.3 convert_reduce_fusion
  40.8 0.3 convolution_bitcast_fusion
  41.1 0.2 copy.23
  41.3 0.1 reshape.85
  41.4 0.1 copy.26
  41.5 0.1 copy.25
  41.6 1.3 %collective-permute-done = f16[64,1152]{1,0:T(8,128)(2,1)S(1)} collective-permute-done((f16[64,1152]{1,0:T(8,128)(2,1)S(1)}, f16[64,1152]{1,0:T(8,128)(2,1)S(1)}, u32[]{:S(2)}, u32[]{:S(2)}) %collective-permute-start) | collective-permute-done | bytes 147488 | tf_op jit(solution)/shard_map/ppermute | solution.py:149
  42.9 3.1 %collective-permute-done.1 = f16[64,1152]{1,0:T(8,128)(2,1)S(1)} collective-permute-done((f16[64,1152]{1,0:T(8,128)(2,1)S(1)}, f16[64,1152]{1,0:T(8,128)(2,1)S(1)}, u32[]{:S(2)}, u32[]{:S(2)}) %collective-permute-start.1) | collective-permute-done | bytes 147488 | tf_op jit(solution)/shard_map/ppermute | solution.py:149
  46.1 0.0 collective-permute-done.2
  46.1 0.1 add_add_fusion
  46.3 0.1 div.11
  46.4 0.1 mul.90
  46.5 0.1 mul.94
  46.7 0.1 mul.98
  46.8 0.1 mul.102
  46.9 0.1 mul.106
  47.1 1.0 %fusion.1 = bf16[64,1024]{1,0:T(8,128)(2,1)} fusion(f32[8,8,8,128]{3,2,1,0:T(8,128)S(1)} %bitcast.53, f32[8,8,8,128]{3,2,1,0:T(8,128)S(1)} %bitcast.58, f32[8,8,8,128]{3,2,1,0:T(8,128)S(1)} %bitcast.57, f32[8,8,8,128]{3,2,1,0:T(8,128)S(1)} %bitcast.56, f32[8,8,8,128]{3,2,1,0:T(8,128)S(1)} %bitcast.55, f32[64,1024]{1,0:T(8,128)S(1)} %reshape.85, ...), kind=kLoop, calls=%fused_computation.7 | loop fusion | flops 720896 | bytes 3014656 | tf_op jit(solution)/shard_map/convert_element_type | solution.py:209
  (11 shorter events, 0.3 us)
Async XLA Ops:
  33.7 5.1 %copy-start = (bf16[64,1024]{1,0:T(8,128)(2,1)S(1)}, bf16[64,1024]{1,0:T(8,128)(2,1)}, u32[]{:S(2)}) copy-start(bf16[64,1024]{1,0:T(8,128)(2,1)} %param.7) | copy-start | bytes 393220
  34.7 5.3 %copy-start.1 = (s32[256]{0:T(256)S(1)}, s32[256]{0:T(256)}, u32[]{:S(2)}) copy-start(s32[256]{0:T(256)} %param.12) | copy-start | bytes 3076
  34.8 8.2 %collective-permute-start = (f16[64,1152]{1,0:T(8,128)(2,1)S(1)}, f16[64,1152]{1,0:T(8,128)(2,1)S(1)}, u32[]{:S(2)}, u32[]{:S(2)}) collective-permute-start(f16[64,1152]{1,0:T(8,128)(2,1)S(1)} %pad_maximum_fusion.1), channel_id=1, source_target_pairs={{0,1},{1,2},{2,3},{3,0},{4,5},{5,6},{6,7},{7,4},{8,9},{9,10},{10,1... | collective-permute-start | bytes 442376 | tf_op jit(solution)/shard_map/ppermute | solution.py:149
  34.9 11.2 %collective-permute-start.1 = (f16[64,1152]{1,0:T(8,128)(2,1)S(1)}, f16[64,1152]{1,0:T(8,128)(2,1)S(1)}, u32[]{:S(2)}, u32[]{:S(2)}) collective-permute-start(f16[64,1152]{1,0:T(8,128)(2,1)S(1)} %pad_maximum_fusion.2), channel_id=1, source_target_pairs={{0,2},{1,3},{2,0},{3,1},{4,6},{5,7},{6,4},{7,5},{8,10},{9,11},{10,... | collective-permute-start | bytes 442376 | tf_op jit(solution)/shard_map/ppermute | solution.py:149
  37.6 8.5 %collective-permute-start.2 = (f16[64,1152]{1,0:T(8,128)(2,1)S(1)}, f16[64,1152]{1,0:T(8,128)(2,1)S(1)}, u32[]{:S(2)}, u32[]{:S(2)}) collective-permute-start(f16[64,1152]{1,0:T(8,128)(2,1)S(1)} %pad_maximum_fusion.3), channel_id=1, source_target_pairs={{0,3},{1,0},{2,1},{3,2},{4,7},{5,4},{6,5},{7,6},{8,11},{9,8},{10,9... | collective-permute-start | bytes 442376 | tf_op jit(solution)/shard_map/ppermute | solution.py:149

commit v7 on v5

--- a/solution.py
+++ b/solution.py
@@ -12,41 +12,58 @@
 NEG_FILL = -1e30
 
 
-def cache_kernel(scalar_ref, q_ref, k_ref, v_ref, out_ref):
-    live = scalar_ref[0]
-    rows = q_ref.shape[0]
+def cache_kernel(seq_count, first, pieces, stack, len_ref, q_ref, k_ref, v_ref, *rest):
+    out_ref = rest[-1]
+    rank = lax.axis_index("seq")
+    cache_rows = k_ref.shape[0]
+    live = jnp.clip(len_ref[0] - rank * cache_rows, 0, cache_rows)
+    rows = out_ref.shape[0]
     heads_q = (out_ref.shape[1] - 128) // HEAD_DIM
     heads_kv = k_ref.shape[1] // HEAD_DIM
     group = heads_q // heads_kv
-    tiles = k_ref.shape[0] // SUB
-    ones = jnp.ones((SUB, 128), jnp.bfloat16)
+    tiles = cache_rows // SUB
     scale = HEAD_DIM ** (-0.5)
-    col = lax.broadcasted_iota(jnp.int32, (group * rows, SUB), 1)
     lane = lax.broadcasted_iota(jnp.int32, (rows, 128), 1)
     extra = jnp.zeros((rows, 128), jnp.float32)
-    for g in range(heads_kv):
-        qg = jnp.concatenate(
-            [q_ref[:, (g * group + r) * HEAD_DIM:(g * group + r + 1) * HEAD_DIM] for r in range(group)],
-            axis=0,
-        )
+
+    def query_rows(h):
+        cols = slice(h * HEAD_DIM, (h + 1) * HEAD_DIM)
+        if pieces == 0:
+            return q_ref[:, cols]
+        piece = rows // pieces
+        blocks = []
+        for p in range(pieces):
+            index = lax.rem(rank + first + p, seq_count)
+            blocks.append(q_ref[pl.ds(pl.multiple_of(index * piece, piece), piece), cols])
+        return jnp.concatenate(blocks, axis=0)
+
+    if stack > 1:
+        units = [list(range(g * group, (g + 1) * group)) for g in range(heads_kv)]
+    else:
+        units = [[h] for h in range(heads_q)]
+    for heads in units:
+        g = heads[0] // group
+        qx = jnp.concatenate([query_rows(h) for h in heads], axis=0)
+        span = qx.shape[0]
+        col = lax.broadcasted_iota(jnp.int32, (span, SUB), 1)
         maxes, numers, denoms = [], [], []
         for b in range(tiles):
             kb = k_ref[b * SUB:(b + 1) * SUB, g * HEAD_DIM:(g + 1) * HEAD_DIM]
             s = lax.dot_general(
-                qg, kb, (((1,), (1,)), ((), ())), preferred_element_type=jnp.float32
+                qx, kb, (((1,), (1,)), ((), ())), preferred_element_type=jnp.float32
             ) * scale
             ok = (col + b * SUB) < live
             tm = jnp.max(jnp.where(ok, s, NEG_FILL), axis=1, keepdims=True)
             w = jnp.exp(jnp.where(ok, s - tm, NEG_FILL)).astype(jnp.bfloat16)
             vb = v_ref[b * SUB:(b + 1) * SUB, g * HEAD_DIM:(g + 1) * HEAD_DIM]
             numers.append(jnp.dot(w, vb, preferred_element_type=jnp.float32))
-            denoms.append(jnp.dot(w, ones, preferred_element_type=jnp.float32)[:, :1])
+            denoms.append(jnp.sum(w.astype(jnp.float32), axis=1, keepdims=True))
             maxes.append(tm)
         m = maxes[0]
         for tm in maxes[1:]:
             m = jnp.maximum(m, tm)
-        numer = jnp.zeros((group * rows, HEAD_DIM), jnp.float32)
-        denom = jnp.zeros((group * rows, 1), jnp.float32)
+        numer = jnp.zeros((span, HEAD_DIM), jnp.float32)
+        denom = jnp.zeros((span, 1), jnp.float32)
         for tm, nb, db in zip(maxes, numers, denoms):
             f = jnp.exp(tm - m)
             numer = numer + nb * f
@@ -56,9 +73,8 @@
         numer = numer * f
         denom = denom * f
         mean = numer / jnp.where(denom > 0, denom, 1.0)
-        for r in range(group):
-            h = g * group + r
-            rs = slice(r * rows, (r + 1) * rows)
+        for i, h in enumerate(heads):
+            rs = slice(i * rows, (i + 1) * rows)
             out_ref[:, h * HEAD_DIM:(h + 1) * HEAD_DIM] = mean[rs]
             extra = jnp.where((lane == h) | (lane == heads_q + h), denom[rs], extra)
             extra = jnp.where(lane == 2 * heads_q + h, top[rs], extra)
@@ -76,32 +92,38 @@
     )
 
 
-def cache_partials(scalars, gathered, keys, values, block, first_slot, count, qcols):
-    gcols = gathered.shape[1]
-    rows = block * count
+def cache_partials(cache_length, queries, keys, values, qcols, rows, block, first, pieces,
+                   stack, seq_count, after=None):
+    qrows, qcols_in = queries.shape
     cache_rows, kcols = keys.shape
     out_cols = qcols + 128
     heads_q = qcols // HEAD_DIM
-    flops = 4 * rows * cache_rows * qcols + 2 * rows * cache_rows * 128 * (qcols // HEAD_DIM)
+    if pieces > 0 or block == qrows:
+        q_spec = pl.BlockSpec((qrows, qcols_in), lambda i: (0, 0))
+    else:
+        q_spec = pl.BlockSpec((block, qcols_in), lambda i: (i, 0))
+    in_specs = [
+        pl.BlockSpec(memory_space=pltpu.SMEM),
+        q_spec,
+        pl.BlockSpec((cache_rows, kcols), lambda i: (0, 0)),
+        pl.BlockSpec((cache_rows, kcols), lambda i: (0, 0)),
+    ]
+    operands = [cache_length, queries, keys, values]
+    if after is not None:
+        in_specs.append(pl.BlockSpec(memory_space=pl.ANY))
+        operands.append(after)
     return pl.pallas_call(
-        cache_kernel,
-        grid_spec=pltpu.PrefetchScalarGridSpec(
-            num_scalar_prefetch=1,
-            grid=(count,),
-            in_specs=[
-                pl.BlockSpec((block, gcols), lambda i, s: (s[first_slot + i], 0)),
-                pl.BlockSpec((cache_rows, kcols), lambda i, s: (0, 0)),
-                pl.BlockSpec((cache_rows, kcols), lambda i, s: (0, 0)),
-            ],
-            out_specs=pl.BlockSpec((block, out_cols), lambda i, s: (i, 0)),
-        ),
+        functools.partial(cache_kernel, seq_count, first, pieces, stack),
+        grid=(rows // block,),
+        in_specs=in_specs,
+        out_specs=pl.BlockSpec((block, out_cols), lambda i: (i, 0)),
         out_shape=jax.ShapeDtypeStruct((rows, out_cols), jnp.float32),
         cost_estimate=pl.CostEstimate(
-            flops=flops,
+            flops=4 * rows * cache_rows * qcols,
             transcendentals=rows * cache_rows * heads_q,
-            bytes_accessed=2 * (rows * gcols + 2 * cache_rows * kcols) + 4 * rows * out_cols,
+            bytes_accessed=2 * (rows * qcols_in + 2 * cache_rows * kcols) + 4 * rows * out_cols,
         ),
-    )(scalars, gathered, keys, values)
+    )(*operands)
 
 
 def on_device(
@@ -125,42 +147,42 @@
     all_keys = gathered[:, qcols:qcols + kcols]
     all_values = gathered[:, qcols + kcols:]
 
-    live_rows = jnp.clip(cache_length[0] - seq_rank * cache_rows, 0, cache_rows)
-    live_rows = live_rows.astype(jnp.int32)
-
     if seq_count <= 8:
-        shifts = list(range(1, seq_count))
-        scalars = jnp.stack(
-            [live_rows]
-            + [lax.rem(seq_rank + s, seq_count).astype(jnp.int32) for s in shifts]
-            + [seq_rank.astype(jnp.int32)]
-        )
         remote = cache_partials(
-            scalars, gathered, cache_keys, cache_values, own_count, 1, seq_count - 1, qcols
+            cache_length, gathered, cache_keys, cache_values, qcols,
+            (seq_count - 1) * own_count, (seq_count - 1) * own_count, 1, seq_count - 1, 1,
+            seq_count,
         )
         parts = []
-        for k, shift in enumerate(shifts):
-            part = to_half(remote[k * own_count:(k + 1) * own_count], qcols, heads_q)
+        for shift in range(1, seq_count):
+            piece = remote[(shift - 1) * own_count:shift * own_count]
             parts.append(
                 lax.ppermute(
-                    part, "seq", [(i, (i + shift) % seq_count) for i in range(seq_count)]
-                )
+                    to_half(piece, qcols, heads_q),
+                    "seq",
+                    [(i, (i + shift) % seq_count) for i in range(seq_count)],
+                ).astype(jnp.float32)
             )
         own = cache_partials(
-            scalars, gathered, cache_keys, cache_values, own_count, seq_count, 1, qcols
-        )
-        parts.append(to_half(own, qcols, heads_q))
+            cache_length, new_queries, cache_keys, cache_values, qcols,
+            own_count, own_count, 0, 0, group_size, seq_count, after=remote,
+        )
+        split_denom = [True] * (seq_count - 1) + [False]
+        parts.append(own)
     else:
-        scalars = jnp.stack([live_rows] + [jnp.int32(j) for j in range(join_rows // 256)])
         partial = cache_partials(
-            scalars, gathered, cache_keys, cache_values, 256, 1, join_rows // 256, qcols
+            cache_length, gathered, cache_keys, cache_values, qcols,
+            join_rows, min(join_rows, 256), 0, 0, 1, seq_count,
         )
         recv = lax.all_to_all(to_half(partial, qcols, heads_q), "seq", 0, 0, tiled=True)
+        recv = recv.astype(jnp.float32)
         parts = [recv[j * own_count:(j + 1) * own_count] for j in range(seq_count)]
-    parts = [p.astype(jnp.float32) for p in parts]
+        split_denom = [True] * seq_count
     part_mean = [p[:, :qcols].reshape(own_count, heads_q, head_size) for p in parts]
     part_denom = [
-        p[:, qcols:qcols + heads_q] + p[:, qcols + heads_q:qcols + 2 * heads_q] for p in parts
+        p[:, qcols:qcols + heads_q] + p[:, qcols + heads_q:qcols + 2 * heads_q]
+        if two else p[:, qcols:qcols + heads_q]
+        for p, two in zip(parts, split_denom)
     ]
     part_max = [p[:, qcols + 2 * heads_q:qcols + 3 * heads_q] for p in parts]
 

time: 56.5 us -> 46.8 us (0.83)
  Pallas kernels: 15.5 us -> 10.1 us
  waiting for transfers between devices: 4.61 us -> 1.1 us
  local copies, waits for them, and re-layouts: 5.01 us -> 4.36 us
    pallas_call x2, Pallas kernels: 15.5 us -> 10.1 us  [cache_partials(): pl.pallas_call(functools.partial(cache_kernel, seq_count, first, pieces,...]
    ppermute x3, waiting for transfers between devices: 4.61 us -> 1.1 us  [on_device(): lax.ppermute(to_half(piece, qcols, heads_q), 'seq', [(i, (i + shift) % se...]
    another operation x1 -> x0, local copies, waits for them, and re-layouts: 0.6 us -> none  [on_device(): jnp.stack([live_rows] + [lax.rem(seq_rank + s, seq_count).astype(jnp.int3...]
    unnamed x8 -> x6, local copies, waits for them, and re-layouts: 1.92 us -> 1.87 us
    another operation x2 -> x1, other arithmetic: 1.23 us -> 1.22 us
  transfers between devices with their start and end apart: 3 -> 3, of which waited for: 1 -> 1; matrix products, arithmetic and copies ran while one was open for 5% -> 6% of each run, Pallas kernels for 0% -> 8%
where the time goes in v7:
time: 46.8 us; the launch traced here: 46.4 us
  blocking collectives  21.7 us (46%)
  Pallas kernels  10.1 us (22%)
  other arithmetic  4.64 us (10%)
  local copies, waits for them, and re-layouts  4.36 us (9%)
  starting transfers between devices  3.02 us (6%)
  waiting for transfers between devices  1.1 us (2%)
  between operations  0.85 us (2%)
  matrix products  0.61 us (1%)
    all_gather x1, blocking collectives, on_device(): gathered = lax.all_gather(packed, 'seq', axis=0, tiled=True)  21.7 us
    pallas_call x2, Pallas kernels, cache_partials(): pl.pallas_call(functools.partial(cache_kernel, seq_count, first, pieces,...  10.1 us
    ppermute x3, starting transfers between devices, on_device(): lax.ppermute(to_half(piece, qcols, heads_q), 'seq', [(i, (i + shift) % se...  3.02 us
    unnamed x6, local copies, waits for them, and re-layouts  1.87 us
    another operation x1, other arithmetic  1.22 us
    ppermute x3, waiting for transfers between devices, on_device(): lax.ppermute(to_half(piece, qcols, heads_q), 'seq', [(i, (i + shift) % se...  1.1 us
    slice x1, local copies, waits for them, and re-layouts, on_device(): all_values = gathered[:, qcols + kcols:]  0.99 us
    convert_element_type x1, other arithmetic, on_device(): return attended.reshape(own_count, qcols).astype(jnp.bfloat16)  0.96 us
  transfers between devices with their start and end apart: 3, of which 1 were waited for; matrix products, arithmetic and copies ran while one was open for 6% of the time, Pallas kernels for 8%

profile of v7, /device:TPU:0, one launch (start us, length us, event | category | flops | bytes accessed | tf_op | source)
XLA Modules:
  0.0 46.4 jit_solution(4478380559068942476)
XLA Ops:
  0.7 1.0 %pad_maximum_fusion = bf16[64,1536]{1,0:T(8,128)(2,1)S(1)} fusion(bf16[64,256]{1,0:T(8,128)(2,1)} %param.9, bf16[64,256]{1,0:T(8,128)(2,1)} %param.8, bf16[64,1024]{1,0:T(8,128)(2,1)} %q_ref.1), kind=kLoop, calls=%fused_computation.17 | loop fusion | flops 589824 | bytes 393216 | tf_op jit(solution)/shard_map/concatenate | solution.py:145
  1.6 21.7 %all_gather.3.q_ref = bf16[256,1536]{1,0:T(8,128)(2,1)} all-gather(bf16[64,1536]{1,0:T(8,128)(2,1)S(1)} %pad_maximum_fusion), channel_id=1, replica_groups=mesh['group'=2,'head'=4,'seq'=4] {'seq'}, dimensions={0}, use_global_device_ids=true | all-gather | bytes 983040 | tf_op jit(solution)/shard_map/all_gather | solution.py:146
  23.3 6.6 %shard_map.73.rest_0_ = f32[192,1152]{1,0:T(8,128)} custom-call(s32[1]{0:T(128)S(6)} %copy.55.len_ref, bf16[256,1536]{1,0:T(8,128)(2,1)} %all_gather.3.q_ref, bf16[1024,256]{1,0:T(8,128)(2,1)} %k_ref.3, bf16[1024,256]{1,0:T(8,128)(2,1)} %v_ref.3), custom_call_target="tpu_custom_call" | custom-call | flops 805306368 | bytes 2523136 | tf_op jit(solution)/shard_map/pallas_call | solution.py:115
  29.9 1.2 %convert.5 = f16[192,1152]{1,0:T(8,128)(2,1)S(1)} convert(f32[192,1152]{1,0:T(8,128)} %shard_map.73.rest_0_) | non-fusion elementwise | flops 221184 | bytes 1327104 | tf_op jit(solution)/shard_map/convert.2
  31.1 0.8 %fusion.13 = (f16[64,128]{1,0:T(8,128)(2,1)S(1)}, f16[64,128]{1,0:T(8,128)(2,1)S(1)}, f16[64,128]{1,0:T(8,128)(2,1)S(1)}) fusion(f32[192,1152]{1,0:T(8,128)} %shard_map.73.rest_0_, pred[128]{0:T(512)(128)(4,1)S(1)} %compare_and_fusion), kind=kLoop, calls=%fused_computation.42 | loop fusion | flops 122880 | bytes 147584 | tf_op jit(solution)/shard_map/jit(_where)/select_n | solution.py:91
  31.9 0.1 fusion.21
  32.1 0.9 %collective-permute-start.1 = (f16[64,1152]{1,0:T(8,128)(2,1)S(1)}, f16[64,1152]{1,0:T(8,128)(2,1)S(1)}, u32[]{:S(2)}, u32[]{:S(2)}) collective-permute-start(f16[64,1152]{1,0:T(8,128)(2,1)S(1)} %pad_maximum_fusion.2), channel_id=1, source_target_pairs={{0,2},{1,3},{2,0},{3,1},{4,6},{5,7},{6,4},{7,5},{8,10},{9,11},{10,... | collective-permute-start | bytes 442376 | tf_op jit(solution)/shard_map/ppermute | solution.py:160
  33.0 1.6 %collective-permute-start.2 = (f16[64,1152]{1,0:T(8,128)(2,1)S(1)}, f16[64,1152]{1,0:T(8,128)(2,1)S(1)}, u32[]{:S(2)}, u32[]{:S(2)}) collective-permute-start(f16[64,1152]{1,0:T(8,128)(2,1)S(1)} %pad_maximum_fusion.3), channel_id=1, source_target_pairs={{0,3},{1,0},{2,1},{3,2},{4,7},{5,4},{6,5},{7,6},{8,11},{9,8},{10,9... | collective-permute-start | bytes 442376 | tf_op jit(solution)/shard_map/ppermute | solution.py:160
  34.6 0.0 copy-start.1
  34.6 0.6 %collective-permute-start = (f16[64,1152]{1,0:T(8,128)(2,1)S(1)}, f16[64,1152]{1,0:T(8,128)(2,1)S(1)}, u32[]{:S(2)}, u32[]{:S(2)}) collective-permute-start(f16[64,1152]{1,0:T(8,128)(2,1)S(1)} %pad_maximum_fusion.1), channel_id=1, source_target_pairs={{0,1},{1,2},{2,3},{3,0},{4,5},{5,6},{6,7},{7,4},{8,9},{9,10},{10,1... | collective-permute-start | bytes 442376 | tf_op jit(solution)/shard_map/ppermute | solution.py:160
  35.2 0.3 copy-done.1
  35.5 0.1 reshape.84
  35.5 1.0 %fusion.20 = (bf16[256,256]{1,0:T(8,128)(2,1)S(1)}, bf16[256,256]{1,0:T(8,128)(2,1)S(1)}) fusion(bf16[256,1536]{1,0:T(8,128)(2,1)} %all_gather.3.q_ref), kind=kLoop, calls=%fused_computation.48 | loop fusion | bytes 524288 | tf_op jit(solution)/shard_map/slice | solution.py:148
  36.6 0.0 copy-start.2
  36.6 0.7 %copy-done.2 = s32[256]{0:T(256)S(1)} copy-done((s32[256]{0:T(256)S(1)}, s32[256]{0:T(256)}, u32[]{:S(2)}) %copy-start.2) | copy-done | bytes 1048
  37.3 0.1 dynamic_slice.3
  37.4 0.1 fusion.9
  37.5 0.3 select_reduce_fusion
  37.8 0.3 convolution_bitcast_fusion
  38.1 0.2 copy.23
  38.3 0.1 reshape.85
  38.4 0.3 convert_reduce_fusion
  38.7 0.1 copy.26
  38.8 0.1 copy.25
  38.8 3.6 %shard_map.74 = f32[64,1152]{1,0:T(8,128)} custom-call(s32[1]{0:T(128)S(6)} %copy.55.len_ref, bf16[64,1024]{1,0:T(8,128)(2,1)} %q_ref.1, bf16[1024,256]{1,0:T(8,128)(2,1)} %k_ref.3, bf16[1024,256]{1,0:T(8,128)(2,1)} %v_ref.3, f32[192,1152]{1,0:T(8,128)} %shard_map.73.rest_0_), custom_call_target="tpu_custom_call" | custom-call | flops 268435456 | bytes 1474560 | tf_op jit(solution)/shard_map/pallas_call | solution.py:115
  42.4 1.1 %collective-permute-done.1 = f16[64,1152]{1,0:T(8,128)(2,1)S(1)} collective-permute-done((f16[64,1152]{1,0:T(8,128)(2,1)S(1)}, f16[64,1152]{1,0:T(8,128)(2,1)S(1)}, u32[]{:S(2)}, u32[]{:S(2)}) %collective-permute-start.1) | collective-permute-done | bytes 147488 | tf_op jit(solution)/shard_map/ppermute | solution.py:160
  43.5 0.0 collective-permute-done.2
  43.6 0.0 copy-start
  43.6 0.0 collective-permute-done
  43.6 0.9 %copy-done = f32[64,1152]{1,0:T(8,128)S(1)} copy-done((f32[64,1152]{1,0:T(8,128)S(1)}, f32[64,1152]{1,0:T(8,128)}, u32[]{:S(2)}) %copy-start) | copy-done | bytes 294936
  44.5 0.1 add_add_fusion
  44.7 0.1 div.11
  44.8 0.1 mul.86
  44.9 0.1 mul.90
  45.1 0.1 mul.94
  45.2 0.1 mul.98
  45.3 0.1 mul.102
  45.5 1.0 %fusion.1 = bf16[64,1024]{1,0:T(8,128)(2,1)} fusion(f32[8,8,8,128]{3,2,1,0:T(8,128)S(1)} %bitcast.46, f32[8,8,8,128]{3,2,1,0:T(8,128)S(1)} %bitcast.51, f32[8,8,8,128]{3,2,1,0:T(8,128)S(1)} %bitcast.50, f32[8,8,8,128]{3,2,1,0:T(8,128)S(1)} %bitcast.49, f32[8,8,8,128]{3,2,1,0:T(8,128)S(1)} %bitcast.48, f32[64,1024]{1,0:T(8,128)S(1)} %reshape.85, ...), kind=kLoop, calls=%fused_computation.7 | loop fusion | flops 720896 | bytes 3014656 | tf_op jit(solution)/shard_map/convert_element_type | solution.py:231
  (10 shorter events, 0.3 us)
Async XLA Ops:
  32.1 11.4 %collective-permute-start.1 = (f16[64,1152]{1,0:T(8,128)(2,1)S(1)}, f16[64,1152]{1,0:T(8,128)(2,1)S(1)}, u32[]{:S(2)}, u32[]{:S(2)}) collective-permute-start(f16[64,1152]{1,0:T(8,128)(2,1)S(1)} %pad_maximum_fusion.2), channel_id=1, source_target_pairs={{0,2},{1,3},{2,0},{3,1},{4,6},{5,7},{6,4},{7,5},{8,10},{9,11},{10,... | collective-permute-start | bytes 442376 | tf_op jit(solution)/shard_map/ppermute | solution.py:160
  33.0 10.5 %collective-permute-start.2 = (f16[64,1152]{1,0:T(8,128)(2,1)S(1)}, f16[64,1152]{1,0:T(8,128)(2,1)S(1)}, u32[]{:S(2)}, u32[]{:S(2)}) collective-permute-start(f16[64,1152]{1,0:T(8,128)(2,1)S(1)} %pad_maximum_fusion.3), channel_id=1, source_target_pairs={{0,3},{1,0},{2,1},{3,2},{4,7},{5,4},{6,5},{7,6},{8,11},{9,8},{10,9... | collective-permute-start | bytes 442376 | tf_op jit(solution)/shard_map/ppermute | solution.py:160
  34.6 0.9 %copy-start.1 = (bf16[64,1024]{1,0:T(8,128)(2,1)S(1)}, bf16[64,1024]{1,0:T(8,128)(2,1)}, u32[]{:S(2)}) copy-start(bf16[64,1024]{1,0:T(8,128)(2,1)} %q_ref.1) | copy-start | bytes 393220
  34.6 9.0 %collective-permute-start = (f16[64,1152]{1,0:T(8,128)(2,1)S(1)}, f16[64,1152]{1,0:T(8,128)(2,1)S(1)}, u32[]{:S(2)}, u32[]{:S(2)}) collective-permute-start(f16[64,1152]{1,0:T(8,128)(2,1)S(1)} %pad_maximum_fusion.1), channel_id=1, source_target_pairs={{0,1},{1,2},{2,3},{3,0},{4,5},{5,6},{6,7},{7,4},{8,9},{9,10},{10,1... | collective-permute-start | bytes 442376 | tf_op jit(solution)/shard_map/ppermute | solution.py:160
  36.6 0.7 %copy-start.2 = (s32[256]{0:T(256)S(1)}, s32[256]{0:T(256)}, u32[]{:S(2)}) copy-start(s32[256]{0:T(256)} %param.12) | copy-start | bytes 3076
  43.6 1.0 %copy-start = (f32[64,1152]{1,0:T(8,128)S(1)}, f32[64,1152]{1,0:T(8,128)}, u32[]{:S(2)}) copy-start(f32[64,1152]{1,0:T(8,128)} %shard_map.74) | copy-start | bytes 884740

commit v8 on v7

--- a/solution.py
+++ b/solution.py
@@ -24,6 +24,8 @@
     tiles = cache_rows // SUB
     scale = HEAD_DIM ** (-0.5)
     lane = lax.broadcasted_iota(jnp.int32, (rows, 128), 1)
+    position = lax.broadcasted_iota(jnp.int32, (1, cache_rows), 1)
+    ones = jnp.ones((SUB, 128), jnp.bfloat16)
     extra = jnp.zeros((rows, 128), jnp.float32)
 
     def query_rows(h):
@@ -45,19 +47,18 @@
         g = heads[0] // group
         qx = jnp.concatenate([query_rows(h) for h in heads], axis=0)
         span = qx.shape[0]
-        col = lax.broadcasted_iota(jnp.int32, (span, SUB), 1)
         maxes, numers, denoms = [], [], []
         for b in range(tiles):
             kb = k_ref[b * SUB:(b + 1) * SUB, g * HEAD_DIM:(g + 1) * HEAD_DIM]
+            bias = jnp.where(position[:, b * SUB:(b + 1) * SUB] < live, 0.0, NEG_FILL)
             s = lax.dot_general(
                 qx, kb, (((1,), (1,)), ((), ())), preferred_element_type=jnp.float32
-            ) * scale
-            ok = (col + b * SUB) < live
-            tm = jnp.max(jnp.where(ok, s, NEG_FILL), axis=1, keepdims=True)
-            w = jnp.exp(jnp.where(ok, s - tm, NEG_FILL)).astype(jnp.bfloat16)
+            ) * scale + bias
+            tm = jnp.max(s, axis=1, keepdims=True)
+            w = jnp.exp(s - tm).astype(jnp.bfloat16)
             vb = v_ref[b * SUB:(b + 1) * SUB, g * HEAD_DIM:(g + 1) * HEAD_DIM]
             numers.append(jnp.dot(w, vb, preferred_element_type=jnp.float32))
-            denoms.append(jnp.sum(w.astype(jnp.float32), axis=1, keepdims=True))
+            denoms.append(jnp.dot(w, ones, preferred_element_type=jnp.float32)[:, :1])
             maxes.append(tm)
         m = maxes[0]
         for tm in maxes[1:]:
@@ -73,23 +74,19 @@
         numer = numer * f
         denom = denom * f
         mean = numer / jnp.where(denom > 0, denom, 1.0)
+        ulp = jnp.exp2(jnp.floor(jnp.log2(jnp.where(denom > 0, denom, 1.0))) - 10.0)
+        hi = jnp.where(denom > 0, jnp.round(denom / ulp) * ulp, 0.0)
         for i, h in enumerate(heads):
             rs = slice(i * rows, (i + 1) * rows)
             out_ref[:, h * HEAD_DIM:(h + 1) * HEAD_DIM] = mean[rs]
-            extra = jnp.where((lane == h) | (lane == heads_q + h), denom[rs], extra)
+            extra = jnp.where(lane == h, hi[rs], extra)
+            extra = jnp.where(lane == heads_q + h, denom[rs] - hi[rs], extra)
             extra = jnp.where(lane == 2 * heads_q + h, top[rs], extra)
     out_ref[:, heads_q * HEAD_DIM:] = extra
 
 
 def to_half(part, qcols, heads_q):
-    extra = part[:, qcols:]
-    rounded = extra.astype(jnp.float16)
-    rest = (extra - rounded.astype(jnp.float32)).astype(jnp.float16)
-    lane = lax.broadcasted_iota(jnp.int32, extra.shape, 1)
-    second = (lane >= heads_q) & (lane < 2 * heads_q)
-    return jnp.concatenate(
-        [part[:, :qcols].astype(jnp.float16), jnp.where(second, rest, rounded)], axis=1
-    )
+    return part.astype(jnp.float16)
 
 
 def cache_partials(cache_length, queries, keys, values, qcols, rows, block, first, pieces,
@@ -167,7 +164,6 @@
             cache_length, new_queries, cache_keys, cache_values, qcols,
             own_count, own_count, 0, 0, group_size, seq_count, after=remote,
         )
-        split_denom = [True] * (seq_count - 1) + [False]
         parts.append(own)
     else:
         partial = cache_partials(
@@ -177,12 +173,9 @@
         recv = lax.all_to_all(to_half(partial, qcols, heads_q), "seq", 0, 0, tiled=True)
         recv = recv.astype(jnp.float32)
         parts = [recv[j * own_count:(j + 1) * own_count] for j in range(seq_count)]
-        split_denom = [True] * seq_count
     part_mean = [p[:, :qcols].reshape(own_count, heads_q, head_size) for p in parts]
     part_denom = [
-        p[:, qcols:qcols + heads_q] + p[:, qcols + heads_q:qcols + 2 * heads_q]
-        if two else p[:, qcols:qcols + heads_q]
-        for p, two in zip(parts, split_denom)
+        p[:, qcols:qcols + heads_q] + p[:, qcols + heads_q:qcols + 2 * heads_q] for p in parts
     ]
     part_max = [p[:, qcols + 2 * heads_q:qcols + 3 * heads_q] for p in parts]
 

time: 46.8 us -> 51.6 us (1.10)
  Pallas kernels: 10.1 us -> 15.8 us
  local copies, waits for them, and re-layouts: 4.36 us -> 3.18 us
  other arithmetic: 4.64 us -> 3.71 us
  starting transfers between devices: 3.02 us -> 3.87 us
    pallas_call x2, Pallas kernels: 10.1 us -> 15.8 us  [cache_partials(): pl.pallas_call(functools.partial(cache_kernel, seq_count, first, pieces,...]
    unnamed x6, local copies, waits for them, and re-layouts: 1.87 us -> 0.68 us
    ppermute x3, starting transfers between devices: 3.02 us -> 3.87 us  [on_device(): lax.ppermute(to_half(piece, qcols, heads_q), 'seq', [(i, (i + shift) % se...]
    select_n x1 -> x0, other arithmetic: 0.81 us -> none  [to_half(): jnp.where(second, rest, rounded)]
  transfers between devices with their start and end apart: 3 -> 3, of which waited for: 1 -> 1; matrix products, arithmetic and copies ran while one was open for 6% -> 5% of each run, Pallas kernels for 8% -> 9%
where the time goes in v8:
time: 51.6 us; the launch traced here: 51.4 us
  blocking collectives  21.7 us (42%)
  Pallas kernels  15.8 us (31%)
  starting transfers between devices  3.87 us (8%)
  other arithmetic  3.71 us (7%)
  local copies, waits for them, and re-layouts  3.18 us (6%)
  waiting for transfers between devices  1.61 us (3%)
  between operations  0.84 us (2%)
  matrix products  0.62 us (1%)
    all_gather x1, blocking collectives, on_device(): gathered = lax.all_gather(packed, 'seq', axis=0, tiled=True)  21.7 us
    pallas_call x2, Pallas kernels, cache_partials(): pl.pallas_call(functools.partial(cache_kernel, seq_count, first, pieces,...  15.8 us
    ppermute x3, starting transfers between devices, on_device(): lax.ppermute(to_half(piece, qcols, heads_q), 'seq', [(i, (i + shift) % se...  3.87 us
    ppermute x3, waiting for transfers between devices, on_device(): lax.ppermute(to_half(piece, qcols, heads_q), 'seq', [(i, (i + shift) % se...  1.61 us
    another operation x1, other arithmetic  1.22 us
  transfers between devices with their start and end apart: 3, of which 1 were waited for; matrix products, arithmetic and copies ran while one was open for 5% of the time, Pallas kernels for 9%

profile of v8, /device:TPU:0, one launch (start us, length us, event | category | flops | bytes accessed | tf_op | source)
XLA Modules:
  0.0 51.4 jit_solution(1115814250310922993)
XLA Ops:
  0.7 1.0 %pad_maximum_fusion = bf16[64,1536]{1,0:T(8,128)(2,1)S(1)} fusion(bf16[64,256]{1,0:T(8,128)(2,1)} %param.9, bf16[64,256]{1,0:T(8,128)(2,1)} %param.8, bf16[64,1024]{1,0:T(8,128)(2,1)} %q_ref.1), kind=kLoop, calls=%fused_computation.17 | loop fusion | flops 589824 | bytes 393216 | tf_op jit(solution)/shard_map/concatenate | solution.py:142
  1.6 21.7 %all_gather.3.q_ref = bf16[256,1536]{1,0:T(8,128)(2,1)} all-gather(bf16[64,1536]{1,0:T(8,128)(2,1)S(1)} %pad_maximum_fusion), channel_id=1, replica_groups=mesh['group'=2,'head'=4,'seq'=4] {'seq'}, dimensions={0}, use_global_device_ids=true | all-gather | bytes 983040 | tf_op jit(solution)/shard_map/all_gather | solution.py:143
  23.3 11.3 %shard_map.73.rest_0_ = f32[192,1152]{1,0:T(8,128)} custom-call(s32[1]{0:T(128)S(6)} %copy.55.len_ref, bf16[256,1536]{1,0:T(8,128)(2,1)} %all_gather.3.q_ref, bf16[1024,256]{1,0:T(8,128)(2,1)} %k_ref.3, bf16[1024,256]{1,0:T(8,128)(2,1)} %v_ref.3), custom_call_target="tpu_custom_call" | custom-call | flops 805306368 | bytes 2523136 | tf_op jit(solution)/shard_map/pallas_call | solution.py:112
  34.6 1.2 %convert.5 = f16[192,1152]{1,0:T(8,128)(2,1)S(1)} convert(f32[192,1152]{1,0:T(8,128)} %shard_map.73.rest_0_) | non-fusion elementwise | flops 221184 | bytes 1327104 | tf_op jit(solution)/shard_map/convert.2
  35.8 0.0 copy-start.1
  35.9 0.1 fusion.20
  35.9 0.1 collective-permute-start
  36.0 3.8 %collective-permute-start.2 = (f16[64,1152]{1,0:T(8,128)(2,1)S(1)}, f16[64,1152]{1,0:T(8,128)(2,1)S(1)}, u32[]{:S(2)}, u32[]{:S(2)}) collective-permute-start(f16[64,1152]{1,0:T(8,128)(2,1)S(1)} %get-tuple-element.14), channel_id=1, source_target_pairs={{0,3},{1,0},{2,1},{3,2},{4,7},{5,4},{6,5},{7,6},{8,11},{9,8},{10,9... | collective-permute-start | bytes 442376 | tf_op jit(solution)/shard_map/ppermute | solution.py:157
  39.8 0.0 collective-permute-start.1
  39.8 0.0 copy-done.1
  39.8 0.1 reshape.84
  39.9 1.0 %fusion.19 = (bf16[256,256]{1,0:T(8,128)(2,1)S(1)}, bf16[256,256]{1,0:T(8,128)(2,1)S(1)}) fusion(bf16[256,1536]{1,0:T(8,128)(2,1)} %all_gather.3.q_ref), kind=kLoop, calls=%fused_computation.36 | loop fusion | bytes 524288 | tf_op jit(solution)/shard_map/slice | solution.py:145
  41.0 0.0 copy-start.2
  41.0 0.7 %copy-done.2 = s32[256]{0:T(256)S(1)} copy-done((s32[256]{0:T(256)S(1)}, s32[256]{0:T(256)}, u32[]{:S(2)}) %copy-start.2) | copy-done | bytes 1048
  41.7 0.1 dynamic_slice.3
  41.7 0.1 fusion.9
  41.8 0.3 select_reduce_fusion
  42.2 0.3 convolution_bitcast_fusion
  42.5 0.2 copy.23
  42.6 0.1 reshape.85
  42.8 0.3 convert_reduce_fusion
  43.0 0.1 copy.26
  43.1 0.1 copy.25
  43.2 4.5 %shard_map.74 = f32[64,1152]{1,0:T(8,128)} custom-call(s32[1]{0:T(128)S(6)} %copy.55.len_ref, bf16[64,1024]{1,0:T(8,128)(2,1)} %q_ref.1, bf16[1024,256]{1,0:T(8,128)(2,1)} %k_ref.3, bf16[1024,256]{1,0:T(8,128)(2,1)} %v_ref.3, f32[192,1152]{1,0:T(8,128)} %shard_map.73.rest_0_), custom_call_target="tpu_custom_call" | custom-call | flops 268435456 | bytes 1474560 | tf_op jit(solution)/shard_map/pallas_call | solution.py:112
  47.7 0.0 collective-permute-done
  47.8 0.0 collective-permute-done.2
  47.8 0.0 copy-start
  47.8 1.6 %collective-permute-done.1 = f16[64,1152]{1,0:T(8,128)(2,1)S(1)} collective-permute-done((f16[64,1152]{1,0:T(8,128)(2,1)S(1)}, f16[64,1152]{1,0:T(8,128)(2,1)S(1)}, u32[]{:S(2)}, u32[]{:S(2)}) %collective-permute-start.1) | collective-permute-done | bytes 147488 | tf_op jit(solution)/shard_map/ppermute | solution.py:157
  49.5 0.0 copy-done
  49.5 0.1 add_add_fusion
  49.6 0.1 div.11
  49.7 0.1 mul.86
  49.9 0.1 mul.90
  50.0 0.1 mul.94
  50.1 0.1 mul.98
  50.3 0.1 mul.102
  50.4 1.0 %fusion.1 = bf16[64,1024]{1,0:T(8,128)(2,1)} fusion(f32[8,8,8,128]{3,2,1,0:T(8,128)S(1)} %bitcast.46, f32[8,8,8,128]{3,2,1,0:T(8,128)S(1)} %bitcast.51, f32[8,8,8,128]{3,2,1,0:T(8,128)S(1)} %bitcast.50, f32[8,8,8,128]{3,2,1,0:T(8,128)S(1)} %bitcast.49, f32[8,8,8,128]{3,2,1,0:T(8,128)S(1)} %bitcast.48, f32[64,1024]{1,0:T(8,128)S(1)} %reshape.85, ...), kind=kLoop, calls=%fused_computation.7 | loop fusion | flops 720896 | bytes 3014656 | tf_op jit(solution)/shard_map/convert_element_type | solution.py:224
  (6 shorter events, 0.1 us)
Async XLA Ops:
  35.8 4.0 %copy-start.1 = (bf16[64,1024]{1,0:T(8,128)(2,1)S(1)}, bf16[64,1024]{1,0:T(8,128)(2,1)}, u32[]{:S(2)}) copy-start(bf16[64,1024]{1,0:T(8,128)(2,1)} %q_ref.1) | copy-start | bytes 393220
  35.9 11.8 %collective-permute-start = (f16[64,1152]{1,0:T(8,128)(2,1)S(1)}, f16[64,1152]{1,0:T(8,128)(2,1)S(1)}, u32[]{:S(2)}, u32[]{:S(2)}) collective-permute-start(f16[64,1152]{1,0:T(8,128)(2,1)S(1)} %get-tuple-element.13), channel_id=1, source_target_pairs={{0,1},{1,2},{2,3},{3,0},{4,5},{5,6},{6,7},{7,4},{8,9},{9,10},{10,1... | collective-permute-start | bytes 442376 | tf_op jit(solution)/shard_map/ppermute | solution.py:157
  36.0 11.8 %collective-permute-start.2 = (f16[64,1152]{1,0:T(8,128)(2,1)S(1)}, f16[64,1152]{1,0:T(8,128)(2,1)S(1)}, u32[]{:S(2)}, u32[]{:S(2)}) collective-permute-start(f16[64,1152]{1,0:T(8,128)(2,1)S(1)} %get-tuple-element.14), channel_id=1, source_target_pairs={{0,3},{1,0},{2,1},{3,2},{4,7},{5,4},{6,5},{7,6},{8,11},{9,8},{10,9... | collective-permute-start | bytes 442376 | tf_op jit(solution)/shard_map/ppermute | solution.py:157
  39.8 9.6 %collective-permute-start.1 = (f16[64,1152]{1,0:T(8,128)(2,1)S(1)}, f16[64,1152]{1,0:T(8,128)(2,1)S(1)}, u32[]{:S(2)}, u32[]{:S(2)}) collective-permute-start(f16[64,1152]{1,0:T(8,128)(2,1)S(1)} %get-tuple-element.15), channel_id=1, source_target_pairs={{0,2},{1,3},{2,0},{3,1},{4,6},{5,7},{6,4},{7,5},{8,10},{9,11},{10,... | collective-permute-start | bytes 442376 | tf_op jit(solution)/shard_map/ppermute | solution.py:157
  41.0 0.7 %copy-start.2 = (s32[256]{0:T(256)S(1)}, s32[256]{0:T(256)}, u32[]{:S(2)}) copy-start(s32[256]{0:T(256)} %param.12) | copy-start | bytes 3076
  47.8 1.6 %copy-start = (f32[64,1152]{1,0:T(8,128)S(1)}, f32[64,1152]{1,0:T(8,128)}, u32[]{:S(2)}) copy-start(f32[64,1152]{1,0:T(8,128)} %shard_map.74) | copy-start | bytes 884740

commit v9 on v8

--- a/solution.py
+++ b/solution.py
@@ -25,7 +25,6 @@
     scale = HEAD_DIM ** (-0.5)
     lane = lax.broadcasted_iota(jnp.int32, (rows, 128), 1)
     position = lax.broadcasted_iota(jnp.int32, (1, cache_rows), 1)
-    ones = jnp.ones((SUB, 128), jnp.bfloat16)
     extra = jnp.zeros((rows, 128), jnp.float32)
 
     def query_rows(h):
@@ -58,7 +57,7 @@
             w = jnp.exp(s - tm).astype(jnp.bfloat16)
             vb = v_ref[b * SUB:(b + 1) * SUB, g * HEAD_DIM:(g + 1) * HEAD_DIM]
             numers.append(jnp.dot(w, vb, preferred_element_type=jnp.float32))
-            denoms.append(jnp.dot(w, ones, preferred_element_type=jnp.float32)[:, :1])
+            denoms.append(jnp.sum(w.astype(jnp.float32), axis=1, keepdims=True))
             maxes.append(tm)
         m = maxes[0]
         for tm in maxes[1:]:

time: 51.6 us -> 46.5 us (0.901)
  Pallas kernels: 15.8 us -> 9.58 us
  waiting for transfers between devices: 1.61 us -> 2.69 us
    pallas_call x2, Pallas kernels: 15.8 us -> 9.58 us  [cache_partials(): pl.pallas_call(functools.partial(cache_kernel, seq_count, first, pieces,...]
    ppermute x3, waiting for transfers between devices: 1.61 us -> 2.69 us  [on_device(): lax.ppermute(to_half(piece, qcols, heads_q), 'seq', [(i, (i + shift) % se...]
  transfers between devices with their start and end apart: 3 -> 3, of which waited for: 1 -> 1; matrix products, arithmetic and copies ran while one was open for 5% -> 6% of each run, Pallas kernels for 9% -> 7%
where the time goes in v9:
time: 46.5 us; the launch traced here: 46.2 us
  blocking collectives  21.7 us (47%)
  Pallas kernels  9.58 us (21%)
  starting transfers between devices  3.87 us (8%)
  other arithmetic  3.71 us (8%)
  local copies, waits for them, and re-layouts  3.18 us (7%)
  waiting for transfers between devices  2.69 us (6%)
  between operations  0.84 us (2%)
  matrix products  0.61 us (1%)
    all_gather x1, blocking collectives, on_device(): gathered = lax.all_gather(packed, 'seq', axis=0, tiled=True)  21.7 us
    pallas_call x2, Pallas kernels, cache_partials(): pl.pallas_call(functools.partial(cache_kernel, seq_count, first, pieces,...  9.58 us
    ppermute x3, starting transfers between devices, on_device(): lax.ppermute(to_half(piece, qcols, heads_q), 'seq', [(i, (i + shift) % se...  3.87 us
    ppermute x3, waiting for transfers between devices, on_device(): lax.ppermute(to_half(piece, qcols, heads_q), 'seq', [(i, (i + shift) % se...  2.69 us
    another operation x1, other arithmetic  1.22 us
    slice x1, local copies, waits for them, and re-layouts, on_device(): all_values = gathered[:, qcols + kcols:]  0.99 us
    convert_element_type x1, other arithmetic, on_device(): return attended.reshape(own_count, qcols).astype(jnp.bfloat16)  0.96 us
    concatenate x1, other arithmetic, on_device(): packed = jnp.concatenate([new_queries, new_keys, new_values], axis=1)  0.96 us
  transfers between devices with their start and end apart: 3, of which 1 were waited for; matrix products, arithmetic and copies ran while one was open for 6% of the time, Pallas kernels for 7%

profile of v9, /device:TPU:0, one launch (start us, length us, event | category | flops | bytes accessed | tf_op | source)
XLA Modules:
  0.0 46.2 jit_solution(5256282218325488100)
XLA Ops:
  0.7 1.0 %pad_maximum_fusion = bf16[64,1536]{1,0:T(8,128)(2,1)S(1)} fusion(bf16[64,256]{1,0:T(8,128)(2,1)} %param.9, bf16[64,256]{1,0:T(8,128)(2,1)} %param.8, bf16[64,1024]{1,0:T(8,128)(2,1)} %q_ref.1), kind=kLoop, calls=%fused_computation.17 | loop fusion | flops 589824 | bytes 393216 | tf_op jit(solution)/shard_map/concatenate | solution.py:141
  1.6 21.7 %all_gather.3.q_ref = bf16[256,1536]{1,0:T(8,128)(2,1)} all-gather(bf16[64,1536]{1,0:T(8,128)(2,1)S(1)} %pad_maximum_fusion), channel_id=1, replica_groups=mesh['group'=2,'head'=4,'seq'=4] {'seq'}, dimensions={0}, use_global_device_ids=true | all-gather | bytes 983040 | tf_op jit(solution)/shard_map/all_gather | solution.py:142
  23.3 6.1 %shard_map.73.rest_0_ = f32[192,1152]{1,0:T(8,128)} custom-call(s32[1]{0:T(128)S(6)} %copy.55.len_ref, bf16[256,1536]{1,0:T(8,128)(2,1)} %all_gather.3.q_ref, bf16[1024,256]{1,0:T(8,128)(2,1)} %k_ref.3, bf16[1024,256]{1,0:T(8,128)(2,1)} %v_ref.3), custom_call_target="tpu_custom_call" | custom-call | flops 805306368 | bytes 2523136 | tf_op jit(solution)/shard_map/pallas_call | solution.py:111
  29.5 1.2 %convert.5 = f16[192,1152]{1,0:T(8,128)(2,1)S(1)} convert(f32[192,1152]{1,0:T(8,128)} %shard_map.73.rest_0_) | non-fusion elementwise | flops 221184 | bytes 1327104 | tf_op jit(solution)/shard_map/convert.2
  30.7 0.0 copy-start.1
  30.7 0.1 fusion.20
  30.8 0.1 collective-permute-start
  30.8 3.8 %collective-permute-start.2 = (f16[64,1152]{1,0:T(8,128)(2,1)S(1)}, f16[64,1152]{1,0:T(8,128)(2,1)S(1)}, u32[]{:S(2)}, u32[]{:S(2)}) collective-permute-start(f16[64,1152]{1,0:T(8,128)(2,1)S(1)} %get-tuple-element.14), channel_id=1, source_target_pairs={{0,3},{1,0},{2,1},{3,2},{4,7},{5,4},{6,5},{7,6},{8,11},{9,8},{10,9... | collective-permute-start | bytes 442376 | tf_op jit(solution)/shard_map/ppermute | solution.py:156
  34.6 0.0 collective-permute-start.1
  34.6 0.0 copy-done.1
  34.7 0.1 reshape.84
  34.7 1.0 %fusion.19 = (bf16[256,256]{1,0:T(8,128)(2,1)S(1)}, bf16[256,256]{1,0:T(8,128)(2,1)S(1)}) fusion(bf16[256,1536]{1,0:T(8,128)(2,1)} %all_gather.3.q_ref), kind=kLoop, calls=%fused_computation.36 | loop fusion | bytes 524288 | tf_op jit(solution)/shard_map/slice | solution.py:144
  35.8 0.0 copy-start.2
  35.8 0.7 %copy-done.2 = s32[256]{0:T(256)S(1)} copy-done((s32[256]{0:T(256)S(1)}, s32[256]{0:T(256)}, u32[]{:S(2)}) %copy-start.2) | copy-done | bytes 1048
  36.5 0.1 dynamic_slice.3
  36.6 0.1 fusion.9
  36.7 0.3 select_reduce_fusion
  37.0 0.3 convolution_bitcast_fusion
  37.3 0.2 copy.23
  37.5 0.1 reshape.85
  37.6 0.3 convert_reduce_fusion
  37.9 0.1 copy.26
  37.9 0.1 copy.25
  38.0 3.5 %shard_map.74 = f32[64,1152]{1,0:T(8,128)} custom-call(s32[1]{0:T(128)S(6)} %copy.55.len_ref, bf16[64,1024]{1,0:T(8,128)(2,1)} %q_ref.1, bf16[1024,256]{1,0:T(8,128)(2,1)} %k_ref.3, bf16[1024,256]{1,0:T(8,128)(2,1)} %v_ref.3, f32[192,1152]{1,0:T(8,128)} %shard_map.73.rest_0_), custom_call_target="tpu_custom_call" | custom-call | flops 268435456 | bytes 1474560 | tf_op jit(solution)/shard_map/pallas_call | solution.py:111
  41.5 0.0 collective-permute-done
  41.5 0.0 collective-permute-done.2
  41.6 0.0 copy-start
  41.6 2.7 %collective-permute-done.1 = f16[64,1152]{1,0:T(8,128)(2,1)S(1)} collective-permute-done((f16[64,1152]{1,0:T(8,128)(2,1)S(1)}, f16[64,1152]{1,0:T(8,128)(2,1)S(1)}, u32[]{:S(2)}, u32[]{:S(2)}) %collective-permute-start.1) | collective-permute-done | bytes 147488 | tf_op jit(solution)/shard_map/ppermute | solution.py:156
  44.3 0.0 copy-done
  44.3 0.1 add_add_fusion
  44.4 0.1 div.11
  44.6 0.1 mul.86
  44.7 0.1 mul.90
  44.8 0.1 mul.94
  45.0 0.1 mul.98
  45.1 0.1 mul.102
  45.2 1.0 %fusion.1 = bf16[64,1024]{1,0:T(8,128)(2,1)} fusion(f32[8,8,8,128]{3,2,1,0:T(8,128)S(1)} %bitcast.46, f32[8,8,8,128]{3,2,1,0:T(8,128)S(1)} %bitcast.51, f32[8,8,8,128]{3,2,1,0:T(8,128)S(1)} %bitcast.50, f32[8,8,8,128]{3,2,1,0:T(8,128)S(1)} %bitcast.49, f32[8,8,8,128]{3,2,1,0:T(8,128)S(1)} %bitcast.48, f32[64,1024]{1,0:T(8,128)S(1)} %reshape.85, ...), kind=kLoop, calls=%fused_computation.7 | loop fusion | flops 720896 | bytes 3014656 | tf_op jit(solution)/shard_map/convert_element_type | solution.py:223
  (6 shorter events, 0.1 us)
Async XLA Ops:
  30.7 4.0 %copy-start.1 = (bf16[64,1024]{1,0:T(8,128)(2,1)S(1)}, bf16[64,1024]{1,0:T(8,128)(2,1)}, u32[]{:S(2)}) copy-start(bf16[64,1024]{1,0:T(8,128)(2,1)} %q_ref.1) | copy-start | bytes 393220
  30.8 10.7 %collective-permute-start = (f16[64,1152]{1,0:T(8,128)(2,1)S(1)}, f16[64,1152]{1,0:T(8,128)(2,1)S(1)}, u32[]{:S(2)}, u32[]{:S(2)}) collective-permute-start(f16[64,1152]{1,0:T(8,128)(2,1)S(1)} %get-tuple-element.13), channel_id=1, source_target_pairs={{0,1},{1,2},{2,3},{3,0},{4,5},{5,6},{6,7},{7,4},{8,9},{9,10},{10,1... | collective-permute-start | bytes 442376 | tf_op jit(solution)/shard_map/ppermute | solution.py:156
  30.8 10.7 %collective-permute-start.2 = (f16[64,1152]{1,0:T(8,128)(2,1)S(1)}, f16[64,1152]{1,0:T(8,128)(2,1)S(1)}, u32[]{:S(2)}, u32[]{:S(2)}) collective-permute-start(f16[64,1152]{1,0:T(8,128)(2,1)S(1)} %get-tuple-element.14), channel_id=1, source_target_pairs={{0,3},{1,0},{2,1},{3,2},{4,7},{5,4},{6,5},{7,6},{8,11},{9,8},{10,9... | collective-permute-start | bytes 442376 | tf_op jit(solution)/shard_map/ppermute | solution.py:156
  34.6 9.6 %collective-permute-start.1 = (f16[64,1152]{1,0:T(8,128)(2,1)S(1)}, f16[64,1152]{1,0:T(8,128)(2,1)S(1)}, u32[]{:S(2)}, u32[]{:S(2)}) collective-permute-start(f16[64,1152]{1,0:T(8,128)(2,1)S(1)} %get-tuple-element.15), channel_id=1, source_target_pairs={{0,2},{1,3},{2,0},{3,1},{4,6},{5,7},{6,4},{7,5},{8,10},{9,11},{10,... | collective-permute-start | bytes 442376 | tf_op jit(solution)/shard_map/ppermute | solution.py:156
  35.8 0.7 %copy-start.2 = (s32[256]{0:T(256)S(1)}, s32[256]{0:T(256)}, u32[]{:S(2)}) copy-start(s32[256]{0:T(256)} %param.12) | copy-start | bytes 3076
  41.6 2.7 %copy-start = (f32[64,1152]{1,0:T(8,128)S(1)}, f32[64,1152]{1,0:T(8,128)}, u32[]{:S(2)}) copy-start(f32[64,1152]{1,0:T(8,128)} %shard_map.74) | copy-start | bytes 884740

commit v10 on v9

--- a/solution.py
+++ b/solution.py
@@ -38,6 +38,7 @@
             blocks.append(q_ref[pl.ds(pl.multiple_of(index * piece, piece), piece), cols])
         return jnp.concatenate(blocks, axis=0)
 
+    keys_t = [k_ref[:, g * HEAD_DIM:(g + 1) * HEAD_DIM].T for g in range(heads_kv)]
     if stack > 1:
         units = [list(range(g * group, (g + 1) * group)) for g in range(heads_kv)]
     else:
@@ -48,11 +49,9 @@
         span = qx.shape[0]
         maxes, numers, denoms = [], [], []
         for b in range(tiles):
-            kb = k_ref[b * SUB:(b + 1) * SUB, g * HEAD_DIM:(g + 1) * HEAD_DIM]
+            kb = keys_t[g][:, b * SUB:(b + 1) * SUB]
             bias = jnp.where(position[:, b * SUB:(b + 1) * SUB] < live, 0.0, NEG_FILL)
-            s = lax.dot_general(
-                qx, kb, (((1,), (1,)), ((), ())), preferred_element_type=jnp.float32
-            ) * scale + bias
+            s = jnp.dot(qx, kb, preferred_element_type=jnp.float32) * scale + bias
             tm = jnp.max(s, axis=1, keepdims=True)
             w = jnp.exp(s - tm).astype(jnp.bfloat16)
             vb = v_ref[b * SUB:(b + 1) * SUB, g * HEAD_DIM:(g + 1) * HEAD_DIM]

time: 46.5 us -> 46.3 us (level)
  transfers between devices with their start and end apart: 3 -> 3, of which waited for: 1 -> 1; matrix products, arithmetic and copies ran while one was open for 6% -> 6% of each run, Pallas kernels for 7% -> 8%
where the time goes in v10:
time: 46.3 us; the launch traced here: 46.1 us
  blocking collectives  21.7 us (47%)
  Pallas kernels  9.44 us (20%)
  starting transfers between devices  3.87 us (8%)
  other arithmetic  3.71 us (8%)
  local copies, waits for them, and re-layouts  3.18 us (7%)
  waiting for transfers between devices  2.68 us (6%)
  between operations  0.84 us (2%)
  matrix products  0.62 us (1%)
    all_gather x1, blocking collectives, on_device(): gathered = lax.all_gather(packed, 'seq', axis=0, tiled=True)  21.7 us
    pallas_call x2, Pallas kernels, cache_partials(): pl.pallas_call(functools.partial(cache_kernel, seq_count, first, pieces,...  9.44 us
    ppermute x3, starting transfers between devices, on_device(): lax.ppermute(to_half(piece, qcols, heads_q), 'seq', [(i, (i + shift) % se...  3.87 us
    ppermute x3, waiting for transfers between devices, on_device(): lax.ppermute(to_half(piece, qcols, heads_q), 'seq', [(i, (i + shift) % se...  2.68 us
    another operation x1, other arithmetic  1.22 us
    slice x1, local copies, waits for them, and re-layouts, on_device(): all_values = gathered[:, qcols + kcols:]  0.99 us
    convert_element_type x1, other arithmetic, on_device(): return attended.reshape(own_count, qcols).astype(jnp.bfloat16)  0.96 us
    concatenate x1, other arithmetic, on_device(): packed = jnp.concatenate([new_queries, new_keys, new_values], axis=1)  0.96 us
  transfers between devices with their start and end apart: 3, of which 1 were waited for; matrix products, arithmetic and copies ran while one was open for 6% of the time, Pallas kernels for 8%

profile of v10, /device:TPU:0, one launch (start us, length us, event | category | flops | bytes accessed | tf_op | source)
XLA Modules:
  0.0 46.1 jit_solution(11061427603969427357)
XLA Ops:
  0.7 1.0 %pad_maximum_fusion = bf16[64,1536]{1,0:T(8,128)(2,1)S(1)} fusion(bf16[64,256]{1,0:T(8,128)(2,1)} %param.9, bf16[64,256]{1,0:T(8,128)(2,1)} %param.8, bf16[64,1024]{1,0:T(8,128)(2,1)} %q_ref.1), kind=kLoop, calls=%fused_computation.17 | loop fusion | flops 589824 | bytes 393216 | tf_op jit(solution)/shard_map/concatenate | solution.py:140
  1.6 21.7 %all_gather.3.q_ref = bf16[256,1536]{1,0:T(8,128)(2,1)} all-gather(bf16[64,1536]{1,0:T(8,128)(2,1)S(1)} %pad_maximum_fusion), channel_id=1, replica_groups=mesh['group'=2,'head'=4,'seq'=4] {'seq'}, dimensions={0}, use_global_device_ids=true | all-gather | bytes 983040 | tf_op jit(solution)/shard_map/all_gather | solution.py:141
  23.3 6.0 %shard_map.73.rest_0_ = f32[192,1152]{1,0:T(8,128)} custom-call(s32[1]{0:T(128)S(6)} %copy.55.len_ref, bf16[256,1536]{1,0:T(8,128)(2,1)} %all_gather.3.q_ref, bf16[1024,256]{1,0:T(8,128)(2,1)} %k_ref.3, bf16[1024,256]{1,0:T(8,128)(2,1)} %v_ref.3), custom_call_target="tpu_custom_call" | custom-call | flops 805306368 | bytes 2523136 | tf_op jit(solution)/shard_map/pallas_call | solution.py:110
  29.3 1.2 %convert.5 = f16[192,1152]{1,0:T(8,128)(2,1)S(1)} convert(f32[192,1152]{1,0:T(8,128)} %shard_map.73.rest_0_) | non-fusion elementwise | flops 221184 | bytes 1327104 | tf_op jit(solution)/shard_map/convert.2
  30.5 0.0 copy-start.1
  30.5 0.1 fusion.20
  30.6 0.1 collective-permute-start
  30.7 3.8 %collective-permute-start.2 = (f16[64,1152]{1,0:T(8,128)(2,1)S(1)}, f16[64,1152]{1,0:T(8,128)(2,1)S(1)}, u32[]{:S(2)}, u32[]{:S(2)}) collective-permute-start(f16[64,1152]{1,0:T(8,128)(2,1)S(1)} %get-tuple-element.14), channel_id=1, source_target_pairs={{0,3},{1,0},{2,1},{3,2},{4,7},{5,4},{6,5},{7,6},{8,11},{9,8},{10,9... | collective-permute-start | bytes 442376 | tf_op jit(solution)/shard_map/ppermute | solution.py:155
  34.5 0.0 collective-permute-start.1
  34.5 0.0 copy-done.1
  34.5 0.1 reshape.84
  34.6 1.0 %fusion.19 = (bf16[256,256]{1,0:T(8,128)(2,1)S(1)}, bf16[256,256]{1,0:T(8,128)(2,1)S(1)}) fusion(bf16[256,1536]{1,0:T(8,128)(2,1)} %all_gather.3.q_ref), kind=kLoop, calls=%fused_computation.36 | loop fusion | bytes 524288 | tf_op jit(solution)/shard_map/slice | solution.py:143
  35.7 0.0 copy-start.2
  35.7 0.7 %copy-done.2 = s32[256]{0:T(256)S(1)} copy-done((s32[256]{0:T(256)S(1)}, s32[256]{0:T(256)}, u32[]{:S(2)}) %copy-start.2) | copy-done | bytes 1048
  36.4 0.1 dynamic_slice.3
  36.4 0.1 fusion.9
  36.5 0.3 select_reduce_fusion
  36.9 0.3 convolution_bitcast_fusion
  37.2 0.2 copy.23
  37.3 0.1 reshape.85
  37.5 0.3 convert_reduce_fusion
  37.7 0.1 copy.26
  37.8 0.1 copy.25
  37.9 3.5 %shard_map.74 = f32[64,1152]{1,0:T(8,128)} custom-call(s32[1]{0:T(128)S(6)} %copy.55.len_ref, bf16[64,1024]{1,0:T(8,128)(2,1)} %q_ref.1, bf16[1024,256]{1,0:T(8,128)(2,1)} %k_ref.3, bf16[1024,256]{1,0:T(8,128)(2,1)} %v_ref.3, f32[192,1152]{1,0:T(8,128)} %shard_map.73.rest_0_), custom_call_target="tpu_custom_call" | custom-call | flops 268435456 | bytes 1474560 | tf_op jit(solution)/shard_map/pallas_call | solution.py:110
  41.4 0.0 collective-permute-done
  41.4 0.0 collective-permute-done.2
  41.4 0.0 copy-start
  41.4 2.7 %collective-permute-done.1 = f16[64,1152]{1,0:T(8,128)(2,1)S(1)} collective-permute-done((f16[64,1152]{1,0:T(8,128)(2,1)S(1)}, f16[64,1152]{1,0:T(8,128)(2,1)S(1)}, u32[]{:S(2)}, u32[]{:S(2)}) %collective-permute-start.1) | collective-permute-done | bytes 147488 | tf_op jit(solution)/shard_map/ppermute | solution.py:155
  44.1 0.0 copy-done
  44.1 0.1 add_add_fusion
  44.3 0.1 div.11
  44.4 0.1 mul.86
  44.6 0.1 mul.90
  44.7 0.1 mul.94
  44.8 0.1 mul.98
  45.0 0.1 mul.102
  45.1 1.0 %fusion.1 = bf16[64,1024]{1,0:T(8,128)(2,1)} fusion(f32[8,8,8,128]{3,2,1,0:T(8,128)S(1)} %bitcast.46, f32[8,8,8,128]{3,2,1,0:T(8,128)S(1)} %bitcast.51, f32[8,8,8,128]{3,2,1,0:T(8,128)S(1)} %bitcast.50, f32[8,8,8,128]{3,2,1,0:T(8,128)S(1)} %bitcast.49, f32[8,8,8,128]{3,2,1,0:T(8,128)S(1)} %bitcast.48, f32[64,1024]{1,0:T(8,128)S(1)} %reshape.85, ...), kind=kLoop, calls=%fused_computation.7 | loop fusion | flops 720896 | bytes 3014656 | tf_op jit(solution)/shard_map/convert_element_type | solution.py:222
  (6 shorter events, 0.1 us)
Async XLA Ops:
  30.5 4.0 %copy-start.1 = (bf16[64,1024]{1,0:T(8,128)(2,1)S(1)}, bf16[64,1024]{1,0:T(8,128)(2,1)}, u32[]{:S(2)}) copy-start(bf16[64,1024]{1,0:T(8,128)(2,1)} %q_ref.1) | copy-start | bytes 393220
  30.6 10.7 %collective-permute-start = (f16[64,1152]{1,0:T(8,128)(2,1)S(1)}, f16[64,1152]{1,0:T(8,128)(2,1)S(1)}, u32[]{:S(2)}, u32[]{:S(2)}) collective-permute-start(f16[64,1152]{1,0:T(8,128)(2,1)S(1)} %get-tuple-element.13), channel_id=1, source_target_pairs={{0,1},{1,2},{2,3},{3,0},{4,5},{5,6},{6,7},{7,4},{8,9},{9,10},{10,1... | collective-permute-start | bytes 442376 | tf_op jit(solution)/shard_map/ppermute | solution.py:155
  30.7 10.7 %collective-permute-start.2 = (f16[64,1152]{1,0:T(8,128)(2,1)S(1)}, f16[64,1152]{1,0:T(8,128)(2,1)S(1)}, u32[]{:S(2)}, u32[]{:S(2)}) collective-permute-start(f16[64,1152]{1,0:T(8,128)(2,1)S(1)} %get-tuple-element.14), channel_id=1, source_target_pairs={{0,3},{1,0},{2,1},{3,2},{4,7},{5,4},{6,5},{7,6},{8,11},{9,8},{10,9... | collective-permute-start | bytes 442376 | tf_op jit(solution)/shard_map/ppermute | solution.py:155
  34.5 9.6 %collective-permute-start.1 = (f16[64,1152]{1,0:T(8,128)(2,1)S(1)}, f16[64,1152]{1,0:T(8,128)(2,1)S(1)}, u32[]{:S(2)}, u32[]{:S(2)}) collective-permute-start(f16[64,1152]{1,0:T(8,128)(2,1)S(1)} %get-tuple-element.15), channel_id=1, source_target_pairs={{0,2},{1,3},{2,0},{3,1},{4,6},{5,7},{6,4},{7,5},{8,10},{9,11},{10,... | collective-permute-start | bytes 442376 | tf_op jit(solution)/shard_map/ppermute | solution.py:155
  35.7 0.7 %copy-start.2 = (s32[256]{0:T(256)S(1)}, s32[256]{0:T(256)}, u32[]{:S(2)}) copy-start(s32[256]{0:T(256)} %param.12) | copy-start | bytes 3076
  41.4 2.7 %copy-start = (f32[64,1152]{1,0:T(8,128)S(1)}, f32[64,1152]{1,0:T(8,128)}, u32[]{:S(2)}) copy-start(f32[64,1152]{1,0:T(8,128)} %shard_map.74) | copy-start | bytes 884740

commit v11 on v10

--- a/solution.py
+++ b/solution.py
@@ -171,7 +171,7 @@
         recv = lax.all_to_all(to_half(partial, qcols, heads_q), "seq", 0, 0, tiled=True)
         recv = recv.astype(jnp.float32)
         parts = [recv[j * own_count:(j + 1) * own_count] for j in range(seq_count)]
-    part_mean = [p[:, :qcols].reshape(own_count, heads_q, head_size) for p in parts]
+    part_mean = [p[:, :qcols] for p in parts]
     part_denom = [
         p[:, qcols:qcols + heads_q] + p[:, qcols + heads_q:qcols + 2 * heads_q] for p in parts
     ]
@@ -204,22 +204,35 @@
         fresh_weights,
         all_values.reshape(join_rows, heads_kv, head_size),
         preferred_element_type=jnp.float32,
-    ).reshape(own_count, heads_q, head_size)
+    ).reshape(own_count, qcols)
     fresh_denom = jnp.sum(fresh_weights.astype(jnp.float32), axis=-1).reshape(own_count, heads_q)
     fresh_max = fresh_max.reshape(own_count, heads_q)
 
-    row_max = fresh_max
-    for m in part_max:
+
+    def spread(x):
+        return jnp.broadcast_to(x[:, :, None], (own_count, heads_q, head_size)).reshape(
+            own_count, qcols
+        )
+
+    own_mean, own_denom, own_max = part_mean[-1], part_denom[-1], part_max[-1]
+    local_max = jnp.maximum(fresh_max, own_max)
+    fresh_factor = jnp.exp(fresh_max - local_max)
+    own_weight = jnp.exp(own_max - local_max) * own_denom
+    local_numer = fresh_numer * spread(fresh_factor) + own_mean * spread(own_weight)
+    local_denom = fresh_denom * fresh_factor + own_weight
+
+    row_max = local_max
+    for m in part_max[:-1]:
         row_max = jnp.maximum(row_max, m)
-    fresh_factor = jnp.exp(fresh_max - row_max)
-    total_numer = fresh_numer * fresh_factor[..., None]
-    total_denom = fresh_denom * fresh_factor
-    for o_j, d_j, m_j in zip(part_mean, part_denom, part_max):
+    local_factor = jnp.exp(local_max - row_max)
+    total_numer = local_numer * spread(local_factor)
+    total_denom = local_denom * local_factor
+    for o_j, d_j, m_j in zip(part_mean[:-1], part_denom[:-1], part_max[:-1]):
         w_j = jnp.exp(m_j - row_max) * d_j
-        total_numer = total_numer + o_j * w_j[..., None]
+        total_numer = total_numer + o_j * spread(w_j)
         total_denom = total_denom + w_j
-    attended = total_numer / total_denom[..., None]
-    return attended.reshape(own_count, qcols).astype(jnp.bfloat16)
+    attended = total_numer / spread(total_denom)
+    return attended.astype(jnp.bfloat16)
 
 
 def solution(mesh):

time: 46.3 us -> 46.5 us (level)
    broadcast_in_dim x0 -> x7, local copies, waits for them, and re-layouts: none -> 0.88 us  [spread(): jnp.broadcast_to(x[:, :, None], (own_count, heads_q, head_size))]
    mul x5 -> x0, local copies, waits for them, and re-layouts: 0.63 us -> none  [the longest x4 0.51 us: on_device(): total_numer = total_numer + o_j * w_j[..., None]]
  transfers between devices with their start and end apart: 3 -> 3, of which waited for: 1 -> 1; matrix products, arithmetic and copies ran while one was open for 6% -> 6% of each run, Pallas kernels for 8% -> 7%
where the time goes in v11:
time: 46.5 us; the launch traced here: 46.3 us
  blocking collectives  21.7 us (47%)
  Pallas kernels  9.44 us (20%)
  starting transfers between devices  3.87 us (8%)
  other arithmetic  3.77 us (8%)
  local copies, waits for them, and re-layouts  3.31 us (7%)
  waiting for transfers between devices  2.68 us (6%)
  between operations  0.85 us (2%)
  matrix products  0.62 us (1%)
    all_gather x1, blocking collectives, on_device(): gathered = lax.all_gather(packed, 'seq', axis=0, tiled=True)  21.7 us
    pallas_call x2, Pallas kernels, cache_partials(): pl.pallas_call(functools.partial(cache_kernel, seq_count, first, pieces,...  9.44 us
    ppermute x3, starting transfers between devices, on_device(): lax.ppermute(to_half(piece, qcols, heads_q), 'seq', [(i, (i + shift) % se...  3.87 us
    ppermute x3, waiting for transfers between devices, on_device(): lax.ppermute(to_half(piece, qcols, heads_q), 'seq', [(i, (i + shift) % se...  2.68 us
    another operation x1, other arithmetic  1.22 us
    convert_element_type x1, other arithmetic, on_device(): return attended.astype(jnp.bfloat16)  1.02 us
    slice x1, local copies, waits for them, and re-layouts, on_device(): all_values = gathered[:, qcols + kcols:]  0.99 us
    concatenate x1, other arithmetic, on_device(): packed = jnp.concatenate([new_queries, new_keys, new_values], axis=1)  0.96 us
  transfers between devices with their start and end apart: 3, of which 1 were waited for; matrix products, arithmetic and copies ran while one was open for 6% of the time, Pallas kernels for 7%

profile of v11, /device:TPU:0, one launch (start us, length us, event | category | flops | bytes accessed | tf_op | source)
XLA Modules:
  0.0 46.3 jit_solution(16348474427993243171)
XLA Ops:
  0.7 1.0 %pad_maximum_fusion = bf16[64,1536]{1,0:T(8,128)(2,1)S(1)} fusion(bf16[64,256]{1,0:T(8,128)(2,1)} %param.9, bf16[64,256]{1,0:T(8,128)(2,1)} %param.8, bf16[64,1024]{1,0:T(8,128)(2,1)} %q_ref.1), kind=kLoop, calls=%fused_computation.18 | loop fusion | flops 589824 | bytes 393216 | tf_op jit(solution)/shard_map/concatenate | solution.py:140
  1.6 21.7 %all_gather.3.q_ref = bf16[256,1536]{1,0:T(8,128)(2,1)} all-gather(bf16[64,1536]{1,0:T(8,128)(2,1)S(1)} %pad_maximum_fusion), channel_id=1, replica_groups=mesh['group'=2,'head'=4,'seq'=4] {'seq'}, dimensions={0}, use_global_device_ids=true | all-gather | bytes 983040 | tf_op jit(solution)/shard_map/all_gather | solution.py:141
  23.3 6.0 %shard_map.73.rest_0_ = f32[192,1152]{1,0:T(8,128)} custom-call(s32[1]{0:T(128)S(6)} %copy.57.len_ref, bf16[256,1536]{1,0:T(8,128)(2,1)} %all_gather.3.q_ref, bf16[1024,256]{1,0:T(8,128)(2,1)} %k_ref.3, bf16[1024,256]{1,0:T(8,128)(2,1)} %v_ref.3), custom_call_target="tpu_custom_call" | custom-call | flops 805306368 | bytes 2523136 | tf_op jit(solution)/shard_map/pallas_call | solution.py:110
  29.3 1.2 %convert.5 = f16[192,1152]{1,0:T(8,128)(2,1)S(1)} convert(f32[192,1152]{1,0:T(8,128)} %shard_map.73.rest_0_) | non-fusion elementwise | flops 221184 | bytes 1327104 | tf_op jit(solution)/shard_map/convert.2
  30.5 0.0 copy-start.1
  30.5 0.1 fusion.20
  30.6 0.1 collective-permute-start
  30.7 3.8 %collective-permute-start.2 = (f16[64,1152]{1,0:T(8,128)(2,1)S(1)}, f16[64,1152]{1,0:T(8,128)(2,1)S(1)}, u32[]{:S(2)}, u32[]{:S(2)}) collective-permute-start(f16[64,1152]{1,0:T(8,128)(2,1)S(1)} %get-tuple-element.15), channel_id=1, source_target_pairs={{0,3},{1,0},{2,1},{3,2},{4,7},{5,4},{6,5},{7,6},{8,11},{9,8},{10,9... | collective-permute-start | bytes 442376 | tf_op jit(solution)/shard_map/ppermute | solution.py:155
  34.5 0.0 collective-permute-start.1
  34.5 0.0 copy-done.1
  34.5 0.1 reshape.94
  34.6 1.0 %fusion.19 = (bf16[256,256]{1,0:T(8,128)(2,1)S(1)}, bf16[256,256]{1,0:T(8,128)(2,1)S(1)}) fusion(bf16[256,1536]{1,0:T(8,128)(2,1)} %all_gather.3.q_ref), kind=kLoop, calls=%fused_computation.39 | loop fusion | bytes 524288 | tf_op jit(solution)/shard_map/slice | solution.py:143
  35.7 0.0 copy-start.2
  35.7 0.7 %copy-done.2 = s32[256]{0:T(256)S(1)} copy-done((s32[256]{0:T(256)S(1)}, s32[256]{0:T(256)}, u32[]{:S(2)}) %copy-start.2) | copy-done | bytes 1048
  36.4 0.1 dynamic_slice.3
  36.4 0.1 fusion.9
  36.5 0.3 select_reduce_fusion
  36.9 0.3 convolution_bitcast_fusion
  37.2 0.2 copy.23
  37.3 0.1 reshape.95
  37.5 0.3 convert_reduce_fusion
  37.7 0.1 copy.26
  37.8 0.1 copy.25
  37.9 3.5 %shard_map.74 = f32[64,1152]{1,0:T(8,128)} custom-call(s32[1]{0:T(128)S(6)} %copy.57.len_ref, bf16[64,1024]{1,0:T(8,128)(2,1)} %q_ref.1, bf16[1024,256]{1,0:T(8,128)(2,1)} %k_ref.3, bf16[1024,256]{1,0:T(8,128)(2,1)} %v_ref.3, f32[192,1152]{1,0:T(8,128)} %shard_map.73.rest_0_), custom_call_target="tpu_custom_call" | custom-call | flops 268435456 | bytes 1474560 | tf_op jit(solution)/shard_map/pallas_call | solution.py:110
  41.4 0.0 collective-permute-done
  41.4 0.0 collective-permute-done.2
  41.4 0.0 copy-start
  41.4 2.7 %collective-permute-done.1 = f16[64,1152]{1,0:T(8,128)(2,1)S(1)} collective-permute-done((f16[64,1152]{1,0:T(8,128)(2,1)S(1)}, f16[64,1152]{1,0:T(8,128)(2,1)S(1)}, u32[]{:S(2)}, u32[]{:S(2)}) %collective-permute-start.1) | collective-permute-done | bytes 147488 | tf_op jit(solution)/shard_map/ppermute | solution.py:155
  44.1 0.0 copy-done
  44.1 0.1 add_add_fusion
  44.3 0.1 broadcast_in_dim.38
  44.4 0.1 broadcast_in_dim.32
  44.6 0.1 broadcast_in_dim.33
  44.7 0.1 broadcast_in_dim.34
  44.8 0.1 broadcast_in_dim.35
  45.0 0.1 broadcast_in_dim.36
  45.1 0.1 broadcast_in_dim.37
  45.2 1.0 %fusion.1 = bf16[64,1024]{1,0:T(8,128)(2,1)} fusion(f32[8,8,8,128]{3,2,1,0:T(8,128)S(1)} %bitcast.51, f32[8,8,8,128]{3,2,1,0:T(8,128)S(1)} %bitcast.57, f32[8,8,8,128]{3,2,1,0:T(8,128)S(1)} %bitcast.56, f32[8,8,8,128]{3,2,1,0:T(8,128)S(1)} %bitcast.55, f32[8,8,8,128]{3,2,1,0:T(8,128)S(1)} %bitcast.54, f32[8,8,8,128]{3,2,1,0:T(8,128)S(1)} %bitcast.53, ...), kind=kLoop, calls=%fused_computation.7 | loop fusion | flops 786432 | bytes 3276800 | tf_op jit(solution)/shard_map/convert_element_type | solution.py:235
  (6 shorter events, 0.1 us)
Async XLA Ops:
  30.5 4.0 %copy-start.1 = (bf16[64,1024]{1,0:T(8,128)(2,1)S(1)}, bf16[64,1024]{1,0:T(8,128)(2,1)}, u32[]{:S(2)}) copy-start(bf16[64,1024]{1,0:T(8,128)(2,1)} %q_ref.1) | copy-start | bytes 393220
  30.6 10.7 %collective-permute-start = (f16[64,1152]{1,0:T(8,128)(2,1)S(1)}, f16[64,1152]{1,0:T(8,128)(2,1)S(1)}, u32[]{:S(2)}, u32[]{:S(2)}) collective-permute-start(f16[64,1152]{1,0:T(8,128)(2,1)S(1)} %get-tuple-element.14), channel_id=1, source_target_pairs={{0,1},{1,2},{2,3},{3,0},{4,5},{5,6},{6,7},{7,4},{8,9},{9,10},{10,1... | collective-permute-start | bytes 442376 | tf_op jit(solution)/shard_map/ppermute | solution.py:155
  30.7 10.7 %collective-permute-start.2 = (f16[64,1152]{1,0:T(8,128)(2,1)S(1)}, f16[64,1152]{1,0:T(8,128)(2,1)S(1)}, u32[]{:S(2)}, u32[]{:S(2)}) collective-permute-start(f16[64,1152]{1,0:T(8,128)(2,1)S(1)} %get-tuple-element.15), channel_id=1, source_target_pairs={{0,3},{1,0},{2,1},{3,2},{4,7},{5,4},{6,5},{7,6},{8,11},{9,8},{10,9... | collective-permute-start | bytes 442376 | tf_op jit(solution)/shard_map/ppermute | solution.py:155
  34.5 9.6 %collective-permute-start.1 = (f16[64,1152]{1,0:T(8,128)(2,1)S(1)}, f16[64,1152]{1,0:T(8,128)(2,1)S(1)}, u32[]{:S(2)}, u32[]{:S(2)}) collective-permute-start(f16[64,1152]{1,0:T(8,128)(2,1)S(1)} %get-tuple-element.16), channel_id=1, source_target_pairs={{0,2},{1,3},{2,0},{3,1},{4,6},{5,7},{6,4},{7,5},{8,10},{9,11},{10,... | collective-permute-start | bytes 442376 | tf_op jit(solution)/shard_map/ppermute | solution.py:155
  35.7 0.7 %copy-start.2 = (s32[256]{0:T(256)S(1)}, s32[256]{0:T(256)}, u32[]{:S(2)}) copy-start(s32[256]{0:T(256)} %param.12) | copy-start | bytes 3076
  41.4 2.7 %copy-start = (f32[64,1152]{1,0:T(8,128)S(1)}, f32[64,1152]{1,0:T(8,128)}, u32[]{:S(2)}) copy-start(f32[64,1152]{1,0:T(8,128)} %shard_map.74) | copy-start | bytes 884740

commit v12 on v10

--- a/solution.py
+++ b/solution.py
@@ -121,6 +121,30 @@
     )(*operands)
 
 
+def combine_kernel(heads_q, fnum_ref, fmax_ref, fden_ref, *refs):
+    out_ref = refs[-1]
+    part_refs = refs[:-1]
+    qcols = heads_q * HEAD_DIM
+    for h in range(heads_q):
+        cols = slice(h * HEAD_DIM, (h + 1) * HEAD_DIM)
+        tops = [fmax_ref[:, h:h + 1]]
+        sums = [fden_ref[:, h:h + 1]]
+        for p in part_refs:
+            tops.append(p[:, qcols + 2 * heads_q + h:qcols + 2 * heads_q + h + 1])
+            sums.append(p[:, qcols + h:qcols + h + 1] + p[:, qcols + heads_q + h:qcols + heads_q + h + 1])
+        top = tops[0]
+        for t in tops[1:]:
+            top = jnp.maximum(top, t)
+        weights = [jnp.exp(t - top) * s for t, s in zip(tops, sums)]
+        numer = fnum_ref[:, cols] * jnp.exp(tops[0] - top)
+        for p, w in zip(part_refs, weights[1:]):
+            numer = numer + p[:, cols] * w
+        denom = weights[0]
+        for w in weights[1:]:
+            denom = denom + w
+        out_ref[:, cols] = (numer / denom).astype(out_ref.dtype)
+
+
 def on_device(
     new_queries, new_keys, new_values, cache_keys, cache_values, segment_ids, cache_length
 ):
@@ -171,12 +195,6 @@
         recv = lax.all_to_all(to_half(partial, qcols, heads_q), "seq", 0, 0, tiled=True)
         recv = recv.astype(jnp.float32)
         parts = [recv[j * own_count:(j + 1) * own_count] for j in range(seq_count)]
-    part_mean = [p[:, :qcols].reshape(own_count, heads_q, head_size) for p in parts]
-    part_denom = [
-        p[:, qcols:qcols + heads_q] + p[:, qcols + heads_q:qcols + 2 * heads_q] for p in parts
-    ]
-    part_max = [p[:, qcols + 2 * heads_q:qcols + 3 * heads_q] for p in parts]
-
     own_queries = new_queries.reshape(own_count, heads_kv, group_size, head_size)
     fresh_scores = (
         jnp.einsum(
@@ -204,22 +222,15 @@
         fresh_weights,
         all_values.reshape(join_rows, heads_kv, head_size),
         preferred_element_type=jnp.float32,
-    ).reshape(own_count, heads_q, head_size)
+    ).reshape(own_count, qcols)
     fresh_denom = jnp.sum(fresh_weights.astype(jnp.float32), axis=-1).reshape(own_count, heads_q)
     fresh_max = fresh_max.reshape(own_count, heads_q)
 
-    row_max = fresh_max
-    for m in part_max:
-        row_max = jnp.maximum(row_max, m)
-    fresh_factor = jnp.exp(fresh_max - row_max)
-    total_numer = fresh_numer * fresh_factor[..., None]
-    total_denom = fresh_denom * fresh_factor
-    for o_j, d_j, m_j in zip(part_mean, part_denom, part_max):
-        w_j = jnp.exp(m_j - row_max) * d_j
-        total_numer = total_numer + o_j * w_j[..., None]
-        total_denom = total_denom + w_j
-    attended = total_numer / total_denom[..., None]
-    return attended.reshape(own_count, qcols).astype(jnp.bfloat16)
+
+    return pl.pallas_call(
+        functools.partial(combine_kernel, heads_q),
+        out_shape=jax.ShapeDtypeStruct((own_count, qcols), jnp.bfloat16),
+    )(fresh_numer, fresh_max, fresh_denom, *parts)
 
 
 def solution(mesh):

time: 46.3 us -> 50.3 us (1.086)
  Pallas kernels: 9.44 us -> 14.3 us
  waiting for transfers between devices: 2.68 us -> 0.64 us
  local copies, waits for them, and re-layouts: 3.18 us -> 4.36 us
  other arithmetic: 3.71 us -> 4.74 us
  starting transfers between devices: 3.87 us -> 2.9 us
    pallas_call x0 -> x1, Pallas kernels: none -> 4.84 us  [on_device(): pl.pallas_call(functools.partial(combine_kernel, heads_q), out_shape=jax....]
    convert_element_type x3, other arithmetic: 0.06 us -> 2.19 us  [on_device(): parts.append(lax.ppermute(to_half(piece, qcols, heads_q), 'seq', [(i, (i...]
    ppermute x3, waiting for transfers between devices: 2.68 us -> 0.64 us  [on_device(): lax.ppermute(to_half(piece, qcols, heads_q), 'seq', [(i, (i + shift) % se...]
    ppermute x3, starting transfers between devices: 3.87 us -> 2.9 us  [on_device(): lax.ppermute(to_half(piece, qcols, heads_q), 'seq', [(i, (i + shift) % se...]
    convert_element_type x1 -> x0, other arithmetic: 0.96 us -> none  [on_device(): return attended.reshape(own_count, qcols).astype(jnp.bfloat16)]
    reshape x1, local copies, waits for them, and re-layouts: 0.11 us -> 0.81 us  [on_device(): fresh_numer = jnp.einsum('cgrt,tgd->cgrd', fresh_weights, all_values.resh...]
    mul x5 -> x0, local copies, waits for them, and re-layouts: 0.63 us -> none  [the longest x4 0.51 us: on_device(): total_numer = total_numer + o_j * w_j[..., None]]
    reshape x1, local copies, waits for them, and re-layouts: 0.09 us -> 0.7 us  [on_device(): jnp.sum(fresh_weights.astype(jnp.float32), axis=-1)]
  transfers between devices with their start and end apart: 3 -> 3, of which waited for: 1 -> 1; matrix products, arithmetic and copies ran while one was open for 6% -> 12% of each run, Pallas kernels for 8% -> 7%
where the time goes in v12:
time: 50.3 us; the launch traced here: 50 us
  blocking collectives  21.7 us (43%)
  Pallas kernels  14.3 us (28%)
  other arithmetic  4.74 us (9%)
  local copies, waits for them, and re-layouts  4.36 us (9%)
  starting transfers between devices  2.9 us (6%)
  between operations  0.73 us (1%)
  waiting for transfers between devices  0.64 us (1%)
  matrix products  0.62 us (1%)
    all_gather x1, blocking collectives, on_device(): gathered = lax.all_gather(packed, 'seq', axis=0, tiled=True)  21.7 us
    pallas_call x2, Pallas kernels, cache_partials(): pl.pallas_call(functools.partial(cache_kernel, seq_count, first, pieces,...  9.43 us
    pallas_call x1, Pallas kernels, on_device(): pl.pallas_call(functools.partial(combine_kernel, heads_q), out_shape=jax....  4.84 us
    ppermute x3, starting transfers between devices, on_device(): lax.ppermute(to_half(piece, qcols, heads_q), 'seq', [(i, (i + shift) % se...  2.9 us
    convert_element_type x3, other arithmetic, on_device(): parts.append(lax.ppermute(to_half(piece, qcols, heads_q), 'seq', [(i, (i...  2.19 us
    another operation x1, other arithmetic  1.22 us
  transfers between devices with their start and end apart: 3, of which 1 were waited for; matrix products, arithmetic and copies ran while one was open for 12% of the time, Pallas kernels for 7%

profile of v12, /device:TPU:0, one launch (start us, length us, event | category | flops | bytes accessed | tf_op | source)
XLA Modules:
  0.0 50.0 jit_solution(8605018376206427300)
XLA Ops:
  0.7 1.0 %pad_maximum_fusion = bf16[64,1536]{1,0:T(8,128)(2,1)S(1)} fusion(bf16[64,256]{1,0:T(8,128)(2,1)} %param.9, bf16[64,256]{1,0:T(8,128)(2,1)} %param.8, bf16[64,1024]{1,0:T(8,128)(2,1)} %q_ref.1), kind=kLoop, calls=%fused_computation.6 | loop fusion | flops 589824 | bytes 393216 | tf_op jit(solution)/shard_map/concatenate | solution.py:164
  1.6 21.7 %all_gather.3.q_ref = bf16[256,1536]{1,0:T(8,128)(2,1)} all-gather(bf16[64,1536]{1,0:T(8,128)(2,1)S(1)} %pad_maximum_fusion), channel_id=1, replica_groups=mesh['group'=2,'head'=4,'seq'=4] {'seq'}, dimensions={0}, use_global_device_ids=true | all-gather | bytes 983040 | tf_op jit(solution)/shard_map/all_gather | solution.py:165
  23.3 6.0 %shard_map.73.rest_0_ = f32[192,1152]{1,0:T(8,128)} custom-call(s32[1]{0:T(128)S(6)} %copy.35.len_ref, bf16[256,1536]{1,0:T(8,128)(2,1)} %all_gather.3.q_ref, bf16[1024,256]{1,0:T(8,128)(2,1)} %k_ref.3, bf16[1024,256]{1,0:T(8,128)(2,1)} %v_ref.3), custom_call_target="tpu_custom_call" | custom-call | flops 805306368 | bytes 2523136 | tf_op jit(solution)/shard_map/pallas_call | solution.py:110
  29.3 1.2 %convert.5 = f16[192,1152]{1,0:T(8,128)(2,1)S(1)} convert(f32[192,1152]{1,0:T(8,128)} %shard_map.73.rest_0_) | non-fusion elementwise | flops 221184 | bytes 1327104 | tf_op jit(solution)/shard_map/convert.2
  30.5 0.0 copy-start
  30.6 0.1 fusion.7
  30.6 2.1 %collective-permute-start.2 = (f16[64,1152]{1,0:T(8,128)(2,1)S(1)}, f16[64,1152]{1,0:T(8,128)(2,1)S(1)}, u32[]{:S(2)}, u32[]{:S(2)}) collective-permute-start(f16[64,1152]{1,0:T(8,128)(2,1)S(1)} %get-tuple-element.7), channel_id=1, source_target_pairs={{0,3},{1,0},{2,1},{3,2},{4,7},{5,4},{6,5},{7,6},{8,11},{9,8},{10,9... | collective-permute-start | bytes 442376 | tf_op jit(solution)/shard_map/ppermute | solution.py:179
  32.7 0.0 collective-permute-start.1
  32.7 0.8 %collective-permute-start = (f16[64,1152]{1,0:T(8,128)(2,1)S(1)}, f16[64,1152]{1,0:T(8,128)(2,1)S(1)}, u32[]{:S(2)}, u32[]{:S(2)}) collective-permute-start(f16[64,1152]{1,0:T(8,128)(2,1)S(1)} %get-tuple-element.9), channel_id=1, source_target_pairs={{0,1},{1,2},{2,3},{3,0},{4,5},{5,6},{6,7},{7,4},{8,9},{9,10},{10,1... | collective-permute-start | bytes 442376 | tf_op jit(solution)/shard_map/ppermute | solution.py:179
  33.5 0.0 copy-done
  33.5 0.1 reshape.66
  33.6 1.0 %fusion.6 = (bf16[256,256]{1,0:T(8,128)(2,1)S(1)}, bf16[256,256]{1,0:T(8,128)(2,1)S(1)}) fusion(bf16[256,1536]{1,0:T(8,128)(2,1)} %all_gather.3.q_ref), kind=kLoop, calls=%fused_computation.14 | loop fusion | bytes 524288 | tf_op jit(solution)/shard_map/slice | solution.py:166
  34.7 0.0 copy-start.1
  34.7 0.7 %copy-done.1 = s32[256]{0:T(256)S(1)} copy-done((s32[256]{0:T(256)S(1)}, s32[256]{0:T(256)}, u32[]{:S(2)}) %copy-start.1) | copy-done | bytes 1048
  35.4 0.1 dynamic_slice.3
  35.5 0.1 fusion.4
  35.6 0.3 select_reduce_fusion
  35.9 0.3 convolution_bitcast_fusion
  36.2 0.2 copy.16
  36.4 0.8 %reshape.67.fnum_ref = f32[64,1024]{1,0:T(8,128)} reshape(f32[64,2,4,128]{3,2,1,0:T(4,128)S(1)} %copy.16) | data formatting | bytes 524288 | tf_op jit(solution)/shard_map/reshape | solution.py:225
  37.2 0.3 convert_reduce_fusion
  37.5 0.7 %copy.18.fden_ref = f32[64,8]{1,0:T(8,128)} copy(f32[64,8]{0,1:T(8,128)S(1)} %bitcast.11) | data formatting | bytes 4096 | tf_op jit(solution)/shard_map/reshape | solution.py:226
  38.2 0.7 %copy.17.fmax_ref = f32[64,8]{1,0:T(8,128)} copy(f32[64,8]{0,1:T(8,128)S(1)} %bitcast.10) | data formatting | bytes 4096 | tf_op jit(solution)/shard_map/reshape | solution.py:227
  38.9 3.4 %shard_map.74.refs_3_ = f32[64,1152]{1,0:T(8,128)} custom-call(s32[1]{0:T(128)S(6)} %copy.35.len_ref, bf16[64,1024]{1,0:T(8,128)(2,1)} %q_ref.1, bf16[1024,256]{1,0:T(8,128)(2,1)} %k_ref.3, bf16[1024,256]{1,0:T(8,128)(2,1)} %v_ref.3, f32[192,1152]{1,0:T(8,128)} %shard_map.73.rest_0_), custom_call_target="tpu_custom_call" | custom-call | flops 268435456 | bytes 1474560 | tf_op jit(solution)/shard_map/pallas_call | solution.py:110
  42.3 0.0 collective-permute-done.2
  42.3 0.7 %convert_element_type.22.refs_2_ = f32[64,1152]{1,0:T(8,128)} convert(f16[64,1152]{1,0:T(8,128)(2,1)S(1)} %collective-permute-done.2) | non-fusion elementwise | flops 73728 | bytes 442368 | tf_op jit(solution)/shard_map/convert_element_type | solution.py:183
  43.0 0.6 %collective-permute-done.1 = f16[64,1152]{1,0:T(8,128)(2,1)S(1)} collective-permute-done((f16[64,1152]{1,0:T(8,128)(2,1)S(1)}, f16[64,1152]{1,0:T(8,128)(2,1)S(1)}, u32[]{:S(2)}, u32[]{:S(2)}) %collective-permute-start.1) | collective-permute-done | bytes 147488 | tf_op jit(solution)/shard_map/ppermute | solution.py:179
  43.7 0.7 %convert_element_type.21.refs_1_ = f32[64,1152]{1,0:T(8,128)} convert(f16[64,1152]{1,0:T(8,128)(2,1)S(1)} %collective-permute-done.1) | non-fusion elementwise | flops 73728 | bytes 442368 | tf_op jit(solution)/shard_map/convert_element_type | solution.py:183
  44.4 0.0 collective-permute-done
  44.4 0.7 %convert_element_type.20.refs_0_ = f32[64,1152]{1,0:T(8,128)} convert(f16[64,1152]{1,0:T(8,128)(2,1)S(1)} %collective-permute-done) | non-fusion elementwise | flops 73728 | bytes 442368 | tf_op jit(solution)/shard_map/convert_element_type | solution.py:183
  45.1 4.8 %shard_map.75 = bf16[64,1024]{1,0:T(8,128)(2,1)} custom-call(f32[64,1024]{1,0:T(8,128)} %reshape.67.fnum_ref, f32[64,8]{1,0:T(8,128)} %copy.17.fmax_ref, f32[64,8]{1,0:T(8,128)} %copy.18.fden_ref, f32[64,1152]{1,0:T(8,128)} %convert_element_type.20.refs_0_, f32[64,1152]{1,0:T(8,128)} %convert_element_type.21.refs_1_, ...), custom_call_target="tpu_custom_call" | custom-call | tf_op jit(solution)/shard_map/pallas_call | solution.py:230
  (3 shorter events, 0.1 us)
Async XLA Ops:
  30.5 3.0 %copy-start = (bf16[64,1024]{1,0:T(8,128)(2,1)S(1)}, bf16[64,1024]{1,0:T(8,128)(2,1)}, u32[]{:S(2)}) copy-start(bf16[64,1024]{1,0:T(8,128)(2,1)} %q_ref.1) | copy-start | bytes 393220
  30.6 11.7 %collective-permute-start.2 = (f16[64,1152]{1,0:T(8,128)(2,1)S(1)}, f16[64,1152]{1,0:T(8,128)(2,1)S(1)}, u32[]{:S(2)}, u32[]{:S(2)}) collective-permute-start(f16[64,1152]{1,0:T(8,128)(2,1)S(1)} %get-tuple-element.7), channel_id=1, source_target_pairs={{0,3},{1,0},{2,1},{3,2},{4,7},{5,4},{6,5},{7,6},{8,11},{9,8},{10,9... | collective-permute-start | bytes 442376 | tf_op jit(solution)/shard_map/ppermute | solution.py:179
  32.7 11.0 %collective-permute-start.1 = (f16[64,1152]{1,0:T(8,128)(2,1)S(1)}, f16[64,1152]{1,0:T(8,128)(2,1)S(1)}, u32[]{:S(2)}, u32[]{:S(2)}) collective-permute-start(f16[64,1152]{1,0:T(8,128)(2,1)S(1)} %get-tuple-element.8), channel_id=1, source_target_pairs={{0,2},{1,3},{2,0},{3,1},{4,6},{5,7},{6,4},{7,5},{8,10},{9,11},{10,... | collective-permute-start | bytes 442376 | tf_op jit(solution)/shard_map/ppermute | solution.py:179
  32.7 11.7 %collective-permute-start = (f16[64,1152]{1,0:T(8,128)(2,1)S(1)}, f16[64,1152]{1,0:T(8,128)(2,1)S(1)}, u32[]{:S(2)}, u32[]{:S(2)}) collective-permute-start(f16[64,1152]{1,0:T(8,128)(2,1)S(1)} %get-tuple-element.9), channel_id=1, source_target_pairs={{0,1},{1,2},{2,3},{3,0},{4,5},{5,6},{6,7},{7,4},{8,9},{9,10},{10,1... | collective-permute-start | bytes 442376 | tf_op jit(solution)/shard_map/ppermute | solution.py:179
  34.7 0.7 %copy-start.1 = (s32[256]{0:T(256)S(1)}, s32[256]{0:T(256)}, u32[]{:S(2)}) copy-start(s32[256]{0:T(256)} %param.12) | copy-start | bytes 3076

commit v13 on v11

--- a/solution.py
+++ b/solution.py
@@ -61,16 +61,13 @@
         m = maxes[0]
         for tm in maxes[1:]:
             m = jnp.maximum(m, tm)
+        top = jnp.floor(jnp.maximum(m, -60000.0) * 0.25 + 0.5) * 4.0
         numer = jnp.zeros((span, HEAD_DIM), jnp.float32)
         denom = jnp.zeros((span, 1), jnp.float32)
         for tm, nb, db in zip(maxes, numers, denoms):
-            f = jnp.exp(tm - m)
+            f = jnp.exp(tm - top)
             numer = numer + nb * f
             denom = denom + db * f
-        top = jnp.floor(jnp.maximum(m, -60000.0) * 0.25 + 0.5) * 4.0
-        f = jnp.exp(m - top)
-        numer = numer * f
-        denom = denom * f
         mean = numer / jnp.where(denom > 0, denom, 1.0)
         ulp = jnp.exp2(jnp.floor(jnp.log2(jnp.where(denom > 0, denom, 1.0))) - 10.0)
         hi = jnp.where(denom > 0, jnp.round(denom / ulp) * ulp, 0.0)

time: 46.5 us -> 46.5 us (level)
  no operation moved by 1% of the time
where the time goes in v13:
time: 46.5 us; the launch traced here: 46.2 us
  blocking collectives  21.7 us (47%)
  Pallas kernels  9.36 us (20%)
  starting transfers between devices  3.87 us (8%)
  other arithmetic  3.77 us (8%)
  local copies, waits for them, and re-layouts  3.31 us (7%)
  waiting for transfers between devices  2.73 us (6%)
  between operations  0.85 us (2%)
  matrix products  0.61 us (1%)
    all_gather x1, blocking collectives, on_device(): gathered = lax.all_gather(packed, 'seq', axis=0, tiled=True)  21.7 us
    pallas_call x2, Pallas kernels, cache_partials(): pl.pallas_call(functools.partial(cache_kernel, seq_count, first, pieces,...  9.36 us
    ppermute x3, starting transfers between devices, on_device(): lax.ppermute(to_half(piece, qcols, heads_q), 'seq', [(i, (i + shift) % se...  3.87 us
    ppermute x3, waiting for transfers between devices, on_device(): lax.ppermute(to_half(piece, qcols, heads_q), 'seq', [(i, (i + shift) % se...  2.73 us
    another operation x1, other arithmetic  1.22 us
    convert_element_type x1, other arithmetic, on_device(): return attended.astype(jnp.bfloat16)  1.02 us
    slice x1, local copies, waits for them, and re-layouts, on_device(): all_values = gathered[:, qcols + kcols:]  0.99 us
    concatenate x1, other arithmetic, on_device(): packed = jnp.concatenate([new_queries, new_keys, new_values], axis=1)  0.96 us
  transfers between devices with their start and end apart: 3, of which 1 were waited for; matrix products, arithmetic and copies ran while one was open for 6% of the time, Pallas kernels for 7%

profile of v13, /device:TPU:0, one launch (start us, length us, event | category | flops | bytes accessed | tf_op | source)
XLA Modules:
  0.0 46.2 jit_solution(7253177910426186171)
XLA Ops:
  0.7 1.0 %pad_maximum_fusion = bf16[64,1536]{1,0:T(8,128)(2,1)S(1)} fusion(bf16[64,256]{1,0:T(8,128)(2,1)} %param.9, bf16[64,256]{1,0:T(8,128)(2,1)} %param.8, bf16[64,1024]{1,0:T(8,128)(2,1)} %q_ref.1), kind=kLoop, calls=%fused_computation.18 | loop fusion | flops 589824 | bytes 393216 | tf_op jit(solution)/shard_map/concatenate | solution.py:137
  1.6 21.7 %all_gather.3.q_ref = bf16[256,1536]{1,0:T(8,128)(2,1)} all-gather(bf16[64,1536]{1,0:T(8,128)(2,1)S(1)} %pad_maximum_fusion), channel_id=1, replica_groups=mesh['group'=2,'head'=4,'seq'=4] {'seq'}, dimensions={0}, use_global_device_ids=true | all-gather | bytes 983040 | tf_op jit(solution)/shard_map/all_gather | solution.py:138
  23.3 5.9 %shard_map.73.rest_0_ = f32[192,1152]{1,0:T(8,128)} custom-call(s32[1]{0:T(128)S(6)} %copy.57.len_ref, bf16[256,1536]{1,0:T(8,128)(2,1)} %all_gather.3.q_ref, bf16[1024,256]{1,0:T(8,128)(2,1)} %k_ref.3, bf16[1024,256]{1,0:T(8,128)(2,1)} %v_ref.3), custom_call_target="tpu_custom_call" | custom-call | flops 805306368 | bytes 2523136 | tf_op jit(solution)/shard_map/pallas_call | solution.py:107
  29.3 1.2 %convert.5 = f16[192,1152]{1,0:T(8,128)(2,1)S(1)} convert(f32[192,1152]{1,0:T(8,128)} %shard_map.73.rest_0_) | non-fusion elementwise | flops 221184 | bytes 1327104 | tf_op jit(solution)/shard_map/convert.2
  30.5 0.0 copy-start.1
  30.5 0.1 fusion.20
  30.6 0.1 collective-permute-start
  30.7 3.8 %collective-permute-start.2 = (f16[64,1152]{1,0:T(8,128)(2,1)S(1)}, f16[64,1152]{1,0:T(8,128)(2,1)S(1)}, u32[]{:S(2)}, u32[]{:S(2)}) collective-permute-start(f16[64,1152]{1,0:T(8,128)(2,1)S(1)} %get-tuple-element.15), channel_id=1, source_target_pairs={{0,3},{1,0},{2,1},{3,2},{4,7},{5,4},{6,5},{7,6},{8,11},{9,8},{10,9... | collective-permute-start | bytes 442376 | tf_op jit(solution)/shard_map/ppermute | solution.py:152
  34.5 0.0 collective-permute-start.1
  34.5 0.0 copy-done.1
  34.5 0.1 reshape.94
  34.5 1.0 %fusion.19 = (bf16[256,256]{1,0:T(8,128)(2,1)S(1)}, bf16[256,256]{1,0:T(8,128)(2,1)S(1)}) fusion(bf16[256,1536]{1,0:T(8,128)(2,1)} %all_gather.3.q_ref), kind=kLoop, calls=%fused_computation.39 | loop fusion | bytes 524288 | tf_op jit(solution)/shard_map/slice | solution.py:140
  35.6 0.0 copy-start.2
  35.6 0.7 %copy-done.2 = s32[256]{0:T(256)S(1)} copy-done((s32[256]{0:T(256)S(1)}, s32[256]{0:T(256)}, u32[]{:S(2)}) %copy-start.2) | copy-done | bytes 1048
  36.3 0.1 dynamic_slice.3
  36.4 0.1 fusion.9
  36.5 0.3 select_reduce_fusion
  36.8 0.3 convolution_bitcast_fusion
  37.1 0.2 copy.23
  37.3 0.1 reshape.95
  37.4 0.3 convert_reduce_fusion
  37.7 0.1 copy.26
  37.8 0.1 copy.25
  37.8 3.4 %shard_map.74 = f32[64,1152]{1,0:T(8,128)} custom-call(s32[1]{0:T(128)S(6)} %copy.57.len_ref, bf16[64,1024]{1,0:T(8,128)(2,1)} %q_ref.1, bf16[1024,256]{1,0:T(8,128)(2,1)} %k_ref.3, bf16[1024,256]{1,0:T(8,128)(2,1)} %v_ref.3, f32[192,1152]{1,0:T(8,128)} %shard_map.73.rest_0_), custom_call_target="tpu_custom_call" | custom-call | flops 268435456 | bytes 1474560 | tf_op jit(solution)/shard_map/pallas_call | solution.py:107
  41.3 0.0 collective-permute-done
  41.3 0.0 collective-permute-done.2
  41.3 0.0 copy-start
  41.3 2.7 %collective-permute-done.1 = f16[64,1152]{1,0:T(8,128)(2,1)S(1)} collective-permute-done((f16[64,1152]{1,0:T(8,128)(2,1)S(1)}, f16[64,1152]{1,0:T(8,128)(2,1)S(1)}, u32[]{:S(2)}, u32[]{:S(2)}) %collective-permute-start.1) | collective-permute-done | bytes 147488 | tf_op jit(solution)/shard_map/ppermute | solution.py:152
  44.1 0.0 copy-done
  44.1 0.1 add_add_fusion
  44.3 0.1 broadcast_in_dim.38
  44.4 0.1 broadcast_in_dim.32
  44.5 0.1 broadcast_in_dim.33
  44.6 0.1 broadcast_in_dim.34
  44.8 0.1 broadcast_in_dim.35
  44.9 0.1 broadcast_in_dim.36
  45.1 0.1 broadcast_in_dim.37
  45.2 1.0 %fusion.1 = bf16[64,1024]{1,0:T(8,128)(2,1)} fusion(f32[8,8,8,128]{3,2,1,0:T(8,128)S(1)} %bitcast.51, f32[8,8,8,128]{3,2,1,0:T(8,128)S(1)} %bitcast.57, f32[8,8,8,128]{3,2,1,0:T(8,128)S(1)} %bitcast.56, f32[8,8,8,128]{3,2,1,0:T(8,128)S(1)} %bitcast.55, f32[8,8,8,128]{3,2,1,0:T(8,128)S(1)} %bitcast.54, f32[8,8,8,128]{3,2,1,0:T(8,128)S(1)} %bitcast.53, ...), kind=kLoop, calls=%fused_computation.7 | loop fusion | flops 786432 | bytes 3276800 | tf_op jit(solution)/shard_map/convert_element_type | solution.py:232
  (6 shorter events, 0.1 us)
Async XLA Ops:
  30.5 4.0 %copy-start.1 = (bf16[64,1024]{1,0:T(8,128)(2,1)S(1)}, bf16[64,1024]{1,0:T(8,128)(2,1)}, u32[]{:S(2)}) copy-start(bf16[64,1024]{1,0:T(8,128)(2,1)} %q_ref.1) | copy-start | bytes 393220
  30.6 10.7 %collective-permute-start = (f16[64,1152]{1,0:T(8,128)(2,1)S(1)}, f16[64,1152]{1,0:T(8,128)(2,1)S(1)}, u32[]{:S(2)}, u32[]{:S(2)}) collective-permute-start(f16[64,1152]{1,0:T(8,128)(2,1)S(1)} %get-tuple-element.14), channel_id=1, source_target_pairs={{0,1},{1,2},{2,3},{3,0},{4,5},{5,6},{6,7},{7,4},{8,9},{9,10},{10,1... | collective-permute-start | bytes 442376 | tf_op jit(solution)/shard_map/ppermute | solution.py:152
  30.7 10.6 %collective-permute-start.2 = (f16[64,1152]{1,0:T(8,128)(2,1)S(1)}, f16[64,1152]{1,0:T(8,128)(2,1)S(1)}, u32[]{:S(2)}, u32[]{:S(2)}) collective-permute-start(f16[64,1152]{1,0:T(8,128)(2,1)S(1)} %get-tuple-element.15), channel_id=1, source_target_pairs={{0,3},{1,0},{2,1},{3,2},{4,7},{5,4},{6,5},{7,6},{8,11},{9,8},{10,9... | collective-permute-start | bytes 442376 | tf_op jit(solution)/shard_map/ppermute | solution.py:152
  34.5 9.6 %collective-permute-start.1 = (f16[64,1152]{1,0:T(8,128)(2,1)S(1)}, f16[64,1152]{1,0:T(8,128)(2,1)S(1)}, u32[]{:S(2)}, u32[]{:S(2)}) collective-permute-start(f16[64,1152]{1,0:T(8,128)(2,1)S(1)} %get-tuple-element.16), channel_id=1, source_target_pairs={{0,2},{1,3},{2,0},{3,1},{4,6},{5,7},{6,4},{7,5},{8,10},{9,11},{10,... | collective-permute-start | bytes 442376 | tf_op jit(solution)/shard_map/ppermute | solution.py:152
  35.6 0.7 %copy-start.2 = (s32[256]{0:T(256)S(1)}, s32[256]{0:T(256)}, u32[]{:S(2)}) copy-start(s32[256]{0:T(256)} %param.12) | copy-start | bytes 3076
  41.3 2.8 %copy-start = (f32[64,1152]{1,0:T(8,128)S(1)}, f32[64,1152]{1,0:T(8,128)}, u32[]{:S(2)}) copy-start(f32[64,1152]{1,0:T(8,128)} %shard_map.74) | copy-start | bytes 884740

commit v14 on v13

--- a/solution.py
+++ b/solution.py
@@ -10,6 +10,8 @@
 HEAD_DIM = 128
 SUB = 256
 NEG_FILL = -1e30
+LOG2E = 1.4426950408889634
+LN2 = 0.6931471805599453
 
 
 def cache_kernel(seq_count, first, pieces, stack, len_ref, q_ref, k_ref, v_ref, *rest):
@@ -22,7 +24,7 @@
     heads_kv = k_ref.shape[1] // HEAD_DIM
     group = heads_q // heads_kv
     tiles = cache_rows // SUB
-    scale = HEAD_DIM ** (-0.5)
+    scale2 = HEAD_DIM ** (-0.5) * LOG2E
     lane = lax.broadcasted_iota(jnp.int32, (rows, 128), 1)
     position = lax.broadcasted_iota(jnp.int32, (1, cache_rows), 1)
     extra = jnp.zeros((rows, 128), jnp.float32)
@@ -51,9 +53,10 @@
         for b in range(tiles):
             kb = keys_t[g][:, b * SUB:(b + 1) * SUB]
             bias = jnp.where(position[:, b * SUB:(b + 1) * SUB] < live, 0.0, NEG_FILL)
-            s = jnp.dot(qx, kb, preferred_element_type=jnp.float32) * scale + bias
-            tm = jnp.max(s, axis=1, keepdims=True)
-            w = jnp.exp(s - tm).astype(jnp.bfloat16)
+            s2 = jnp.dot(qx, kb, preferred_element_type=jnp.float32) * scale2 + bias
+            tm2 = jnp.max(s2, axis=1, keepdims=True)
+            w = jnp.exp2(s2 - tm2).astype(jnp.bfloat16)
+            tm = tm2 * LN2
             vb = v_ref[b * SUB:(b + 1) * SUB, g * HEAD_DIM:(g + 1) * HEAD_DIM]
             numers.append(jnp.dot(w, vb, preferred_element_type=jnp.float32))
             denoms.append(jnp.sum(w.astype(jnp.float32), axis=1, keepdims=True))

time: 46.5 us -> 46.6 us (level)
  no operation moved by 1% of the time
where the time goes in v14:
time: 46.6 us; the launch traced here: 46.3 us
  blocking collectives  21.7 us (47%)
  Pallas kernels  9.5 us (20%)
  starting transfers between devices  3.87 us (8%)
  other arithmetic  3.77 us (8%)
  local copies, waits for them, and re-layouts  3.31 us (7%)
  waiting for transfers between devices  2.67 us (6%)
  between operations  0.85 us (2%)
  matrix products  0.61 us (1%)
    all_gather x1, blocking collectives, on_device(): gathered = lax.all_gather(packed, 'seq', axis=0, tiled=True)  21.7 us
    pallas_call x2, Pallas kernels, cache_partials(): pl.pallas_call(functools.partial(cache_kernel, seq_count, first, pieces,...  9.5 us
    ppermute x3, starting transfers between devices, on_device(): lax.ppermute(to_half(piece, qcols, heads_q), 'seq', [(i, (i + shift) % se...  3.87 us
    ppermute x3, waiting for transfers between devices, on_device(): lax.ppermute(to_half(piece, qcols, heads_q), 'seq', [(i, (i + shift) % se...  2.67 us
    another operation x1, other arithmetic  1.22 us
    convert_element_type x1, other arithmetic, on_device(): return attended.astype(jnp.bfloat16)  1.02 us
    slice x1, local copies, waits for them, and re-layouts, on_device(): all_values = gathered[:, qcols + kcols:]  0.99 us
    concatenate x1, other arithmetic, on_device(): packed = jnp.concatenate([new_queries, new_keys, new_values], axis=1)  0.96 us
  transfers between devices with their start and end apart: 3, of which 1 were waited for; matrix products, arithmetic and copies ran while one was open for 6% of the time, Pallas kernels for 7%

profile of v14, /device:TPU:0, one launch (start us, length us, event | category | flops | bytes accessed | tf_op | source)
XLA Modules:
  0.0 46.3 jit_solution(12819634083010114152)
XLA Ops:
  0.7 1.0 %pad_maximum_fusion = bf16[64,1536]{1,0:T(8,128)(2,1)S(1)} fusion(bf16[64,256]{1,0:T(8,128)(2,1)} %param.9, bf16[64,256]{1,0:T(8,128)(2,1)} %param.8, bf16[64,1024]{1,0:T(8,128)(2,1)} %q_ref.1), kind=kLoop, calls=%fused_computation.18 | loop fusion | flops 589824 | bytes 393216 | tf_op jit(solution)/shard_map/concatenate | solution.py:140
  1.6 21.7 %all_gather.3.q_ref = bf16[256,1536]{1,0:T(8,128)(2,1)} all-gather(bf16[64,1536]{1,0:T(8,128)(2,1)S(1)} %pad_maximum_fusion), channel_id=1, replica_groups=mesh['group'=2,'head'=4,'seq'=4] {'seq'}, dimensions={0}, use_global_device_ids=true | all-gather | bytes 983040 | tf_op jit(solution)/shard_map/all_gather | solution.py:141
  23.3 6.0 %shard_map.73.rest_0_ = f32[192,1152]{1,0:T(8,128)} custom-call(s32[1]{0:T(128)S(6)} %copy.57.len_ref, bf16[256,1536]{1,0:T(8,128)(2,1)} %all_gather.3.q_ref, bf16[1024,256]{1,0:T(8,128)(2,1)} %k_ref.3, bf16[1024,256]{1,0:T(8,128)(2,1)} %v_ref.3), custom_call_target="tpu_custom_call" | custom-call | flops 805306368 | bytes 2523136 | tf_op jit(solution)/shard_map/pallas_call | solution.py:110
  29.4 1.2 %convert.5 = f16[192,1152]{1,0:T(8,128)(2,1)S(1)} convert(f32[192,1152]{1,0:T(8,128)} %shard_map.73.rest_0_) | non-fusion elementwise | flops 221184 | bytes 1327104 | tf_op jit(solution)/shard_map/convert.2
  30.6 0.0 copy-start.1
  30.6 0.1 fusion.20
  30.7 0.1 collective-permute-start
  30.7 3.8 %collective-permute-start.2 = (f16[64,1152]{1,0:T(8,128)(2,1)S(1)}, f16[64,1152]{1,0:T(8,128)(2,1)S(1)}, u32[]{:S(2)}, u32[]{:S(2)}) collective-permute-start(f16[64,1152]{1,0:T(8,128)(2,1)S(1)} %get-tuple-element.15), channel_id=1, source_target_pairs={{0,3},{1,0},{2,1},{3,2},{4,7},{5,4},{6,5},{7,6},{8,11},{9,8},{10,9... | collective-permute-start | bytes 442376 | tf_op jit(solution)/shard_map/ppermute | solution.py:155
  34.6 0.0 collective-permute-start.1
  34.6 0.0 copy-done.1
  34.6 0.1 reshape.94
  34.6 1.0 %fusion.19 = (bf16[256,256]{1,0:T(8,128)(2,1)S(1)}, bf16[256,256]{1,0:T(8,128)(2,1)S(1)}) fusion(bf16[256,1536]{1,0:T(8,128)(2,1)} %all_gather.3.q_ref), kind=kLoop, calls=%fused_computation.39 | loop fusion | bytes 524288 | tf_op jit(solution)/shard_map/slice | solution.py:143
  35.7 0.0 copy-start.2
  35.7 0.7 %copy-done.2 = s32[256]{0:T(256)S(1)} copy-done((s32[256]{0:T(256)S(1)}, s32[256]{0:T(256)}, u32[]{:S(2)}) %copy-start.2) | copy-done | bytes 1048
  36.4 0.1 dynamic_slice.3
  36.5 0.1 fusion.9
  36.6 0.3 select_reduce_fusion
  36.9 0.3 convolution_bitcast_fusion
  37.2 0.2 copy.23
  37.4 0.1 reshape.95
  37.5 0.3 convert_reduce_fusion
  37.8 0.1 copy.26
  37.9 0.1 copy.25
  37.9 3.5 %shard_map.74 = f32[64,1152]{1,0:T(8,128)} custom-call(s32[1]{0:T(128)S(6)} %copy.57.len_ref, bf16[64,1024]{1,0:T(8,128)(2,1)} %q_ref.1, bf16[1024,256]{1,0:T(8,128)(2,1)} %k_ref.3, bf16[1024,256]{1,0:T(8,128)(2,1)} %v_ref.3, f32[192,1152]{1,0:T(8,128)} %shard_map.73.rest_0_), custom_call_target="tpu_custom_call" | custom-call | flops 268435456 | bytes 1474560 | tf_op jit(solution)/shard_map/pallas_call | solution.py:110
  41.4 0.0 collective-permute-done
  41.4 0.0 collective-permute-done.2
  41.5 0.0 copy-start
  41.5 2.7 %collective-permute-done.1 = f16[64,1152]{1,0:T(8,128)(2,1)S(1)} collective-permute-done((f16[64,1152]{1,0:T(8,128)(2,1)S(1)}, f16[64,1152]{1,0:T(8,128)(2,1)S(1)}, u32[]{:S(2)}, u32[]{:S(2)}) %collective-permute-start.1) | collective-permute-done | bytes 147488 | tf_op jit(solution)/shard_map/ppermute | solution.py:155
  44.2 0.0 copy-done
  44.2 0.1 add_add_fusion
  44.3 0.1 broadcast_in_dim.38
  44.5 0.1 broadcast_in_dim.32
  44.6 0.1 broadcast_in_dim.33
  44.7 0.1 broadcast_in_dim.34
  44.9 0.1 broadcast_in_dim.35
  45.0 0.1 broadcast_in_dim.36
  45.1 0.1 broadcast_in_dim.37
  45.3 1.0 %fusion.1 = bf16[64,1024]{1,0:T(8,128)(2,1)} fusion(f32[8,8,8,128]{3,2,1,0:T(8,128)S(1)} %bitcast.51, f32[8,8,8,128]{3,2,1,0:T(8,128)S(1)} %bitcast.57, f32[8,8,8,128]{3,2,1,0:T(8,128)S(1)} %bitcast.56, f32[8,8,8,128]{3,2,1,0:T(8,128)S(1)} %bitcast.55, f32[8,8,8,128]{3,2,1,0:T(8,128)S(1)} %bitcast.54, f32[8,8,8,128]{3,2,1,0:T(8,128)S(1)} %bitcast.53, ...), kind=kLoop, calls=%fused_computation.7 | loop fusion | flops 786432 | bytes 3276800 | tf_op jit(solution)/shard_map/convert_element_type | solution.py:235
  (6 shorter events, 0.1 us)
Async XLA Ops:
  30.6 4.0 %copy-start.1 = (bf16[64,1024]{1,0:T(8,128)(2,1)S(1)}, bf16[64,1024]{1,0:T(8,128)(2,1)}, u32[]{:S(2)}) copy-start(bf16[64,1024]{1,0:T(8,128)(2,1)} %q_ref.1) | copy-start | bytes 393220
  30.7 10.7 %collective-permute-start = (f16[64,1152]{1,0:T(8,128)(2,1)S(1)}, f16[64,1152]{1,0:T(8,128)(2,1)S(1)}, u32[]{:S(2)}, u32[]{:S(2)}) collective-permute-start(f16[64,1152]{1,0:T(8,128)(2,1)S(1)} %get-tuple-element.14), channel_id=1, source_target_pairs={{0,1},{1,2},{2,3},{3,0},{4,5},{5,6},{6,7},{7,4},{8,9},{9,10},{10,1... | collective-permute-start | bytes 442376 | tf_op jit(solution)/shard_map/ppermute | solution.py:155
  30.7 10.7 %collective-permute-start.2 = (f16[64,1152]{1,0:T(8,128)(2,1)S(1)}, f16[64,1152]{1,0:T(8,128)(2,1)S(1)}, u32[]{:S(2)}, u32[]{:S(2)}) collective-permute-start(f16[64,1152]{1,0:T(8,128)(2,1)S(1)} %get-tuple-element.15), channel_id=1, source_target_pairs={{0,3},{1,0},{2,1},{3,2},{4,7},{5,4},{6,5},{7,6},{8,11},{9,8},{10,9... | collective-permute-start | bytes 442376 | tf_op jit(solution)/shard_map/ppermute | solution.py:155
  34.6 9.6 %collective-permute-start.1 = (f16[64,1152]{1,0:T(8,128)(2,1)S(1)}, f16[64,1152]{1,0:T(8,128)(2,1)S(1)}, u32[]{:S(2)}, u32[]{:S(2)}) collective-permute-start(f16[64,1152]{1,0:T(8,128)(2,1)S(1)} %get-tuple-element.16), channel_id=1, source_target_pairs={{0,2},{1,3},{2,0},{3,1},{4,6},{5,7},{6,4},{7,5},{8,10},{9,11},{10,... | collective-permute-start | bytes 442376 | tf_op jit(solution)/shard_map/ppermute | solution.py:155
  35.7 0.7 %copy-start.2 = (s32[256]{0:T(256)S(1)}, s32[256]{0:T(256)}, u32[]{:S(2)}) copy-start(s32[256]{0:T(256)} %param.12) | copy-start | bytes 3076
  41.5 2.7 %copy-start = (f32[64,1152]{1,0:T(8,128)S(1)}, f32[64,1152]{1,0:T(8,128)}, u32[]{:S(2)}) copy-start(f32[64,1152]{1,0:T(8,128)} %shard_map.74) | copy-start | bytes 884740

commit v15 on v13

--- a/solution.py
+++ b/solution.py
@@ -91,9 +91,9 @@
     out_cols = qcols + 128
     heads_q = qcols // HEAD_DIM
     if pieces > 0 or block == qrows:
-        q_spec = pl.BlockSpec((qrows, qcols_in), lambda i: (0, 0))
+        q_spec = pl.BlockSpec((qrows, qcols), lambda i: (0, 0))
     else:
-        q_spec = pl.BlockSpec((block, qcols_in), lambda i: (i, 0))
+        q_spec = pl.BlockSpec((block, qcols), lambda i: (i, 0))
     in_specs = [
         pl.BlockSpec(memory_space=pltpu.SMEM),
         q_spec,
@@ -113,7 +113,7 @@
         cost_estimate=pl.CostEstimate(
             flops=4 * rows * cache_rows * qcols,
             transcendentals=rows * cache_rows * heads_q,
-            bytes_accessed=2 * (rows * qcols_in + 2 * cache_rows * kcols) + 4 * rows * out_cols,
+            bytes_accessed=2 * (rows * qcols + 2 * cache_rows * kcols) + 4 * rows * out_cols,
         ),
     )(*operands)
 

time: 46.5 us -> 46.4 us (level)
  no operation moved by 1% of the time
where the time goes in v15:
time: 46.4 us; the launch traced here: 46.1 us
  blocking collectives  21.7 us (47%)
  Pallas kernels  9.28 us (20%)
  starting transfers between devices  3.87 us (8%)
  other arithmetic  3.77 us (8%)
  local copies, waits for them, and re-layouts  3.31 us (7%)
  waiting for transfers between devices  2.73 us (6%)
  between operations  0.85 us (2%)
  matrix products  0.61 us (1%)
    all_gather x1, blocking collectives, on_device(): gathered = lax.all_gather(packed, 'seq', axis=0, tiled=True)  21.7 us
    pallas_call x2, Pallas kernels, cache_partials(): pl.pallas_call(functools.partial(cache_kernel, seq_count, first, pieces,...  9.28 us
    ppermute x3, starting transfers between devices, on_device(): lax.ppermute(to_half(piece, qcols, heads_q), 'seq', [(i, (i + shift) % se...  3.87 us
    ppermute x3, waiting for transfers between devices, on_device(): lax.ppermute(to_half(piece, qcols, heads_q), 'seq', [(i, (i + shift) % se...  2.73 us
    another operation x1, other arithmetic  1.22 us
    convert_element_type x1, other arithmetic, on_device(): return attended.astype(jnp.bfloat16)  1.02 us
    slice x1, local copies, waits for them, and re-layouts, on_device(): all_values = gathered[:, qcols + kcols:]  0.99 us
    concatenate x1, other arithmetic, on_device(): packed = jnp.concatenate([new_queries, new_keys, new_values], axis=1)  0.96 us
  transfers between devices with their start and end apart: 3, of which 1 were waited for; matrix products, arithmetic and copies ran while one was open for 6% of the time, Pallas kernels for 7%

profile of v15, /device:TPU:0, one launch (start us, length us, event | category | flops | bytes accessed | tf_op | source)
XLA Modules:
  0.0 46.1 jit_solution(5439915859041327124)
XLA Ops:
  0.7 1.0 %pad_maximum_fusion = bf16[64,1536]{1,0:T(8,128)(2,1)S(1)} fusion(bf16[64,256]{1,0:T(8,128)(2,1)} %param.9, bf16[64,256]{1,0:T(8,128)(2,1)} %param.8, bf16[64,1024]{1,0:T(8,128)(2,1)} %q_ref.1), kind=kLoop, calls=%fused_computation.18 | loop fusion | flops 589824 | bytes 393216 | tf_op jit(solution)/shard_map/concatenate | solution.py:137
  1.6 21.7 %all_gather.3.q_ref = bf16[256,1536]{1,0:T(8,128)(2,1)} all-gather(bf16[64,1536]{1,0:T(8,128)(2,1)S(1)} %pad_maximum_fusion), channel_id=1, replica_groups=mesh['group'=2,'head'=4,'seq'=4] {'seq'}, dimensions={0}, use_global_device_ids=true | all-gather | bytes 983040 | tf_op jit(solution)/shard_map/all_gather | solution.py:138
  23.3 5.9 %shard_map.73.rest_0_ = f32[192,1152]{1,0:T(8,128)} custom-call(s32[1]{0:T(128)S(6)} %copy.57.len_ref, bf16[256,1536]{1,0:T(8,128)(2,1)} %all_gather.3.q_ref, bf16[1024,256]{1,0:T(8,128)(2,1)} %k_ref.3, bf16[1024,256]{1,0:T(8,128)(2,1)} %v_ref.3), custom_call_target="tpu_custom_call" | custom-call | flops 805306368 | bytes 2326528 | tf_op jit(solution)/shard_map/pallas_call | solution.py:107
  29.2 1.2 %convert.5 = f16[192,1152]{1,0:T(8,128)(2,1)S(1)} convert(f32[192,1152]{1,0:T(8,128)} %shard_map.73.rest_0_) | non-fusion elementwise | flops 221184 | bytes 1327104 | tf_op jit(solution)/shard_map/convert.2
  30.4 0.0 copy-start.1
  30.4 0.1 fusion.20
  30.5 0.1 collective-permute-start
  30.6 3.8 %collective-permute-start.2 = (f16[64,1152]{1,0:T(8,128)(2,1)S(1)}, f16[64,1152]{1,0:T(8,128)(2,1)S(1)}, u32[]{:S(2)}, u32[]{:S(2)}) collective-permute-start(f16[64,1152]{1,0:T(8,128)(2,1)S(1)} %get-tuple-element.15), channel_id=1, source_target_pairs={{0,3},{1,0},{2,1},{3,2},{4,7},{5,4},{6,5},{7,6},{8,11},{9,8},{10,9... | collective-permute-start | bytes 442376 | tf_op jit(solution)/shard_map/ppermute | solution.py:152
  34.4 0.0 collective-permute-start.1
  34.4 0.0 copy-done.1
  34.4 0.1 reshape.94
  34.5 1.0 %fusion.19 = (bf16[256,256]{1,0:T(8,128)(2,1)S(1)}, bf16[256,256]{1,0:T(8,128)(2,1)S(1)}) fusion(bf16[256,1536]{1,0:T(8,128)(2,1)} %all_gather.3.q_ref), kind=kLoop, calls=%fused_computation.39 | loop fusion | bytes 524288 | tf_op jit(solution)/shard_map/slice | solution.py:140
  35.6 0.0 copy-start.2
  35.6 0.7 %copy-done.2 = s32[256]{0:T(256)S(1)} copy-done((s32[256]{0:T(256)S(1)}, s32[256]{0:T(256)}, u32[]{:S(2)}) %copy-start.2) | copy-done | bytes 1048
  36.2 0.1 dynamic_slice.3
  36.3 0.1 fusion.9
  36.4 0.3 select_reduce_fusion
  36.7 0.3 convolution_bitcast_fusion
  37.0 0.2 copy.23
  37.2 0.1 reshape.95
  37.3 0.3 convert_reduce_fusion
  37.6 0.1 copy.26
  37.7 0.1 copy.25
  37.8 3.4 %shard_map.74 = f32[64,1152]{1,0:T(8,128)} custom-call(s32[1]{0:T(128)S(6)} %copy.57.len_ref, bf16[64,1024]{1,0:T(8,128)(2,1)} %q_ref.1, bf16[1024,256]{1,0:T(8,128)(2,1)} %k_ref.3, bf16[1024,256]{1,0:T(8,128)(2,1)} %v_ref.3, f32[192,1152]{1,0:T(8,128)} %shard_map.73.rest_0_), custom_call_target="tpu_custom_call" | custom-call | flops 268435456 | bytes 1474560 | tf_op jit(solution)/shard_map/pallas_call | solution.py:107
  41.2 0.0 collective-permute-done
  41.2 0.0 collective-permute-done.2
  41.3 0.0 copy-start
  41.3 2.7 %collective-permute-done.1 = f16[64,1152]{1,0:T(8,128)(2,1)S(1)} collective-permute-done((f16[64,1152]{1,0:T(8,128)(2,1)S(1)}, f16[64,1152]{1,0:T(8,128)(2,1)S(1)}, u32[]{:S(2)}, u32[]{:S(2)}) %collective-permute-start.1) | collective-permute-done | bytes 147488 | tf_op jit(solution)/shard_map/ppermute | solution.py:152
  44.0 0.0 copy-done
  44.0 0.1 add_add_fusion
  44.2 0.1 broadcast_in_dim.38
  44.3 0.1 broadcast_in_dim.32
  44.4 0.1 broadcast_in_dim.33
  44.6 0.1 broadcast_in_dim.34
  44.7 0.1 broadcast_in_dim.35
  44.8 0.1 broadcast_in_dim.36
  45.0 0.1 broadcast_in_dim.37
  45.1 1.0 %fusion.1 = bf16[64,1024]{1,0:T(8,128)(2,1)} fusion(f32[8,8,8,128]{3,2,1,0:T(8,128)S(1)} %bitcast.51, f32[8,8,8,128]{3,2,1,0:T(8,128)S(1)} %bitcast.57, f32[8,8,8,128]{3,2,1,0:T(8,128)S(1)} %bitcast.56, f32[8,8,8,128]{3,2,1,0:T(8,128)S(1)} %bitcast.55, f32[8,8,8,128]{3,2,1,0:T(8,128)S(1)} %bitcast.54, f32[8,8,8,128]{3,2,1,0:T(8,128)S(1)} %bitcast.53, ...), kind=kLoop, calls=%fused_computation.7 | loop fusion | flops 786432 | bytes 3276800 | tf_op jit(solution)/shard_map/convert_element_type | solution.py:232
  (6 shorter events, 0.1 us)
Async XLA Ops:
  30.4 4.0 %copy-start.1 = (bf16[64,1024]{1,0:T(8,128)(2,1)S(1)}, bf16[64,1024]{1,0:T(8,128)(2,1)}, u32[]{:S(2)}) copy-start(bf16[64,1024]{1,0:T(8,128)(2,1)} %q_ref.1) | copy-start | bytes 393220
  30.5 10.7 %collective-permute-start = (f16[64,1152]{1,0:T(8,128)(2,1)S(1)}, f16[64,1152]{1,0:T(8,128)(2,1)S(1)}, u32[]{:S(2)}, u32[]{:S(2)}) collective-permute-start(f16[64,1152]{1,0:T(8,128)(2,1)S(1)} %get-tuple-element.14), channel_id=1, source_target_pairs={{0,1},{1,2},{2,3},{3,0},{4,5},{5,6},{6,7},{7,4},{8,9},{9,10},{10,1... | collective-permute-start | bytes 442376 | tf_op jit(solution)/shard_map/ppermute | solution.py:152
  30.6 10.6 %collective-permute-start.2 = (f16[64,1152]{1,0:T(8,128)(2,1)S(1)}, f16[64,1152]{1,0:T(8,128)(2,1)S(1)}, u32[]{:S(2)}, u32[]{:S(2)}) collective-permute-start(f16[64,1152]{1,0:T(8,128)(2,1)S(1)} %get-tuple-element.15), channel_id=1, source_target_pairs={{0,3},{1,0},{2,1},{3,2},{4,7},{5,4},{6,5},{7,6},{8,11},{9,8},{10,9... | collective-permute-start | bytes 442376 | tf_op jit(solution)/shard_map/ppermute | solution.py:152
  34.4 9.6 %collective-permute-start.1 = (f16[64,1152]{1,0:T(8,128)(2,1)S(1)}, f16[64,1152]{1,0:T(8,128)(2,1)S(1)}, u32[]{:S(2)}, u32[]{:S(2)}) collective-permute-start(f16[64,1152]{1,0:T(8,128)(2,1)S(1)} %get-tuple-element.16), channel_id=1, source_target_pairs={{0,2},{1,3},{2,0},{3,1},{4,6},{5,7},{6,4},{7,5},{8,10},{9,11},{10,... | collective-permute-start | bytes 442376 | tf_op jit(solution)/shard_map/ppermute | solution.py:152
  35.6 0.7 %copy-start.2 = (s32[256]{0:T(256)S(1)}, s32[256]{0:T(256)}, u32[]{:S(2)}) copy-start(s32[256]{0:T(256)} %param.12) | copy-start | bytes 3076
  41.3 2.8 %copy-start = (f32[64,1152]{1,0:T(8,128)S(1)}, f32[64,1152]{1,0:T(8,128)}, u32[]{:S(2)}) copy-start(f32[64,1152]{1,0:T(8,128)} %shard_map.74) | copy-start | bytes 884740

commit v16 on v15

--- a/solution.py
+++ b/solution.py
@@ -12,7 +12,7 @@
 NEG_FILL = -1e30
 
 
-def cache_kernel(seq_count, first, pieces, stack, len_ref, q_ref, k_ref, v_ref, *rest):
+def cache_kernel(seq_count, shifts, stack, len_ref, q_ref, k_ref, v_ref, *rest):
     out_ref = rest[-1]
     rank = lax.axis_index("seq")
     cache_rows = k_ref.shape[0]
@@ -29,12 +29,13 @@
 
     def query_rows(h):
         cols = slice(h * HEAD_DIM, (h + 1) * HEAD_DIM)
+        pieces = len(shifts)
         if pieces == 0:
             return q_ref[:, cols]
         piece = rows // pieces
         blocks = []
-        for p in range(pieces):
-            index = lax.rem(rank + first + p, seq_count)
+        for shift in shifts:
+            index = lax.rem(rank + shift, seq_count)
             blocks.append(q_ref[pl.ds(pl.multiple_of(index * piece, piece), piece), cols])
         return jnp.concatenate(blocks, axis=0)
 
@@ -84,13 +85,13 @@
     return part.astype(jnp.float16)
 
 
-def cache_partials(cache_length, queries, keys, values, qcols, rows, block, first, pieces,
+def cache_partials(cache_length, queries, keys, values, qcols, rows, block, shifts,
                    stack, seq_count, after=None):
     qrows, qcols_in = queries.shape
     cache_rows, kcols = keys.shape
     out_cols = qcols + 128
     heads_q = qcols // HEAD_DIM
-    if pieces > 0 or block == qrows:
+    if shifts or block == qrows:
         q_spec = pl.BlockSpec((qrows, qcols), lambda i: (0, 0))
     else:
         q_spec = pl.BlockSpec((block, qcols), lambda i: (i, 0))
@@ -105,7 +106,7 @@
         in_specs.append(pl.BlockSpec(memory_space=pl.ANY))
         operands.append(after)
     return pl.pallas_call(
-        functools.partial(cache_kernel, seq_count, first, pieces, stack),
+        functools.partial(cache_kernel, seq_count, shifts, stack),
         grid=(rows // block,),
         in_specs=in_specs,
         out_specs=pl.BlockSpec((block, out_cols), lambda i: (i, 0)),
@@ -140,30 +141,41 @@
     all_values = gathered[:, qcols + kcols:]
 
     if seq_count <= 8:
-        remote = cache_partials(
+        lead = seq_count // 2
+        rest_shifts = tuple(s for s in range(1, seq_count) if s != lead)
+        pairs = lambda s: [(i, (i + s) % seq_count) for i in range(seq_count)]
+        first_part = cache_partials(
             cache_length, gathered, cache_keys, cache_values, qcols,
-            (seq_count - 1) * own_count, (seq_count - 1) * own_count, 1, seq_count - 1, 1,
-            seq_count,
-        )
-        parts = []
-        for shift in range(1, seq_count):
-            piece = remote[(shift - 1) * own_count:shift * own_count]
-            parts.append(
-                lax.ppermute(
-                    to_half(piece, qcols, heads_q),
-                    "seq",
-                    [(i, (i + shift) % seq_count) for i in range(seq_count)],
-                ).astype(jnp.float32)
+            own_count, own_count, (lead,), group_size, seq_count,
+        )
+        parts = [
+            lax.ppermute(to_half(first_part, qcols, heads_q), "seq", pairs(lead)).astype(jnp.float32)
+        ]
+        if rest_shifts:
+            rest = cache_partials(
+                cache_length, gathered, cache_keys, cache_values, qcols,
+                len(rest_shifts) * own_count, len(rest_shifts) * own_count, rest_shifts, 1,
+                seq_count, after=first_part,
             )
+            for k, shift in enumerate(rest_shifts):
+                piece = rest[k * own_count:(k + 1) * own_count]
+                parts.append(
+                    lax.ppermute(to_half(piece, qcols, heads_q), "seq", pairs(shift)).astype(
+                        jnp.float32
+                    )
+                )
+            remote = rest
+        else:
+            remote = first_part
         own = cache_partials(
             cache_length, new_queries, cache_keys, cache_values, qcols,
-            own_count, own_count, 0, 0, group_size, seq_count, after=remote,
+            own_count, own_count, (), group_size, seq_count, after=remote,
         )
         parts.append(own)
     else:
         partial = cache_partials(
             cache_length, gathered, cache_keys, cache_values, qcols,
-            join_rows, min(join_rows, 256), 0, 0, 1, seq_count,
+            join_rows, min(join_rows, 256), (), 1, seq_count,
         )
         recv = lax.all_to_all(to_half(partial, qcols, heads_q), "seq", 0, 0, tiled=True)
         recv = recv.astype(jnp.float32)

time: 46.4 us -> 48.7 us (1.050)
  waiting for transfers between devices: 2.73 us -> 0.01 us
  Pallas kernels: 9.28 us -> 11.6 us
  starting transfers between devices: 3.87 us -> 4.77 us
  local copies, waits for them, and re-layouts: 3.31 us -> 4.19 us
  other arithmetic: 3.77 us -> 4.63 us
    ppermute x3, waiting for transfers between devices: 2.73 us -> 0.01 us  [the longest x2 0.01 us: on_device(): lax.ppermute(to_half(piece, qcols, heads_q), 'seq', pairs(shift))]
    pallas_call x2 -> x3, Pallas kernels: 9.28 us -> 11.6 us  [cache_partials(): pl.pallas_call(functools.partial(cache_kernel, seq_count, shifts, stack),...]
    convert_element_type x3 -> x4, other arithmetic: 0.06 us -> 1.04 us  [the longest x1 0.98 us: to_half(): return part.astype(jnp.float16)]
    unnamed x6, local copies, waits for them, and re-layouts: 0.68 us -> 1.59 us
    ppermute x3, starting transfers between devices: 3.87 us -> 4.77 us  [the longest x2 3.88 us: on_device(): lax.ppermute(to_half(piece, qcols, heads_q), 'seq', pairs(shift))]
  transfers between devices with their start and end apart: 3 -> 3, of which waited for: 1 -> 0; matrix products, arithmetic and copies ran while one was open for 6% -> 8% of each run, Pallas kernels for 7% -> 17%
where the time goes in v16:
time: 48.7 us; the launch traced here: 48.4 us
  blocking collectives  21.7 us (45%)
  Pallas kernels  11.6 us (24%)
  starting transfers between devices  4.77 us (10%)
  other arithmetic  4.63 us (10%)
  local copies, waits for them, and re-layouts  4.19 us (9%)
  between operations  0.85 us (2%)
  matrix products  0.62 us (1%)
    all_gather x1, blocking collectives, on_device(): gathered = lax.all_gather(packed, 'seq', axis=0, tiled=True)  21.7 us
    pallas_call x3, Pallas kernels, cache_partials(): pl.pallas_call(functools.partial(cache_kernel, seq_count, shifts, stack),...  11.6 us
    ppermute x2, starting transfers between devices, on_device(): lax.ppermute(to_half(piece, qcols, heads_q), 'seq', pairs(shift))  3.88 us
    unnamed x6, local copies, waits for them, and re-layouts  1.59 us
    another operation x1, other arithmetic  1.1 us
    convert_element_type x1, other arithmetic, on_device(): return attended.astype(jnp.bfloat16)  1.02 us
    slice x1, local copies, waits for them, and re-layouts, on_device(): all_values = gathered[:, qcols + kcols:]  0.99 us
    convert_element_type x1, other arithmetic, to_half(): return part.astype(jnp.float16)  0.98 us
  transfers between devices with their start and end apart: 3, of which 0 were waited for; matrix products, arithmetic and copies ran while one was open for 8% of the time, Pallas kernels for 17%

profile of v16, /device:TPU:0, one launch (start us, length us, event | category | flops | bytes accessed | tf_op | source)
XLA Modules:
  0.0 48.4 jit_solution(1355638714044108071)
XLA Ops:
  0.7 1.0 %pad_maximum_fusion = bf16[64,1536]{1,0:T(8,128)(2,1)S(1)} fusion(bf16[64,256]{1,0:T(8,128)(2,1)} %param.9, bf16[64,256]{1,0:T(8,128)(2,1)} %param.8, bf16[64,1024]{1,0:T(8,128)(2,1)} %q_ref.1), kind=kLoop, calls=%fused_computation.18 | loop fusion | flops 589824 | bytes 393216 | tf_op jit(solution)/shard_map/concatenate | solution.py:138
  1.6 21.7 %all_gather.3.q_ref = bf16[256,1536]{1,0:T(8,128)(2,1)} all-gather(bf16[64,1536]{1,0:T(8,128)(2,1)S(1)} %pad_maximum_fusion), channel_id=1, replica_groups=mesh['group'=2,'head'=4,'seq'=4] {'seq'}, dimensions={0}, use_global_device_ids=true | all-gather | bytes 983040 | tf_op jit(solution)/shard_map/all_gather | solution.py:139
  23.3 3.5 %shard_map.73.rest_0_ = f32[64,1152]{1,0:T(8,128)} custom-call(s32[1]{0:T(128)S(6)} %copy.57.len_ref, bf16[256,1536]{1,0:T(8,128)(2,1)} %all_gather.3.q_ref, bf16[1024,256]{1,0:T(8,128)(2,1)} %k_ref.5, bf16[1024,256]{1,0:T(8,128)(2,1)} %v_ref.5), custom_call_target="tpu_custom_call" | custom-call | flops 268435456 | bytes 1474560 | tf_op jit(solution)/shard_map/pallas_call | solution.py:108
  26.9 1.0 %convert_element_type.24 = f16[64,1152]{1,0:T(8,128)(2,1)S(1)} convert(f32[64,1152]{1,0:T(8,128)} %shard_map.73.rest_0_) | non-fusion elementwise | flops 73728 | bytes 442368 | tf_op jit(solution)/shard_map/convert_element_type | solution.py:85
  27.8 0.9 %collective-permute-start = (f16[64,1152]{1,0:T(8,128)(2,1)S(1)}, f16[64,1152]{1,0:T(8,128)(2,1)S(1)}, u32[]{:S(2)}, u32[]{:S(2)}) collective-permute-start(f16[64,1152]{1,0:T(8,128)(2,1)S(1)} %convert_element_type.24), channel_id=1, source_target_pairs={{0,2},{1,3},{2,0},{3,1},{4,6},{5,7},{6,4},{7,5},{8,10},{9,11},{10,... | collective-permute-start | bytes 442376 | tf_op jit(solution)/shard_map/ppermute | solution.py:152
  28.7 4.7 %shard_map.74.rest_0_ = f32[128,1152]{1,0:T(8,128)} custom-call(s32[1]{0:T(128)S(6)} %copy.57.len_ref, bf16[256,1536]{1,0:T(8,128)(2,1)} %all_gather.3.q_ref, bf16[1024,256]{1,0:T(8,128)(2,1)} %k_ref.5, bf16[1024,256]{1,0:T(8,128)(2,1)} %v_ref.5, f32[64,1152]{1,0:T(8,128)} %shard_map.73.rest_0_), custom_call_target="tpu_custom_call" | custom-call | flops 536870912 | bytes 1900544 | tf_op jit(solution)/shard_map/pallas_call | solution.py:108
  33.4 1.1 %convert.4 = f16[128,1152]{1,0:T(8,128)(2,1)S(1)} convert(f32[128,1152]{1,0:T(8,128)} %shard_map.74.rest_0_) | non-fusion elementwise | flops 147456 | bytes 884736 | tf_op jit(solution)/shard_map/convert.1
  34.5 0.0 copy-start.1
  34.5 0.1 fusion.20
  34.6 1.8 %collective-permute-start.1 = (f16[64,1152]{1,0:T(8,128)(2,1)S(1)}, f16[64,1152]{1,0:T(8,128)(2,1)S(1)}, u32[]{:S(2)}, u32[]{:S(2)}) collective-permute-start(f16[64,1152]{1,0:T(8,128)(2,1)S(1)} %get-tuple-element.14), channel_id=1, source_target_pairs={{0,1},{1,2},{2,3},{3,0},{4,5},{5,6},{6,7},{7,4},{8,9},{9,10},{10,1... | collective-permute-start | bytes 442376 | tf_op jit(solution)/shard_map/ppermute | solution.py:163
  36.4 2.1 %collective-permute-start.2 = (f16[64,1152]{1,0:T(8,128)(2,1)S(1)}, f16[64,1152]{1,0:T(8,128)(2,1)S(1)}, u32[]{:S(2)}, u32[]{:S(2)}) collective-permute-start(f16[64,1152]{1,0:T(8,128)(2,1)S(1)} %get-tuple-element.15), channel_id=1, source_target_pairs={{0,3},{1,0},{2,1},{3,2},{4,7},{5,4},{6,5},{7,6},{8,11},{9,8},{10,9... | collective-permute-start | bytes 442376 | tf_op jit(solution)/shard_map/ppermute | solution.py:163
  38.4 0.0 copy-done.1
  38.4 0.1 reshape.94
  38.5 1.0 %fusion.19 = (bf16[256,256]{1,0:T(8,128)(2,1)S(1)}, bf16[256,256]{1,0:T(8,128)(2,1)S(1)}) fusion(bf16[256,1536]{1,0:T(8,128)(2,1)} %all_gather.3.q_ref), kind=kLoop, calls=%fused_computation.39 | loop fusion | bytes 524288 | tf_op jit(solution)/shard_map/slice | solution.py:141
  39.6 0.0 copy-start.2
  39.6 0.7 %copy-done.2 = s32[256]{0:T(256)S(1)} copy-done((s32[256]{0:T(256)S(1)}, s32[256]{0:T(256)}, u32[]{:S(2)}) %copy-start.2) | copy-done | bytes 1048
  40.3 0.1 dynamic_slice.3
  40.4 0.1 fusion.9
  40.5 0.3 select_reduce_fusion
  40.8 0.3 convolution_bitcast_fusion
  41.1 0.2 copy.23
  41.3 0.1 reshape.95
  41.4 0.3 convert_reduce_fusion
  41.7 0.1 copy.26
  41.7 0.1 copy.25
  41.8 3.4 %shard_map.75 = f32[64,1152]{1,0:T(8,128)} custom-call(s32[1]{0:T(128)S(6)} %copy.57.len_ref, bf16[64,1024]{1,0:T(8,128)(2,1)} %q_ref.1, bf16[1024,256]{1,0:T(8,128)(2,1)} %k_ref.5, bf16[1024,256]{1,0:T(8,128)(2,1)} %v_ref.5, f32[128,1152]{1,0:T(8,128)} %shard_map.74.rest_0_), custom_call_target="tpu_custom_call" | custom-call | flops 268435456 | bytes 1474560 | tf_op jit(solution)/shard_map/pallas_call | solution.py:108
  45.2 0.0 collective-permute-done
  45.3 0.0 collective-permute-done.1
  45.3 0.0 copy-start
  45.3 0.0 collective-permute-done.2
  45.4 0.9 %copy-done = f32[64,1152]{1,0:T(8,128)S(1)} copy-done((f32[64,1152]{1,0:T(8,128)S(1)}, f32[64,1152]{1,0:T(8,128)}, u32[]{:S(2)}) %copy-start) | copy-done | bytes 294936
  46.3 0.1 add_add_fusion
  46.4 0.1 broadcast_in_dim.38
  46.5 0.1 broadcast_in_dim.32
  46.7 0.1 broadcast_in_dim.33
  46.8 0.1 broadcast_in_dim.34
  46.9 0.1 broadcast_in_dim.35
  47.1 0.1 broadcast_in_dim.36
  47.2 0.1 broadcast_in_dim.37
  47.3 1.0 %fusion.1 = bf16[64,1024]{1,0:T(8,128)(2,1)} fusion(f32[8,8,8,128]{3,2,1,0:T(8,128)S(1)} %bitcast.51, f32[8,8,8,128]{3,2,1,0:T(8,128)S(1)} %bitcast.57, f32[8,8,8,128]{3,2,1,0:T(8,128)S(1)} %bitcast.56, f32[8,8,8,128]{3,2,1,0:T(8,128)S(1)} %bitcast.55, f32[8,8,8,128]{3,2,1,0:T(8,128)S(1)} %bitcast.54, f32[8,8,8,128]{3,2,1,0:T(8,128)S(1)} %bitcast.53, ...), kind=kLoop, calls=%fused_computation.7 | loop fusion | flops 786432 | bytes 3276800 | tf_op jit(solution)/shard_map/convert_element_type | solution.py:244
  (6 shorter events, 0.1 us)
Async XLA Ops:
  27.8 17.4 %collective-permute-start = (f16[64,1152]{1,0:T(8,128)(2,1)S(1)}, f16[64,1152]{1,0:T(8,128)(2,1)S(1)}, u32[]{:S(2)}, u32[]{:S(2)}) collective-permute-start(f16[64,1152]{1,0:T(8,128)(2,1)S(1)} %convert_element_type.24), channel_id=1, source_target_pairs={{0,2},{1,3},{2,0},{3,1},{4,6},{5,7},{6,4},{7,5},{8,10},{9,11},{10,... | collective-permute-start | bytes 442376 | tf_op jit(solution)/shard_map/ppermute | solution.py:152
  34.5 4.0 %copy-start.1 = (bf16[64,1024]{1,0:T(8,128)(2,1)S(1)}, bf16[64,1024]{1,0:T(8,128)(2,1)}, u32[]{:S(2)}) copy-start(bf16[64,1024]{1,0:T(8,128)(2,1)} %q_ref.1) | copy-start | bytes 393220
  34.6 10.7 %collective-permute-start.1 = (f16[64,1152]{1,0:T(8,128)(2,1)S(1)}, f16[64,1152]{1,0:T(8,128)(2,1)S(1)}, u32[]{:S(2)}, u32[]{:S(2)}) collective-permute-start(f16[64,1152]{1,0:T(8,128)(2,1)S(1)} %get-tuple-element.14), channel_id=1, source_target_pairs={{0,1},{1,2},{2,3},{3,0},{4,5},{5,6},{6,7},{7,4},{8,9},{9,10},{10,1... | collective-permute-start | bytes 442376 | tf_op jit(solution)/shard_map/ppermute | solution.py:163
  36.4 8.9 %collective-permute-start.2 = (f16[64,1152]{1,0:T(8,128)(2,1)S(1)}, f16[64,1152]{1,0:T(8,128)(2,1)S(1)}, u32[]{:S(2)}, u32[]{:S(2)}) collective-permute-start(f16[64,1152]{1,0:T(8,128)(2,1)S(1)} %get-tuple-element.15), channel_id=1, source_target_pairs={{0,3},{1,0},{2,1},{3,2},{4,7},{5,4},{6,5},{7,6},{8,11},{9,8},{10,9... | collective-permute-start | bytes 442376 | tf_op jit(solution)/shard_map/ppermute | solution.py:163
  39.6 0.7 %copy-start.2 = (s32[256]{0:T(256)S(1)}, s32[256]{0:T(256)}, u32[]{:S(2)}) copy-start(s32[256]{0:T(256)} %param.12) | copy-start | bytes 3076
  45.3 1.0 %copy-start = (f32[64,1152]{1,0:T(8,128)S(1)}, f32[64,1152]{1,0:T(8,128)}, u32[]{:S(2)}) copy-start(f32[64,1152]{1,0:T(8,128)} %shard_map.75) | copy-start | bytes 884740

commit v17 on v15

--- a/solution.py
+++ b/solution.py
@@ -146,7 +146,7 @@
             seq_count,
         )
         parts = []
-        for shift in range(1, seq_count):
+        for shift in sorted(range(1, seq_count), key=lambda s: abs(2 * s - seq_count)):
             piece = remote[(shift - 1) * own_count:shift * own_count]
             parts.append(
                 lax.ppermute(

time: 46.4 us -> 45.4 us (0.978)
  waiting for transfers between devices: 2.73 us -> 1.7 us
  starting transfers between devices: 3.87 us -> 2.92 us
  local copies, waits for them, and re-layouts: 3.31 us -> 4.22 us
    ppermute x3, waiting for transfers between devices: 2.73 us -> 1.7 us  [on_device(): lax.ppermute(to_half(piece, qcols, heads_q), 'seq', [(i, (i + shift) % se...]
    ppermute x3, starting transfers between devices: 3.87 us -> 2.92 us  [on_device(): lax.ppermute(to_half(piece, qcols, heads_q), 'seq', [(i, (i + shift) % se...]
    unnamed x6, local copies, waits for them, and re-layouts: 0.68 us -> 1.59 us
  transfers between devices with their start and end apart: 3 -> 3, of which waited for: 1 -> 1; matrix products, arithmetic and copies ran while one was open for 6% -> 6% of each run, Pallas kernels for 7% -> 8%
where the time goes in v17:
time: 45.4 us; the launch traced here: 45.1 us
  blocking collectives  21.7 us (48%)
  Pallas kernels  9.28 us (20%)
  local copies, waits for them, and re-layouts  4.22 us (9%)
  other arithmetic  3.76 us (8%)
  starting transfers between devices  2.92 us (6%)
  waiting for transfers between devices  1.7 us (4%)
  between operations  0.85 us (2%)
  matrix products  0.62 us (1%)
    all_gather x1, blocking collectives, on_device(): gathered = lax.all_gather(packed, 'seq', axis=0, tiled=True)  21.7 us
    pallas_call x2, Pallas kernels, cache_partials(): pl.pallas_call(functools.partial(cache_kernel, seq_count, first, pieces,...  9.28 us
    ppermute x3, starting transfers between devices, on_device(): lax.ppermute(to_half(piece, qcols, heads_q), 'seq', [(i, (i + shift) % se...  2.92 us
    ppermute x3, waiting for transfers between devices, on_device(): lax.ppermute(to_half(piece, qcols, heads_q), 'seq', [(i, (i + shift) % se...  1.7 us
    unnamed x6, local copies, waits for them, and re-layouts  1.59 us
    another operation x1, other arithmetic  1.22 us
    convert_element_type x1, other arithmetic, on_device(): return attended.astype(jnp.bfloat16)  1.02 us
    slice x1, local copies, waits for them, and re-layouts, on_device(): all_values = gathered[:, qcols + kcols:]  0.99 us
  transfers between devices with their start and end apart: 3, of which 1 were waited for; matrix products, arithmetic and copies ran while one was open for 6% of the time, Pallas kernels for 8%

profile of v17, /device:TPU:0, one launch (start us, length us, event | category | flops | bytes accessed | tf_op | source)
XLA Modules:
  0.0 45.1 jit_solution(8601078782069539138)
XLA Ops:
  0.7 1.0 %pad_maximum_fusion = bf16[64,1536]{1,0:T(8,128)(2,1)S(1)} fusion(bf16[64,256]{1,0:T(8,128)(2,1)} %param.9, bf16[64,256]{1,0:T(8,128)(2,1)} %param.8, bf16[64,1024]{1,0:T(8,128)(2,1)} %q_ref.1), kind=kLoop, calls=%fused_computation.18 | loop fusion | flops 589824 | bytes 393216 | tf_op jit(solution)/shard_map/concatenate | solution.py:137
  1.6 21.7 %all_gather.3.q_ref = bf16[256,1536]{1,0:T(8,128)(2,1)} all-gather(bf16[64,1536]{1,0:T(8,128)(2,1)S(1)} %pad_maximum_fusion), channel_id=1, replica_groups=mesh['group'=2,'head'=4,'seq'=4] {'seq'}, dimensions={0}, use_global_device_ids=true | all-gather | bytes 983040 | tf_op jit(solution)/shard_map/all_gather | solution.py:138
  23.3 5.9 %shard_map.73.rest_0_ = f32[192,1152]{1,0:T(8,128)} custom-call(s32[1]{0:T(128)S(6)} %copy.57.len_ref, bf16[256,1536]{1,0:T(8,128)(2,1)} %all_gather.3.q_ref, bf16[1024,256]{1,0:T(8,128)(2,1)} %k_ref.3, bf16[1024,256]{1,0:T(8,128)(2,1)} %v_ref.3), custom_call_target="tpu_custom_call" | custom-call | flops 805306368 | bytes 2326528 | tf_op jit(solution)/shard_map/pallas_call | solution.py:107
  29.2 1.2 %convert.5 = f16[192,1152]{1,0:T(8,128)(2,1)S(1)} convert(f32[192,1152]{1,0:T(8,128)} %shard_map.73.rest_0_) | non-fusion elementwise | flops 221184 | bytes 1327104 | tf_op jit(solution)/shard_map/convert.2
  30.4 0.0 copy-start.1
  30.4 0.1 fusion.20
  30.5 0.9 %collective-permute-start = (f16[64,1152]{1,0:T(8,128)(2,1)S(1)}, f16[64,1152]{1,0:T(8,128)(2,1)S(1)}, u32[]{:S(2)}, u32[]{:S(2)}) collective-permute-start(f16[64,1152]{1,0:T(8,128)(2,1)S(1)} %get-tuple-element.14), channel_id=1, source_target_pairs={{0,2},{1,3},{2,0},{3,1},{4,6},{5,7},{6,4},{7,5},{8,10},{9,11},{10,... | collective-permute-start | bytes 442376 | tf_op jit(solution)/shard_map/ppermute | solution.py:152
  31.4 1.5 %collective-permute-start.2 = (f16[64,1152]{1,0:T(8,128)(2,1)S(1)}, f16[64,1152]{1,0:T(8,128)(2,1)S(1)}, u32[]{:S(2)}, u32[]{:S(2)}) collective-permute-start(f16[64,1152]{1,0:T(8,128)(2,1)S(1)} %get-tuple-element.15), channel_id=1, source_target_pairs={{0,3},{1,0},{2,1},{3,2},{4,7},{5,4},{6,5},{7,6},{8,11},{9,8},{10,9... | collective-permute-start | bytes 442376 | tf_op jit(solution)/shard_map/ppermute | solution.py:152
  32.9 0.5 %collective-permute-start.1 = (f16[64,1152]{1,0:T(8,128)(2,1)S(1)}, f16[64,1152]{1,0:T(8,128)(2,1)S(1)}, u32[]{:S(2)}, u32[]{:S(2)}) collective-permute-start(f16[64,1152]{1,0:T(8,128)(2,1)S(1)} %get-tuple-element.16), channel_id=1, source_target_pairs={{0,1},{1,2},{2,3},{3,0},{4,5},{5,6},{6,7},{7,4},{8,9},{9,10},{10,1... | collective-permute-start | bytes 442376 | tf_op jit(solution)/shard_map/ppermute | solution.py:152
  33.4 0.0 copy-done.1
  33.4 0.1 reshape.94
  33.5 1.0 %fusion.19 = (bf16[256,256]{1,0:T(8,128)(2,1)S(1)}, bf16[256,256]{1,0:T(8,128)(2,1)S(1)}) fusion(bf16[256,1536]{1,0:T(8,128)(2,1)} %all_gather.3.q_ref), kind=kLoop, calls=%fused_computation.39 | loop fusion | bytes 524288 | tf_op jit(solution)/shard_map/slice | solution.py:140
  34.6 0.0 copy-start.2
  34.6 0.7 %copy-done.2 = s32[256]{0:T(256)S(1)} copy-done((s32[256]{0:T(256)S(1)}, s32[256]{0:T(256)}, u32[]{:S(2)}) %copy-start.2) | copy-done | bytes 1048
  35.3 0.1 dynamic_slice.3
  35.3 0.1 fusion.9
  35.4 0.3 select_reduce_fusion
  35.8 0.3 convolution_bitcast_fusion
  36.1 0.2 copy.23
  36.3 0.1 reshape.95
  36.4 0.3 convert_reduce_fusion
  36.6 0.1 copy.26
  36.7 0.1 copy.25
  36.8 3.4 %shard_map.74 = f32[64,1152]{1,0:T(8,128)} custom-call(s32[1]{0:T(128)S(6)} %copy.57.len_ref, bf16[64,1024]{1,0:T(8,128)(2,1)} %q_ref.1, bf16[1024,256]{1,0:T(8,128)(2,1)} %k_ref.3, bf16[1024,256]{1,0:T(8,128)(2,1)} %v_ref.3, f32[192,1152]{1,0:T(8,128)} %shard_map.73.rest_0_), custom_call_target="tpu_custom_call" | custom-call | flops 268435456 | bytes 1474560 | tf_op jit(solution)/shard_map/pallas_call | solution.py:107
  40.2 1.7 %collective-permute-done = f16[64,1152]{1,0:T(8,128)(2,1)S(1)} collective-permute-done((f16[64,1152]{1,0:T(8,128)(2,1)S(1)}, f16[64,1152]{1,0:T(8,128)(2,1)S(1)}, u32[]{:S(2)}, u32[]{:S(2)}) %collective-permute-start) | collective-permute-done | bytes 147488 | tf_op jit(solution)/shard_map/ppermute | solution.py:152
  42.0 0.0 collective-permute-done.2
  42.0 0.0 copy-start
  42.0 0.0 collective-permute-done.1
  42.0 0.9 %copy-done = f32[64,1152]{1,0:T(8,128)S(1)} copy-done((f32[64,1152]{1,0:T(8,128)S(1)}, f32[64,1152]{1,0:T(8,128)}, u32[]{:S(2)}) %copy-start) | copy-done | bytes 294936
  43.0 0.1 add_add_fusion
  43.1 0.1 broadcast_in_dim.38
  43.2 0.1 broadcast_in_dim.32
  43.4 0.1 broadcast_in_dim.33
  43.5 0.1 broadcast_in_dim.34
  43.6 0.1 broadcast_in_dim.35
  43.8 0.1 broadcast_in_dim.36
  43.9 0.1 broadcast_in_dim.37
  44.0 1.0 %fusion.1 = bf16[64,1024]{1,0:T(8,128)(2,1)} fusion(f32[8,8,8,128]{3,2,1,0:T(8,128)S(1)} %bitcast.51, f32[8,8,8,128]{3,2,1,0:T(8,128)S(1)} %bitcast.57, f32[8,8,8,128]{3,2,1,0:T(8,128)S(1)} %bitcast.56, f32[8,8,8,128]{3,2,1,0:T(8,128)S(1)} %bitcast.55, f32[8,8,8,128]{3,2,1,0:T(8,128)S(1)} %bitcast.54, f32[8,8,8,128]{3,2,1,0:T(8,128)S(1)} %bitcast.53, ...), kind=kLoop, calls=%fused_computation.7 | loop fusion | flops 786432 | bytes 3276800 | tf_op jit(solution)/shard_map/convert_element_type | solution.py:232
  (6 shorter events, 0.1 us)
Async XLA Ops:
  30.4 3.0 %copy-start.1 = (bf16[64,1024]{1,0:T(8,128)(2,1)S(1)}, bf16[64,1024]{1,0:T(8,128)(2,1)}, u32[]{:S(2)}) copy-start(bf16[64,1024]{1,0:T(8,128)(2,1)} %q_ref.1) | copy-start | bytes 393220
  30.5 11.4 %collective-permute-start = (f16[64,1152]{1,0:T(8,128)(2,1)S(1)}, f16[64,1152]{1,0:T(8,128)(2,1)S(1)}, u32[]{:S(2)}, u32[]{:S(2)}) collective-permute-start(f16[64,1152]{1,0:T(8,128)(2,1)S(1)} %get-tuple-element.14), channel_id=1, source_target_pairs={{0,2},{1,3},{2,0},{3,1},{4,6},{5,7},{6,4},{7,5},{8,10},{9,11},{10,... | collective-permute-start | bytes 442376 | tf_op jit(solution)/shard_map/ppermute | solution.py:152
  31.4 10.6 %collective-permute-start.2 = (f16[64,1152]{1,0:T(8,128)(2,1)S(1)}, f16[64,1152]{1,0:T(8,128)(2,1)S(1)}, u32[]{:S(2)}, u32[]{:S(2)}) collective-permute-start(f16[64,1152]{1,0:T(8,128)(2,1)S(1)} %get-tuple-element.15), channel_id=1, source_target_pairs={{0,3},{1,0},{2,1},{3,2},{4,7},{5,4},{6,5},{7,6},{8,11},{9,8},{10,9... | collective-permute-start | bytes 442376 | tf_op jit(solution)/shard_map/ppermute | solution.py:152
  32.9 9.1 %collective-permute-start.1 = (f16[64,1152]{1,0:T(8,128)(2,1)S(1)}, f16[64,1152]{1,0:T(8,128)(2,1)S(1)}, u32[]{:S(2)}, u32[]{:S(2)}) collective-permute-start(f16[64,1152]{1,0:T(8,128)(2,1)S(1)} %get-tuple-element.16), channel_id=1, source_target_pairs={{0,1},{1,2},{2,3},{3,0},{4,5},{5,6},{6,7},{7,4},{8,9},{9,10},{10,1... | collective-permute-start | bytes 442376 | tf_op jit(solution)/shard_map/ppermute | solution.py:152
  34.6 0.7 %copy-start.2 = (s32[256]{0:T(256)S(1)}, s32[256]{0:T(256)}, u32[]{:S(2)}) copy-start(s32[256]{0:T(256)} %param.12) | copy-start | bytes 3076
  42.0 1.0 %copy-start = (f32[64,1152]{1,0:T(8,128)S(1)}, f32[64,1152]{1,0:T(8,128)}, u32[]{:S(2)}) copy-start(f32[64,1152]{1,0:T(8,128)} %shard_map.74) | copy-start | bytes 884740

commit v18 on v17

--- a/solution.py
+++ b/solution.py
@@ -146,7 +146,7 @@
             seq_count,
         )
         parts = []
-        for shift in sorted(range(1, seq_count), key=lambda s: abs(2 * s - seq_count)):
+        for shift in sorted(range(1, seq_count), key=lambda s: (abs(2 * s - seq_count), -s)):
             piece = remote[(shift - 1) * own_count:shift * own_count]
             parts.append(
                 lax.ppermute(

time: 45.4 us -> 45.5 us (level)
  starting transfers between devices: 2.92 us -> 4.72 us
  waiting for transfers between devices: 1.7 us -> 0.01 us
    ppermute x3, starting transfers between devices: 2.92 us -> 4.72 us  [on_device(): lax.ppermute(to_half(piece, qcols, heads_q), 'seq', [(i, (i + shift) % se...]
    ppermute x3, waiting for transfers between devices: 1.7 us -> 0.01 us  [on_device(): lax.ppermute(to_half(piece, qcols, heads_q), 'seq', [(i, (i + shift) % se...]
  transfers between devices with their start and end apart: 3 -> 3, of which waited for: 1 -> 0; matrix products, arithmetic and copies ran while one was open for 6% -> 6% of each run, Pallas kernels for 8% -> 8%
where the time goes in v18:
time: 45.5 us; the launch traced here: 45.2 us
  blocking collectives  21.7 us (48%)
  Pallas kernels  9.28 us (20%)
  starting transfers between devices  4.72 us (10%)
  local copies, waits for them, and re-layouts  4.22 us (9%)
  other arithmetic  3.76 us (8%)
  between operations  0.85 us (2%)
  matrix products  0.61 us (1%)
    all_gather x1, blocking collectives, on_device(): gathered = lax.all_gather(packed, 'seq', axis=0, tiled=True)  21.7 us
    pallas_call x2, Pallas kernels, cache_partials(): pl.pallas_call(functools.partial(cache_kernel, seq_count, first, pieces,...  9.28 us
    ppermute x3, starting transfers between devices, on_device(): lax.ppermute(to_half(piece, qcols, heads_q), 'seq', [(i, (i + shift) % se...  4.72 us
    unnamed x6, local copies, waits for them, and re-layouts  1.59 us
    another operation x1, other arithmetic  1.22 us
    convert_element_type x1, other arithmetic, on_device(): return attended.astype(jnp.bfloat16)  1.02 us
    slice x1, local copies, waits for them, and re-layouts, on_device(): all_values = gathered[:, qcols + kcols:]  0.99 us
    concatenate x1, other arithmetic, on_device(): packed = jnp.concatenate([new_queries, new_keys, new_values], axis=1)  0.96 us
  transfers between devices with their start and end apart: 3, of which 0 were waited for; matrix products, arithmetic and copies ran while one was open for 6% of the time, Pallas kernels for 8%

profile of v18, /device:TPU:0, one launch (start us, length us, event | category | flops | bytes accessed | tf_op | source)
XLA Modules:
  0.0 45.2 jit_solution(12414382344117982306)
XLA Ops:
  0.7 1.0 %pad_maximum_fusion = bf16[64,1536]{1,0:T(8,128)(2,1)S(1)} fusion(bf16[64,256]{1,0:T(8,128)(2,1)} %param.9, bf16[64,256]{1,0:T(8,128)(2,1)} %param.8, bf16[64,1024]{1,0:T(8,128)(2,1)} %q_ref.1), kind=kLoop, calls=%fused_computation.18 | loop fusion | flops 589824 | bytes 393216 | tf_op jit(solution)/shard_map/concatenate | solution.py:137
  1.6 21.7 %all_gather.3.q_ref = bf16[256,1536]{1,0:T(8,128)(2,1)} all-gather(bf16[64,1536]{1,0:T(8,128)(2,1)S(1)} %pad_maximum_fusion), channel_id=1, replica_groups=mesh['group'=2,'head'=4,'seq'=4] {'seq'}, dimensions={0}, use_global_device_ids=true | all-gather | bytes 983040 | tf_op jit(solution)/shard_map/all_gather | solution.py:138
  23.3 5.9 %shard_map.73.rest_0_ = f32[192,1152]{1,0:T(8,128)} custom-call(s32[1]{0:T(128)S(6)} %copy.57.len_ref, bf16[256,1536]{1,0:T(8,128)(2,1)} %all_gather.3.q_ref, bf16[1024,256]{1,0:T(8,128)(2,1)} %k_ref.3, bf16[1024,256]{1,0:T(8,128)(2,1)} %v_ref.3), custom_call_target="tpu_custom_call" | custom-call | flops 805306368 | bytes 2326528 | tf_op jit(solution)/shard_map/pallas_call | solution.py:107
  29.2 1.2 %convert.5 = f16[192,1152]{1,0:T(8,128)(2,1)S(1)} convert(f32[192,1152]{1,0:T(8,128)} %shard_map.73.rest_0_) | non-fusion elementwise | flops 221184 | bytes 1327104 | tf_op jit(solution)/shard_map/convert.2
  30.4 0.0 copy-start.1
  30.4 0.1 fusion.20
  30.5 0.9 %collective-permute-start = (f16[64,1152]{1,0:T(8,128)(2,1)S(1)}, f16[64,1152]{1,0:T(8,128)(2,1)S(1)}, u32[]{:S(2)}, u32[]{:S(2)}) collective-permute-start(f16[64,1152]{1,0:T(8,128)(2,1)S(1)} %get-tuple-element.14), channel_id=1, source_target_pairs={{0,2},{1,3},{2,0},{3,1},{4,6},{5,7},{6,4},{7,5},{8,10},{9,11},{10,... | collective-permute-start | bytes 442376 | tf_op jit(solution)/shard_map/ppermute | solution.py:152
  31.4 1.8 %collective-permute-start.2 = (f16[64,1152]{1,0:T(8,128)(2,1)S(1)}, f16[64,1152]{1,0:T(8,128)(2,1)S(1)}, u32[]{:S(2)}, u32[]{:S(2)}) collective-permute-start(f16[64,1152]{1,0:T(8,128)(2,1)S(1)} %get-tuple-element.15), channel_id=1, source_target_pairs={{0,1},{1,2},{2,3},{3,0},{4,5},{5,6},{6,7},{7,4},{8,9},{9,10},{10,1... | collective-permute-start | bytes 442376 | tf_op jit(solution)/shard_map/ppermute | solution.py:152
  33.2 2.1 %collective-permute-start.1 = (f16[64,1152]{1,0:T(8,128)(2,1)S(1)}, f16[64,1152]{1,0:T(8,128)(2,1)S(1)}, u32[]{:S(2)}, u32[]{:S(2)}) collective-permute-start(f16[64,1152]{1,0:T(8,128)(2,1)S(1)} %get-tuple-element.16), channel_id=1, source_target_pairs={{0,3},{1,0},{2,1},{3,2},{4,7},{5,4},{6,5},{7,6},{8,11},{9,8},{10,9... | collective-permute-start | bytes 442376 | tf_op jit(solution)/shard_map/ppermute | solution.py:152
  35.2 0.0 copy-done.1
  35.2 0.1 reshape.94
  35.3 1.0 %fusion.19 = (bf16[256,256]{1,0:T(8,128)(2,1)S(1)}, bf16[256,256]{1,0:T(8,128)(2,1)S(1)}) fusion(bf16[256,1536]{1,0:T(8,128)(2,1)} %all_gather.3.q_ref), kind=kLoop, calls=%fused_computation.39 | loop fusion | bytes 524288 | tf_op jit(solution)/shard_map/slice | solution.py:140
  36.4 0.0 copy-start.2
  36.4 0.7 %copy-done.2 = s32[256]{0:T(256)S(1)} copy-done((s32[256]{0:T(256)S(1)}, s32[256]{0:T(256)}, u32[]{:S(2)}) %copy-start.2) | copy-done | bytes 1048
  37.1 0.1 dynamic_slice.3
  37.1 0.1 fusion.9
  37.2 0.3 select_reduce_fusion
  37.6 0.3 convolution_bitcast_fusion
  37.9 0.2 copy.23
  38.0 0.1 reshape.95
  38.2 0.3 convert_reduce_fusion
  38.4 0.1 copy.26
  38.5 0.1 copy.25
  38.6 3.4 %shard_map.74 = f32[64,1152]{1,0:T(8,128)} custom-call(s32[1]{0:T(128)S(6)} %copy.57.len_ref, bf16[64,1024]{1,0:T(8,128)(2,1)} %q_ref.1, bf16[1024,256]{1,0:T(8,128)(2,1)} %k_ref.3, bf16[1024,256]{1,0:T(8,128)(2,1)} %v_ref.3, f32[192,1152]{1,0:T(8,128)} %shard_map.73.rest_0_), custom_call_target="tpu_custom_call" | custom-call | flops 268435456 | bytes 1474560 | tf_op jit(solution)/shard_map/pallas_call | solution.py:107
  42.0 0.0 collective-permute-done
  42.1 0.0 collective-permute-done.2
  42.1 0.0 copy-start
  42.1 0.0 collective-permute-done.1
  42.1 0.9 %copy-done = f32[64,1152]{1,0:T(8,128)S(1)} copy-done((f32[64,1152]{1,0:T(8,128)S(1)}, f32[64,1152]{1,0:T(8,128)}, u32[]{:S(2)}) %copy-start) | copy-done | bytes 294936
  43.1 0.1 add_add_fusion
  43.2 0.1 broadcast_in_dim.38
  43.3 0.1 broadcast_in_dim.32
  43.5 0.1 broadcast_in_dim.33
  43.6 0.1 broadcast_in_dim.34
  43.7 0.1 broadcast_in_dim.35
  43.9 0.1 broadcast_in_dim.36
  44.0 0.1 broadcast_in_dim.37
  44.1 1.0 %fusion.1 = bf16[64,1024]{1,0:T(8,128)(2,1)} fusion(f32[8,8,8,128]{3,2,1,0:T(8,128)S(1)} %bitcast.51, f32[8,8,8,128]{3,2,1,0:T(8,128)S(1)} %bitcast.57, f32[8,8,8,128]{3,2,1,0:T(8,128)S(1)} %bitcast.56, f32[8,8,8,128]{3,2,1,0:T(8,128)S(1)} %bitcast.55, f32[8,8,8,128]{3,2,1,0:T(8,128)S(1)} %bitcast.54, f32[8,8,8,128]{3,2,1,0:T(8,128)S(1)} %bitcast.53, ...), kind=kLoop, calls=%fused_computation.7 | loop fusion | flops 786432 | bytes 3276800 | tf_op jit(solution)/shard_map/convert_element_type | solution.py:232
  (6 shorter events, 0.1 us)
Async XLA Ops:
  30.4 4.8 %copy-start.1 = (bf16[64,1024]{1,0:T(8,128)(2,1)S(1)}, bf16[64,1024]{1,0:T(8,128)(2,1)}, u32[]{:S(2)}) copy-start(bf16[64,1024]{1,0:T(8,128)(2,1)} %q_ref.1) | copy-start | bytes 393220
  30.5 11.5 %collective-permute-start = (f16[64,1152]{1,0:T(8,128)(2,1)S(1)}, f16[64,1152]{1,0:T(8,128)(2,1)S(1)}, u32[]{:S(2)}, u32[]{:S(2)}) collective-permute-start(f16[64,1152]{1,0:T(8,128)(2,1)S(1)} %get-tuple-element.14), channel_id=1, source_target_pairs={{0,2},{1,3},{2,0},{3,1},{4,6},{5,7},{6,4},{7,5},{8,10},{9,11},{10,... | collective-permute-start | bytes 442376 | tf_op jit(solution)/shard_map/ppermute | solution.py:152
  31.4 10.7 %collective-permute-start.2 = (f16[64,1152]{1,0:T(8,128)(2,1)S(1)}, f16[64,1152]{1,0:T(8,128)(2,1)S(1)}, u32[]{:S(2)}, u32[]{:S(2)}) collective-permute-start(f16[64,1152]{1,0:T(8,128)(2,1)S(1)} %get-tuple-element.15), channel_id=1, source_target_pairs={{0,1},{1,2},{2,3},{3,0},{4,5},{5,6},{6,7},{7,4},{8,9},{9,10},{10,1... | collective-permute-start | bytes 442376 | tf_op jit(solution)/shard_map/ppermute | solution.py:152
  33.2 8.9 %collective-permute-start.1 = (f16[64,1152]{1,0:T(8,128)(2,1)S(1)}, f16[64,1152]{1,0:T(8,128)(2,1)S(1)}, u32[]{:S(2)}, u32[]{:S(2)}) collective-permute-start(f16[64,1152]{1,0:T(8,128)(2,1)S(1)} %get-tuple-element.16), channel_id=1, source_target_pairs={{0,3},{1,0},{2,1},{3,2},{4,7},{5,4},{6,5},{7,6},{8,11},{9,8},{10,9... | collective-permute-start | bytes 442376 | tf_op jit(solution)/shard_map/ppermute | solution.py:152
  36.4 0.7 %copy-start.2 = (s32[256]{0:T(256)S(1)}, s32[256]{0:T(256)}, u32[]{:S(2)}) copy-start(s32[256]{0:T(256)} %param.12) | copy-start | bytes 3076
  42.1 1.0 %copy-start = (f32[64,1152]{1,0:T(8,128)S(1)}, f32[64,1152]{1,0:T(8,128)}, u32[]{:S(2)}) copy-start(f32[64,1152]{1,0:T(8,128)} %shard_map.74) | copy-start | bytes 884740

commit v19 on v18

--- a/solution.py
+++ b/solution.py
@@ -110,6 +110,7 @@
         in_specs=in_specs,
         out_specs=pl.BlockSpec((block, out_cols), lambda i: (i, 0)),
         out_shape=jax.ShapeDtypeStruct((rows, out_cols), jnp.float32),
+        compiler_params=pltpu.CompilerParams(vmem_limit_bytes=16 * 1024 * 1024),
         cost_estimate=pl.CostEstimate(
             flops=4 * rows * cache_rows * qcols,
             transcendentals=rows * cache_rows * heads_q,

time: 45.5 us -> 43.7 us (0.960)
  Pallas kernels: 9.28 us -> 5.04 us
  waiting for transfers between devices: 0.01 us -> 1.82 us
  other arithmetic: 3.76 us -> 5.39 us
  local copies, waits for them, and re-layouts: 4.22 us -> 3.69 us
    pallas_call x2, Pallas kernels: 9.28 us -> 5.04 us  [cache_partials(): pl.pallas_call(functools.partial(cache_kernel, seq_count, first, pieces,...]
    convert_element_type x3, other arithmetic: 0.07 us -> 2.79 us  [on_device(): parts.append(lax.ppermute(to_half(piece, qcols, heads_q), 'seq', [(i, (i...]
    ppermute x3, waiting for transfers between devices: 0.01 us -> 1.82 us  [on_device(): lax.ppermute(to_half(piece, qcols, heads_q), 'seq', [(i, (i + shift) % se...]
    another operation x1, other arithmetic: 1.22 us -> 0.05 us
    slice x1, local copies, waits for them, and re-layouts: 0.99 us -> 0.02 us  [on_device(): all_values = gathered[:, qcols + kcols:]]
    unnamed x6 -> x10, local copies, waits for them, and re-layouts: 1.59 us -> 0.73 us
    slice x1, local copies, waits for them, and re-layouts: 0.08 us -> 0.73 us  [on_device(): piece = remote[(shift - 1) * own_count:shift * own_count]]
    reshape x1, local copies, waits for them, and re-layouts: 0.07 us -> 0.73 us  [on_device(): new_queries.reshape(own_count, heads_kv, group_size, head_size)]
  transfers between devices with their start and end apart: 3 -> 3, of which waited for: 0 -> 1; matrix products, arithmetic and copies ran while one was open for 6% -> 10% of each run, Pallas kernels for 8% -> 3%
where the time goes in v19:
time: 43.7 us; the launch traced here: 43.5 us
  blocking collectives  21.4 us (49%)
  other arithmetic  5.39 us (12%)
  Pallas kernels  5.04 us (12%)
  starting transfers between devices  4.65 us (11%)
  local copies, waits for them, and re-layouts  3.69 us (8%)
  waiting for transfers between devices  1.82 us (4%)
  between operations  0.87 us (2%)
  matrix products  0.62 us (1%)
    all_gather x1, blocking collectives, on_device(): gathered = lax.all_gather(packed, 'seq', axis=0, tiled=True)  21.4 us
    pallas_call x2, Pallas kernels, cache_partials(): pl.pallas_call(functools.partial(cache_kernel, seq_count, first, pieces,...  5.04 us
    ppermute x3, starting transfers between devices, on_device(): lax.ppermute(to_half(piece, qcols, heads_q), 'seq', [(i, (i + shift) % se...  4.65 us
    convert_element_type x3, other arithmetic, on_device(): parts.append(lax.ppermute(to_half(piece, qcols, heads_q), 'seq', [(i, (i...  2.79 us
    ppermute x3, waiting for transfers between devices, on_device(): lax.ppermute(to_half(piece, qcols, heads_q), 'seq', [(i, (i + shift) % se...  1.82 us
    concatenate x1, other arithmetic, on_device(): packed = jnp.concatenate([new_queries, new_keys, new_values], axis=1)  1.02 us
    convert_element_type x1, other arithmetic, on_device(): return attended.astype(jnp.bfloat16)  1.02 us
    broadcast_in_dim x7, local copies, waits for them, and re-layouts, spread(): jnp.broadcast_to(x[:, :, None], (own_count, heads_q, head_size))  0.88 us
  transfers between devices with their start and end apart: 3, of which 1 were waited for; matrix products, arithmetic and copies ran while one was open for 10% of the time, Pallas kernels for 3%

profile of v19, /device:TPU:0, one launch (start us, length us, event | category | flops | bytes accessed | tf_op | source)
XLA Modules:
  0.0 43.5 jit_solution(4689238941366042892)
XLA Ops:
  0.7 0.0 copy-start.2
  0.7 1.0 %pad_maximum_fusion = bf16[64,1536]{1,0:T(8,128)(2,1)S(1)} fusion(bf16[64,256]{1,0:T(8,128)(2,1)} %param.9, bf16[64,256]{1,0:T(8,128)(2,1)} %param.8, bf16[64,1024]{1,0:T(8,128)(2,1)} %q_ref.1), kind=kLoop, calls=%fused_computation.18 | loop fusion | flops 589824 | bytes 393216 | tf_op jit(solution)/shard_map/concatenate | solution.py:138
  1.7 0.0 copy-start.1
  1.7 21.4 %all_gather.3.q_ref = bf16[256,1536]{1,0:T(8,128)(2,1)S(1)} all-gather(bf16[64,1536]{1,0:T(8,128)(2,1)S(1)} %pad_maximum_fusion), channel_id=1, replica_groups=mesh['group'=2,'head'=4,'seq'=4] {'seq'}, dimensions={0}, use_global_device_ids=true | all-gather | bytes 983040 | tf_op jit(solution)/shard_map/all_gather | solution.py:139
  23.1 0.0 copy-done.2
  23.1 0.0 copy-done.1
  23.1 3.6 %shard_map.73.rest_0_ = f32[192,1152]{1,0:T(8,128)S(1)} custom-call(s32[1]{0:T(128)S(6)} %copy.57.len_ref, bf16[256,1536]{1,0:T(8,128)(2,1)S(1)} %all_gather.3.q_ref, bf16[1024,256]{1,0:T(8,128)(2,1)S(1)} %copy-done.1, bf16[1024,256]{1,0:T(8,128)(2,1)S(1)} %copy-done.2), custom_call_target="tpu_custom_call" | custom-call | flops 805306368 | bytes 2326528 | tf_op jit(solution)/shard_map/pallas_call | solution.py:107
  26.7 0.1 convert.5
  26.8 0.0 copy-start
  26.8 0.7 %fusion.20 = (f16[64,1152]{1,0:T(8,128)(2,1)}, f16[64,1152]{1,0:T(8,128)(2,1)S(1)}, f16[64,1152]{1,0:T(8,128)(2,1)S(1)}) fusion(f16[192,1152]{1,0:T(8,128)(2,1)S(1)} %convert.5), kind=kLoop, calls=%fused_computation.40 | loop fusion | bytes 884736 | tf_op jit(solution)/shard_map/slice | solution.py:151
  27.5 0.8 %collective-permute-start = (f16[64,1152]{1,0:T(8,128)(2,1)}, f16[64,1152]{1,0:T(8,128)(2,1)}, u32[]{:S(2)}, u32[]{:S(2)}) collective-permute-start(f16[64,1152]{1,0:T(8,128)(2,1)} %get-tuple-element.14), channel_id=1, source_target_pairs={{0,2},{1,3},{2,0},{3,1},{4,6},{5,7},{6,4},{7,5},{8,10},{9,11},{10,... | collective-permute-start | bytes 442376 | tf_op jit(solution)/shard_map/ppermute | solution.py:153
  28.4 1.4 %collective-permute-start.2 = (f16[64,1152]{1,0:T(8,128)(2,1)S(1)}, f16[64,1152]{1,0:T(8,128)(2,1)}, u32[]{:S(2)}, u32[]{:S(2)}) collective-permute-start(f16[64,1152]{1,0:T(8,128)(2,1)S(1)} %get-tuple-element.15), channel_id=1, source_target_pairs={{0,1},{1,2},{2,3},{3,0},{4,5},{5,6},{6,7},{7,4},{8,9},{9,10},{10,1... | collective-permute-start | bytes 442376 | tf_op jit(solution)/shard_map/ppermute | solution.py:153
  29.8 2.4 %collective-permute-start.1 = (f16[64,1152]{1,0:T(8,128)(2,1)S(1)}, f16[64,1152]{1,0:T(8,128)(2,1)}, u32[]{:S(2)}, u32[]{:S(2)}) collective-permute-start(f16[64,1152]{1,0:T(8,128)(2,1)S(1)} %get-tuple-element.16), channel_id=1, source_target_pairs={{0,3},{1,0},{2,1},{3,2},{4,7},{5,4},{6,5},{7,6},{8,11},{9,8},{10,9... | collective-permute-start | bytes 442376 | tf_op jit(solution)/shard_map/ppermute | solution.py:153
  32.2 0.0 copy-done
  32.2 0.7 %reshape.94 = bf16[64,2,4,128]{3,2,1,0:T(4,128)(2,1)} reshape(bf16[64,1024]{1,0:T(8,128)(2,1)S(1)} %copy-done) | data formatting | bytes 262144 | tf_op jit(solution)/shard_map/reshape | solution.py:178
  33.0 0.0 copy-start.3
  33.0 0.0 copy-start.4
  33.1 0.7 %copy-done.4 = s32[256]{0:T(256)S(1)} copy-done((s32[256]{0:T(256)S(1)}, s32[256]{0:T(256)}, u32[]{:S(2)}) %copy-start.4) | copy-done | bytes 1048
  33.8 0.1 dynamic_slice.3
  33.8 0.1 fusion.9
  33.9 0.0 copy-done.3
  33.9 0.3 select_reduce_fusion
  34.3 0.3 convolution_bitcast_fusion
  34.6 0.2 copy.23
  34.7 0.1 reshape.95
  34.9 0.3 convert_reduce_fusion
  35.1 0.1 copy.26
  35.2 0.1 copy.25
  35.3 1.4 %shard_map.74 = f32[64,1152]{1,0:T(8,128)S(1)} custom-call(s32[1]{0:T(128)S(6)} %copy.57.len_ref, bf16[64,1024]{1,0:T(8,128)(2,1)S(1)} %copy-done, bf16[1024,256]{1,0:T(8,128)(2,1)S(1)} %copy-done.1, bf16[1024,256]{1,0:T(8,128)(2,1)S(1)} %copy-done.2, f32[192,1152]{1,0:T(8,128)S(1)} %shard_map.73.rest_0_), custom_call_target="tpu_custom_call" | custom-call | flops 268435456 | bytes 1474560 | tf_op jit(solution)/shard_map/pallas_call | solution.py:107
  36.8 1.8 %collective-permute-done = f16[64,1152]{1,0:T(8,128)(2,1)} collective-permute-done((f16[64,1152]{1,0:T(8,128)(2,1)}, f16[64,1152]{1,0:T(8,128)(2,1)}, u32[]{:S(2)}, u32[]{:S(2)}) %collective-permute-start) | collective-permute-done | bytes 147488 | tf_op jit(solution)/shard_map/ppermute | solution.py:153
  38.6 0.9 %convert_element_type.22 = f32[64,1152]{1,0:T(8,128)S(1)} convert(f16[64,1152]{1,0:T(8,128)(2,1)} %collective-permute-done) | non-fusion elementwise | flops 73728 | bytes 442368 | tf_op jit(solution)/shard_map/convert_element_type | solution.py:157
  39.5 0.0 collective-permute-done.2
  39.5 0.9 %convert_element_type.24 = f32[64,1152]{1,0:T(8,128)S(1)} convert(f16[64,1152]{1,0:T(8,128)(2,1)} %collective-permute-done.2) | non-fusion elementwise | flops 73728 | bytes 442368 | tf_op jit(solution)/shard_map/convert_element_type | solution.py:157
  40.5 0.0 collective-permute-done.1
  40.5 0.9 %convert_element_type.23 = f32[64,1152]{1,0:T(8,128)S(1)} convert(f16[64,1152]{1,0:T(8,128)(2,1)} %collective-permute-done.1) | non-fusion elementwise | flops 73728 | bytes 442368 | tf_op jit(solution)/shard_map/convert_element_type | solution.py:157
  41.4 0.1 add_add_fusion
  41.5 0.1 broadcast_in_dim.38
  41.7 0.1 broadcast_in_dim.32
  41.8 0.1 broadcast_in_dim.33
  41.9 0.1 broadcast_in_dim.34
  42.1 0.1 broadcast_in_dim.35
  42.2 0.1 broadcast_in_dim.36
  42.4 0.1 broadcast_in_dim.37
  42.5 1.0 %fusion.1 = bf16[64,1024]{1,0:T(8,128)(2,1)} fusion(f32[8,8,8,128]{3,2,1,0:T(8,128)S(1)} %bitcast.51, f32[8,8,8,128]{3,2,1,0:T(8,128)S(1)} %bitcast.57, f32[8,8,8,128]{3,2,1,0:T(8,128)S(1)} %bitcast.56, f32[8,8,8,128]{3,2,1,0:T(8,128)S(1)} %bitcast.55, f32[8,8,8,128]{3,2,1,0:T(8,128)S(1)} %bitcast.54, f32[8,8,8,128]{3,2,1,0:T(8,128)S(1)} %bitcast.53, ...), kind=kLoop, calls=%fused_computation.7 | loop fusion | flops 786432 | bytes 3276800 | tf_op jit(solution)/shard_map/convert_element_type | solution.py:233
  (4 shorter events, 0.1 us)
Async XLA Ops:
  0.7 22.5 %copy-start.2 = (bf16[1024,256]{1,0:T(8,128)(2,1)S(1)}, bf16[1024,256]{1,0:T(8,128)(2,1)}, u32[]{:S(2)}) copy-start(bf16[1024,256]{1,0:T(8,128)(2,1)} %v_ref.3) | copy-start | bytes 1572868
  1.7 21.4 %copy-start.1 = (bf16[1024,256]{1,0:T(8,128)(2,1)S(1)}, bf16[1024,256]{1,0:T(8,128)(2,1)}, u32[]{:S(2)}) copy-start(bf16[1024,256]{1,0:T(8,128)(2,1)} %k_ref.3) | copy-start | bytes 1572868
  26.8 5.4 %copy-start = (bf16[64,1024]{1,0:T(8,128)(2,1)S(1)}, bf16[64,1024]{1,0:T(8,128)(2,1)}, u32[]{:S(2)}) copy-start(bf16[64,1024]{1,0:T(8,128)(2,1)} %q_ref.1) | copy-start | bytes 393220
  27.5 11.0 %collective-permute-start = (f16[64,1152]{1,0:T(8,128)(2,1)}, f16[64,1152]{1,0:T(8,128)(2,1)}, u32[]{:S(2)}, u32[]{:S(2)}) collective-permute-start(f16[64,1152]{1,0:T(8,128)(2,1)} %get-tuple-element.14), channel_id=1, source_target_pairs={{0,2},{1,3},{2,0},{3,1},{4,6},{5,7},{6,4},{7,5},{8,10},{9,11},{10,... | collective-permute-start | bytes 442376 | tf_op jit(solution)/shard_map/ppermute | solution.py:153
  28.4 11.1 %collective-permute-start.2 = (f16[64,1152]{1,0:T(8,128)(2,1)S(1)}, f16[64,1152]{1,0:T(8,128)(2,1)}, u32[]{:S(2)}, u32[]{:S(2)}) collective-permute-start(f16[64,1152]{1,0:T(8,128)(2,1)S(1)} %get-tuple-element.15), channel_id=1, source_target_pairs={{0,1},{1,2},{2,3},{3,0},{4,5},{5,6},{6,7},{7,4},{8,9},{9,10},{10,1... | collective-permute-start | bytes 442376 | tf_op jit(solution)/shard_map/ppermute | solution.py:153
  29.8 10.7 %collective-permute-start.1 = (f16[64,1152]{1,0:T(8,128)(2,1)S(1)}, f16[64,1152]{1,0:T(8,128)(2,1)}, u32[]{:S(2)}, u32[]{:S(2)}) collective-permute-start(f16[64,1152]{1,0:T(8,128)(2,1)S(1)} %get-tuple-element.16), channel_id=1, source_target_pairs={{0,3},{1,0},{2,1},{3,2},{4,7},{5,4},{6,5},{7,6},{8,11},{9,8},{10,9... | collective-permute-start | bytes 442376 | tf_op jit(solution)/shard_map/ppermute | solution.py:153
  33.0 0.9 %copy-start.3 = (bf16[64,2,4,128]{3,2,1,0:T(4,128)(2,1)S(1)}, bf16[64,2,4,128]{3,2,1,0:T(4,128)(2,1)}, u32[]{:S(2)}) copy-start(bf16[64,2,4,128]{3,2,1,0:T(4,128)(2,1)} %reshape.94) | copy-start | bytes 393220
  33.0 0.7 %copy-start.4 = (s32[256]{0:T(256)S(1)}, s32[256]{0:T(256)}, u32[]{:S(2)}) copy-start(s32[256]{0:T(256)} %param.12) | copy-start | bytes 3076

commit v20 on v18

--- a/solution.py
+++ b/solution.py
@@ -110,6 +110,7 @@
         in_specs=in_specs,
         out_specs=pl.BlockSpec((block, out_cols), lambda i: (i, 0)),
         out_shape=jax.ShapeDtypeStruct((rows, out_cols), jnp.float32),
+        compiler_params=pltpu.CompilerParams(vmem_limit_bytes=8 * 1024 * 1024),
         cost_estimate=pl.CostEstimate(
             flops=4 * rows * cache_rows * qcols,
             transcendentals=rows * cache_rows * heads_q,

time: 45.5 us -> 43.7 us (0.960)
  Pallas kernels: 9.28 us -> 5.04 us
  waiting for transfers between devices: 0.01 us -> 1.82 us
  other arithmetic: 3.76 us -> 5.39 us
  local copies, waits for them, and re-layouts: 4.22 us -> 3.69 us
    pallas_call x2, Pallas kernels: 9.28 us -> 5.04 us  [cache_partials(): pl.pallas_call(functools.partial(cache_kernel, seq_count, first, pieces,...]
    convert_element_type x3, other arithmetic: 0.07 us -> 2.79 us  [on_device(): parts.append(lax.ppermute(to_half(piece, qcols, heads_q), 'seq', [(i, (i...]
    ppermute x3, waiting for transfers between devices: 0.01 us -> 1.82 us  [on_device(): lax.ppermute(to_half(piece, qcols, heads_q), 'seq', [(i, (i + shift) % se...]
    another operation x1, other arithmetic: 1.22 us -> 0.05 us
    slice x1, local copies, waits for them, and re-layouts: 0.99 us -> 0.02 us  [on_device(): all_values = gathered[:, qcols + kcols:]]
    unnamed x6 -> x10, local copies, waits for them, and re-layouts: 1.59 us -> 0.73 us
    slice x1, local copies, waits for them, and re-layouts: 0.08 us -> 0.73 us  [on_device(): piece = remote[(shift - 1) * own_count:shift * own_count]]
    reshape x1, local copies, waits for them, and re-layouts: 0.07 us -> 0.73 us  [on_device(): new_queries.reshape(own_count, heads_kv, group_size, head_size)]
  transfers between devices with their start and end apart: 3 -> 3, of which waited for: 0 -> 1; matrix products, arithmetic and copies ran while one was open for 6% -> 10% of each run, Pallas kernels for 8% -> 3%
where the time goes in v20:
time: 43.7 us; the launch traced here: 43.5 us
  blocking collectives  21.4 us (49%)
  other arithmetic  5.39 us (12%)
  Pallas kernels  5.04 us (12%)
  starting transfers between devices  4.65 us (11%)
  local copies, waits for them, and re-layouts  3.69 us (8%)
  waiting for transfers between devices  1.82 us (4%)
  between operations  0.87 us (2%)
  matrix products  0.62 us (1%)
    all_gather x1, blocking collectives, on_device(): gathered = lax.all_gather(packed, 'seq', axis=0, tiled=True)  21.4 us
    pallas_call x2, Pallas kernels, cache_partials(): pl.pallas_call(functools.partial(cache_kernel, seq_count, first, pieces,...  5.04 us
    ppermute x3, starting transfers between devices, on_device(): lax.ppermute(to_half(piece, qcols, heads_q), 'seq', [(i, (i + shift) % se...  4.65 us
    convert_element_type x3, other arithmetic, on_device(): parts.append(lax.ppermute(to_half(piece, qcols, heads_q), 'seq', [(i, (i...  2.79 us
    ppermute x3, waiting for transfers between devices, on_device(): lax.ppermute(to_half(piece, qcols, heads_q), 'seq', [(i, (i + shift) % se...  1.82 us
    convert_element_type x1, other arithmetic, on_device(): return attended.astype(jnp.bfloat16)  1.02 us
    concatenate x1, other arithmetic, on_device(): packed = jnp.concatenate([new_queries, new_keys, new_values], axis=1)  1.02 us
    broadcast_in_dim x7, local copies, waits for them, and re-layouts, spread(): jnp.broadcast_to(x[:, :, None], (own_count, heads_q, head_size))  0.88 us
  transfers between devices with their start and end apart: 3, of which 1 were waited for; matrix products, arithmetic and copies ran while one was open for 10% of the time, Pallas kernels for 3%

profile of v20, /device:TPU:0, one launch (start us, length us, event | category | flops | bytes accessed | tf_op | source)
XLA Modules:
  0.0 43.5 jit_solution(17440933298966638944)
XLA Ops:
  0.7 0.0 copy-start.2
  0.7 1.0 %pad_maximum_fusion = bf16[64,1536]{1,0:T(8,128)(2,1)S(1)} fusion(bf16[64,256]{1,0:T(8,128)(2,1)} %param.9, bf16[64,256]{1,0:T(8,128)(2,1)} %param.8, bf16[64,1024]{1,0:T(8,128)(2,1)} %q_ref.1), kind=kLoop, calls=%fused_computation.18 | loop fusion | flops 589824 | bytes 393216 | tf_op jit(solution)/shard_map/concatenate | solution.py:138
  1.7 0.0 copy-start.1
  1.7 21.4 %all_gather.3.q_ref = bf16[256,1536]{1,0:T(8,128)(2,1)S(1)} all-gather(bf16[64,1536]{1,0:T(8,128)(2,1)S(1)} %pad_maximum_fusion), channel_id=1, replica_groups=mesh['group'=2,'head'=4,'seq'=4] {'seq'}, dimensions={0}, use_global_device_ids=true | all-gather | bytes 983040 | tf_op jit(solution)/shard_map/all_gather | solution.py:139
  23.1 0.0 copy-done.2
  23.1 0.0 copy-done.1
  23.1 3.6 %shard_map.73.rest_0_ = f32[192,1152]{1,0:T(8,128)S(1)} custom-call(s32[1]{0:T(128)S(6)} %copy.57.len_ref, bf16[256,1536]{1,0:T(8,128)(2,1)S(1)} %all_gather.3.q_ref, bf16[1024,256]{1,0:T(8,128)(2,1)S(1)} %copy-done.1, bf16[1024,256]{1,0:T(8,128)(2,1)S(1)} %copy-done.2), custom_call_target="tpu_custom_call" | custom-call | flops 805306368 | bytes 2326528 | tf_op jit(solution)/shard_map/pallas_call | solution.py:107
  26.7 0.1 convert.5
  26.8 0.0 copy-start
  26.8 0.7 %fusion.20 = (f16[64,1152]{1,0:T(8,128)(2,1)}, f16[64,1152]{1,0:T(8,128)(2,1)S(1)}, f16[64,1152]{1,0:T(8,128)(2,1)S(1)}) fusion(f16[192,1152]{1,0:T(8,128)(2,1)S(1)} %convert.5), kind=kLoop, calls=%fused_computation.40 | loop fusion | bytes 884736 | tf_op jit(solution)/shard_map/slice | solution.py:151
  27.5 0.8 %collective-permute-start = (f16[64,1152]{1,0:T(8,128)(2,1)}, f16[64,1152]{1,0:T(8,128)(2,1)}, u32[]{:S(2)}, u32[]{:S(2)}) collective-permute-start(f16[64,1152]{1,0:T(8,128)(2,1)} %get-tuple-element.14), channel_id=1, source_target_pairs={{0,2},{1,3},{2,0},{3,1},{4,6},{5,7},{6,4},{7,5},{8,10},{9,11},{10,... | collective-permute-start | bytes 442376 | tf_op jit(solution)/shard_map/ppermute | solution.py:153
  28.4 1.4 %collective-permute-start.2 = (f16[64,1152]{1,0:T(8,128)(2,1)S(1)}, f16[64,1152]{1,0:T(8,128)(2,1)}, u32[]{:S(2)}, u32[]{:S(2)}) collective-permute-start(f16[64,1152]{1,0:T(8,128)(2,1)S(1)} %get-tuple-element.15), channel_id=1, source_target_pairs={{0,1},{1,2},{2,3},{3,0},{4,5},{5,6},{6,7},{7,4},{8,9},{9,10},{10,1... | collective-permute-start | bytes 442376 | tf_op jit(solution)/shard_map/ppermute | solution.py:153
  29.8 2.4 %collective-permute-start.1 = (f16[64,1152]{1,0:T(8,128)(2,1)S(1)}, f16[64,1152]{1,0:T(8,128)(2,1)}, u32[]{:S(2)}, u32[]{:S(2)}) collective-permute-start(f16[64,1152]{1,0:T(8,128)(2,1)S(1)} %get-tuple-element.16), channel_id=1, source_target_pairs={{0,3},{1,0},{2,1},{3,2},{4,7},{5,4},{6,5},{7,6},{8,11},{9,8},{10,9... | collective-permute-start | bytes 442376 | tf_op jit(solution)/shard_map/ppermute | solution.py:153
  32.2 0.0 copy-done
  32.2 0.7 %reshape.94 = bf16[64,2,4,128]{3,2,1,0:T(4,128)(2,1)} reshape(bf16[64,1024]{1,0:T(8,128)(2,1)S(1)} %copy-done) | data formatting | bytes 262144 | tf_op jit(solution)/shard_map/reshape | solution.py:178
  33.0 0.0 copy-start.3
  33.0 0.0 copy-start.4
  33.1 0.7 %copy-done.4 = s32[256]{0:T(256)S(1)} copy-done((s32[256]{0:T(256)S(1)}, s32[256]{0:T(256)}, u32[]{:S(2)}) %copy-start.4) | copy-done | bytes 1048
  33.8 0.1 dynamic_slice.3
  33.8 0.1 fusion.9
  33.9 0.0 copy-done.3
  33.9 0.3 select_reduce_fusion
  34.3 0.3 convolution_bitcast_fusion
  34.6 0.2 copy.23
  34.7 0.1 reshape.95
  34.9 0.3 convert_reduce_fusion
  35.1 0.1 copy.26
  35.2 0.1 copy.25
  35.3 1.4 %shard_map.74 = f32[64,1152]{1,0:T(8,128)S(1)} custom-call(s32[1]{0:T(128)S(6)} %copy.57.len_ref, bf16[64,1024]{1,0:T(8,128)(2,1)S(1)} %copy-done, bf16[1024,256]{1,0:T(8,128)(2,1)S(1)} %copy-done.1, bf16[1024,256]{1,0:T(8,128)(2,1)S(1)} %copy-done.2, f32[192,1152]{1,0:T(8,128)S(1)} %shard_map.73.rest_0_), custom_call_target="tpu_custom_call" | custom-call | flops 268435456 | bytes 1474560 | tf_op jit(solution)/shard_map/pallas_call | solution.py:107
  36.8 1.8 %collective-permute-done = f16[64,1152]{1,0:T(8,128)(2,1)} collective-permute-done((f16[64,1152]{1,0:T(8,128)(2,1)}, f16[64,1152]{1,0:T(8,128)(2,1)}, u32[]{:S(2)}, u32[]{:S(2)}) %collective-permute-start) | collective-permute-done | bytes 147488 | tf_op jit(solution)/shard_map/ppermute | solution.py:153
  38.6 0.9 %convert_element_type.22 = f32[64,1152]{1,0:T(8,128)S(1)} convert(f16[64,1152]{1,0:T(8,128)(2,1)} %collective-permute-done) | non-fusion elementwise | flops 73728 | bytes 442368 | tf_op jit(solution)/shard_map/convert_element_type | solution.py:157
  39.5 0.0 collective-permute-done.2
  39.5 0.9 %convert_element_type.24 = f32[64,1152]{1,0:T(8,128)S(1)} convert(f16[64,1152]{1,0:T(8,128)(2,1)} %collective-permute-done.2) | non-fusion elementwise | flops 73728 | bytes 442368 | tf_op jit(solution)/shard_map/convert_element_type | solution.py:157
  40.5 0.0 collective-permute-done.1
  40.5 0.9 %convert_element_type.23 = f32[64,1152]{1,0:T(8,128)S(1)} convert(f16[64,1152]{1,0:T(8,128)(2,1)} %collective-permute-done.1) | non-fusion elementwise | flops 73728 | bytes 442368 | tf_op jit(solution)/shard_map/convert_element_type | solution.py:157
  41.4 0.1 add_add_fusion
  41.5 0.1 broadcast_in_dim.38
  41.7 0.1 broadcast_in_dim.32
  41.8 0.1 broadcast_in_dim.33
  41.9 0.1 broadcast_in_dim.34
  42.1 0.1 broadcast_in_dim.35
  42.2 0.1 broadcast_in_dim.36
  42.4 0.1 broadcast_in_dim.37
  42.5 1.0 %fusion.1 = bf16[64,1024]{1,0:T(8,128)(2,1)} fusion(f32[8,8,8,128]{3,2,1,0:T(8,128)S(1)} %bitcast.51, f32[8,8,8,128]{3,2,1,0:T(8,128)S(1)} %bitcast.57, f32[8,8,8,128]{3,2,1,0:T(8,128)S(1)} %bitcast.56, f32[8,8,8,128]{3,2,1,0:T(8,128)S(1)} %bitcast.55, f32[8,8,8,128]{3,2,1,0:T(8,128)S(1)} %bitcast.54, f32[8,8,8,128]{3,2,1,0:T(8,128)S(1)} %bitcast.53, ...), kind=kLoop, calls=%fused_computation.7 | loop fusion | flops 786432 | bytes 3276800 | tf_op jit(solution)/shard_map/convert_element_type | solution.py:233
  (4 shorter events, 0.1 us)
Async XLA Ops:
  0.7 22.5 %copy-start.2 = (bf16[1024,256]{1,0:T(8,128)(2,1)S(1)}, bf16[1024,256]{1,0:T(8,128)(2,1)}, u32[]{:S(2)}) copy-start(bf16[1024,256]{1,0:T(8,128)(2,1)} %v_ref.3) | copy-start | bytes 1572868
  1.7 21.4 %copy-start.1 = (bf16[1024,256]{1,0:T(8,128)(2,1)S(1)}, bf16[1024,256]{1,0:T(8,128)(2,1)}, u32[]{:S(2)}) copy-start(bf16[1024,256]{1,0:T(8,128)(2,1)} %k_ref.3) | copy-start | bytes 1572868
  26.8 5.4 %copy-start = (bf16[64,1024]{1,0:T(8,128)(2,1)S(1)}, bf16[64,1024]{1,0:T(8,128)(2,1)}, u32[]{:S(2)}) copy-start(bf16[64,1024]{1,0:T(8,128)(2,1)} %q_ref.1) | copy-start | bytes 393220
  27.5 11.0 %collective-permute-start = (f16[64,1152]{1,0:T(8,128)(2,1)}, f16[64,1152]{1,0:T(8,128)(2,1)}, u32[]{:S(2)}, u32[]{:S(2)}) collective-permute-start(f16[64,1152]{1,0:T(8,128)(2,1)} %get-tuple-element.14), channel_id=1, source_target_pairs={{0,2},{1,3},{2,0},{3,1},{4,6},{5,7},{6,4},{7,5},{8,10},{9,11},{10,... | collective-permute-start | bytes 442376 | tf_op jit(solution)/shard_map/ppermute | solution.py:153
  28.4 11.1 %collective-permute-start.2 = (f16[64,1152]{1,0:T(8,128)(2,1)S(1)}, f16[64,1152]{1,0:T(8,128)(2,1)}, u32[]{:S(2)}, u32[]{:S(2)}) collective-permute-start(f16[64,1152]{1,0:T(8,128)(2,1)S(1)} %get-tuple-element.15), channel_id=1, source_target_pairs={{0,1},{1,2},{2,3},{3,0},{4,5},{5,6},{6,7},{7,4},{8,9},{9,10},{10,1... | collective-permute-start | bytes 442376 | tf_op jit(solution)/shard_map/ppermute | solution.py:153
  29.8 10.7 %collective-permute-start.1 = (f16[64,1152]{1,0:T(8,128)(2,1)S(1)}, f16[64,1152]{1,0:T(8,128)(2,1)}, u32[]{:S(2)}, u32[]{:S(2)}) collective-permute-start(f16[64,1152]{1,0:T(8,128)(2,1)S(1)} %get-tuple-element.16), channel_id=1, source_target_pairs={{0,3},{1,0},{2,1},{3,2},{4,7},{5,4},{6,5},{7,6},{8,11},{9,8},{10,9... | collective-permute-start | bytes 442376 | tf_op jit(solution)/shard_map/ppermute | solution.py:153
  33.0 0.9 %copy-start.3 = (bf16[64,2,4,128]{3,2,1,0:T(4,128)(2,1)S(1)}, bf16[64,2,4,128]{3,2,1,0:T(4,128)(2,1)}, u32[]{:S(2)}) copy-start(bf16[64,2,4,128]{3,2,1,0:T(4,128)(2,1)} %reshape.94) | copy-start | bytes 393220
  33.0 0.7 %copy-start.4 = (s32[256]{0:T(256)S(1)}, s32[256]{0:T(256)}, u32[]{:S(2)}) copy-start(s32[256]{0:T(256)} %param.12) | copy-start | bytes 3076

commit v21 on v19

--- a/solution.py
+++ b/solution.py
@@ -154,7 +154,7 @@
                     to_half(piece, qcols, heads_q),
                     "seq",
                     [(i, (i + shift) % seq_count) for i in range(seq_count)],
-                ).astype(jnp.float32)
+                )
             )
         own = cache_partials(
             cache_length, new_queries, cache_keys, cache_values, qcols,
@@ -169,11 +169,13 @@
         recv = lax.all_to_all(to_half(partial, qcols, heads_q), "seq", 0, 0, tiled=True)
         recv = recv.astype(jnp.float32)
         parts = [recv[j * own_count:(j + 1) * own_count] for j in range(seq_count)]
-    part_mean = [p[:, :qcols] for p in parts]
+    part_mean = [p[:, :qcols].astype(jnp.float32) for p in parts]
     part_denom = [
-        p[:, qcols:qcols + heads_q] + p[:, qcols + heads_q:qcols + 2 * heads_q] for p in parts
+        p[:, qcols:qcols + heads_q].astype(jnp.float32)
+        + p[:, qcols + heads_q:qcols + 2 * heads_q].astype(jnp.float32)
+        for p in parts
     ]
-    part_max = [p[:, qcols + 2 * heads_q:qcols + 3 * heads_q] for p in parts]
+    part_max = [p[:, qcols + 2 * heads_q:qcols + 3 * heads_q].astype(jnp.float32) for p in parts]
 
     own_queries = new_queries.reshape(own_count, heads_kv, group_size, head_size)
     fresh_scores = (

time: 43.7 us -> 43.7 us (level)
  other arithmetic: 5.39 us -> 4.34 us
  waiting for transfers between devices: 1.82 us -> 2.83 us
    convert_element_type x3 -> x0, other arithmetic: 2.79 us -> none  [on_device(): parts.append(lax.ppermute(to_half(piece, qcols, heads_q), 'seq', [(i, (i...]
    ppermute x3, waiting for transfers between devices: 1.82 us -> 2.83 us  [on_device(): lax.ppermute(to_half(piece, qcols, heads_q), 'seq', [(i, (i + shift) % se...]
    convert_element_type x1, other arithmetic: 1.02 us -> 1.92 us  [on_device(): return attended.astype(jnp.bfloat16)]
    add x1, other arithmetic: 0.14 us -> 0.98 us  [on_device(): total_denom = total_denom + w_j]
  transfers between devices with their start and end apart: 3 -> 3, of which waited for: 1 -> 2; matrix products, arithmetic and copies ran while one was open for 10% -> 5% of each run, Pallas kernels for 3% -> 3%
where the time goes in v21:
time: 43.7 us; the launch traced here: 43.5 us
  blocking collectives  21.4 us (49%)
  Pallas kernels  5.04 us (12%)
  starting transfers between devices  4.65 us (11%)
  other arithmetic  4.34 us (10%)
  local copies, waits for them, and re-layouts  3.75 us (9%)
  waiting for transfers between devices  2.83 us (6%)
  between operations  0.84 us (2%)
  matrix products  0.62 us (1%)
    all_gather x1, blocking collectives, on_device(): gathered = lax.all_gather(packed, 'seq', axis=0, tiled=True)  21.4 us
    pallas_call x2, Pallas kernels, cache_partials(): pl.pallas_call(functools.partial(cache_kernel, seq_count, first, pieces,...  5.04 us
    ppermute x3, starting transfers between devices, on_device(): lax.ppermute(to_half(piece, qcols, heads_q), 'seq', [(i, (i + shift) % se...  4.65 us
    ppermute x3, waiting for transfers between devices, on_device(): lax.ppermute(to_half(piece, qcols, heads_q), 'seq', [(i, (i + shift) % se...  2.83 us
    convert_element_type x1, other arithmetic, on_device(): return attended.astype(jnp.bfloat16)  1.92 us
    concatenate x1, other arithmetic, on_device(): packed = jnp.concatenate([new_queries, new_keys, new_values], axis=1)  1.02 us
    add x1, other arithmetic, on_device(): total_denom = total_denom + w_j  0.98 us
    broadcast_in_dim x7, local copies, waits for them, and re-layouts, spread(): jnp.broadcast_to(x[:, :, None], (own_count, heads_q, head_size))  0.88 us
  transfers between devices with their start and end apart: 3, of which 2 were waited for; matrix products, arithmetic and copies ran while one was open for 5% of the time, Pallas kernels for 3%

profile of v21, /device:TPU:0, one launch (start us, length us, event | category | flops | bytes accessed | tf_op | source)
XLA Modules:
  0.0 43.5 jit_solution(16903103188988186441)
XLA Ops:
  0.7 0.0 copy-start.2
  0.7 1.0 %pad_maximum_fusion = bf16[64,1536]{1,0:T(8,128)(2,1)S(1)} fusion(bf16[64,256]{1,0:T(8,128)(2,1)} %param.9, bf16[64,256]{1,0:T(8,128)(2,1)} %param.8, bf16[64,1024]{1,0:T(8,128)(2,1)} %q_ref.1), kind=kLoop, calls=%fused_computation.18 | loop fusion | flops 589824 | bytes 393216 | tf_op jit(solution)/shard_map/concatenate | solution.py:138
  1.7 0.0 copy-start.1
  1.7 21.4 %all_gather.3.q_ref = bf16[256,1536]{1,0:T(8,128)(2,1)S(1)} all-gather(bf16[64,1536]{1,0:T(8,128)(2,1)S(1)} %pad_maximum_fusion), channel_id=1, replica_groups=mesh['group'=2,'head'=4,'seq'=4] {'seq'}, dimensions={0}, use_global_device_ids=true | all-gather | bytes 983040 | tf_op jit(solution)/shard_map/all_gather | solution.py:139
  23.1 0.0 copy-done.2
  23.1 0.0 copy-done.1
  23.1 3.6 %shard_map.73.rest_0_ = f32[192,1152]{1,0:T(8,128)S(1)} custom-call(s32[1]{0:T(128)S(6)} %copy.57.len_ref, bf16[256,1536]{1,0:T(8,128)(2,1)S(1)} %all_gather.3.q_ref, bf16[1024,256]{1,0:T(8,128)(2,1)S(1)} %copy-done.1, bf16[1024,256]{1,0:T(8,128)(2,1)S(1)} %copy-done.2), custom_call_target="tpu_custom_call" | custom-call | flops 805306368 | bytes 2326528 | tf_op jit(solution)/shard_map/pallas_call | solution.py:107
  26.7 0.1 convert.5
  26.8 0.0 copy-start
  26.8 0.8 %fusion.23 = (f16[64,1152]{1,0:T(8,128)(2,1)}, f16[64,1152]{1,0:T(8,128)(2,1)}, f16[64,1152]{1,0:T(8,128)(2,1)}) fusion(f16[192,1152]{1,0:T(8,128)(2,1)S(1)} %convert.5), kind=kLoop, calls=%fused_computation.45 | loop fusion | bytes 884736 | tf_op jit(solution)/shard_map/slice | solution.py:151
  27.6 0.8 %collective-permute-start = (f16[64,1152]{1,0:T(8,128)(2,1)}, f16[64,1152]{1,0:T(8,128)(2,1)S(1)}, u32[]{:S(2)}, u32[]{:S(2)}) collective-permute-start(f16[64,1152]{1,0:T(8,128)(2,1)} %get-tuple-element.14), channel_id=1, source_target_pairs={{0,2},{1,3},{2,0},{3,1},{4,6},{5,7},{6,4},{7,5},{8,10},{9,11},{10,... | collective-permute-start | bytes 442376 | tf_op jit(solution)/shard_map/ppermute | solution.py:153
  28.4 1.4 %collective-permute-start.2 = (f16[64,1152]{1,0:T(8,128)(2,1)}, f16[64,1152]{1,0:T(8,128)(2,1)S(1)}, u32[]{:S(2)}, u32[]{:S(2)}) collective-permute-start(f16[64,1152]{1,0:T(8,128)(2,1)} %get-tuple-element.15), channel_id=1, source_target_pairs={{0,1},{1,2},{2,3},{3,0},{4,5},{5,6},{6,7},{7,4},{8,9},{9,10},{10,1... | collective-permute-start | bytes 442376 | tf_op jit(solution)/shard_map/ppermute | solution.py:153
  29.9 2.4 %collective-permute-start.1 = (f16[64,1152]{1,0:T(8,128)(2,1)}, f16[64,1152]{1,0:T(8,128)(2,1)}, u32[]{:S(2)}, u32[]{:S(2)}) collective-permute-start(f16[64,1152]{1,0:T(8,128)(2,1)} %get-tuple-element.16), channel_id=1, source_target_pairs={{0,3},{1,0},{2,1},{3,2},{4,7},{5,4},{6,5},{7,6},{8,11},{9,8},{10,9... | collective-permute-start | bytes 442376 | tf_op jit(solution)/shard_map/ppermute | solution.py:153
  32.2 0.0 copy-done
  32.3 0.7 %reshape.94 = bf16[64,2,4,128]{3,2,1,0:T(4,128)(2,1)} reshape(bf16[64,1024]{1,0:T(8,128)(2,1)S(1)} %copy-done) | data formatting | bytes 262144 | tf_op jit(solution)/shard_map/reshape | solution.py:180
  33.1 0.0 copy-start.3
  33.1 0.0 copy-start.4
  33.1 0.7 %copy-done.4 = s32[256]{0:T(256)S(1)} copy-done((s32[256]{0:T(256)S(1)}, s32[256]{0:T(256)}, u32[]{:S(2)}) %copy-start.4) | copy-done | bytes 1048
  33.8 0.1 dynamic_slice.3
  33.9 0.1 fusion.9
  34.0 0.0 copy-done.3
  34.0 0.3 select_reduce_fusion
  34.3 0.3 convolution_bitcast_fusion
  34.6 0.2 copy.23
  34.8 0.1 reshape.95
  34.9 0.3 convert_reduce_fusion
  35.2 0.1 copy.26
  35.3 0.1 copy.25
  35.4 1.4 %shard_map.74 = f32[64,1152]{1,0:T(8,128)S(1)} custom-call(s32[1]{0:T(128)S(6)} %copy.57.len_ref, bf16[64,1024]{1,0:T(8,128)(2,1)S(1)} %copy-done, bf16[1024,256]{1,0:T(8,128)(2,1)S(1)} %copy-done.1, bf16[1024,256]{1,0:T(8,128)(2,1)S(1)} %copy-done.2, f32[192,1152]{1,0:T(8,128)S(1)} %shard_map.73.rest_0_), custom_call_target="tpu_custom_call" | custom-call | flops 268435456 | bytes 1474560 | tf_op jit(solution)/shard_map/pallas_call | solution.py:107
  36.8 1.7 %collective-permute-done = f16[64,1152]{1,0:T(8,128)(2,1)S(1)} collective-permute-done((f16[64,1152]{1,0:T(8,128)(2,1)}, f16[64,1152]{1,0:T(8,128)(2,1)S(1)}, u32[]{:S(2)}, u32[]{:S(2)}) %collective-permute-start) | collective-permute-done | bytes 147488 | tf_op jit(solution)/shard_map/ppermute | solution.py:153
  38.5 0.0 collective-permute-done.2
  38.5 1.1 %collective-permute-done.1 = f16[64,1152]{1,0:T(8,128)(2,1)} collective-permute-done((f16[64,1152]{1,0:T(8,128)(2,1)}, f16[64,1152]{1,0:T(8,128)(2,1)}, u32[]{:S(2)}, u32[]{:S(2)}) %collective-permute-start.1) | collective-permute-done | bytes 147488 | tf_op jit(solution)/shard_map/ppermute | solution.py:153
  39.7 1.0 %add_add_fusion = (f32[64,8]{1,0:T(8,128)S(1)}, f32[64,8]{1,0:T(8,128)S(1)}, f32[64,8]{1,0:T(8,128)S(1)}, f32[64,8]{1,0:T(8,128)S(1)}, f32[64,8]{1,0:T(8,128)S(1)}, /*index=5*/f32[64,8]{1,0:T(8,128)S(1)}, f32[64,8]{1,0:T(8,128)S(1)}) fusion(f32[64,8]{1,0:T(8,128)S(1)} %copy.26, f32[64,8]{1,0:T(8,128)S(1)} %copy.25, f32[64,1152]{1,0:T(8,128)S(1)} %shard_map.74, ...), kind=kLoop, calls=%fused_computation.38 | loop fusion | flops 16896 | bytes 33792 | tf_op jit(solution)/shard_map/add | solution.py:233
  40.6 0.1 broadcast_in_dim.38
  40.8 0.1 broadcast_in_dim.32
  40.9 0.1 broadcast_in_dim.33
  41.0 0.1 broadcast_in_dim.34
  41.2 0.1 broadcast_in_dim.35
  41.3 0.1 broadcast_in_dim.36
  41.4 0.1 broadcast_in_dim.37
  41.6 1.9 %fusion.1 = bf16[64,1024]{1,0:T(8,128)(2,1)} fusion(f32[8,8,8,128]{3,2,1,0:T(8,128)S(1)} %bitcast.51, f32[8,8,8,128]{3,2,1,0:T(8,128)S(1)} %bitcast.57, f32[8,8,8,128]{3,2,1,0:T(8,128)S(1)} %bitcast.56, f32[8,8,8,128]{3,2,1,0:T(8,128)S(1)} %bitcast.55, f32[8,8,8,128]{3,2,1,0:T(8,128)S(1)} %bitcast.54, f32[8,8,8,128]{3,2,1,0:T(8,128)S(1)} %bitcast.53, ...), kind=kLoop, calls=%fused_computation.7 | loop fusion | flops 983040 | bytes 2883584 | tf_op jit(solution)/shard_map/convert_element_type | solution.py:235
  (4 shorter events, 0.1 us)
Async XLA Ops:
  0.7 22.5 %copy-start.2 = (bf16[1024,256]{1,0:T(8,128)(2,1)S(1)}, bf16[1024,256]{1,0:T(8,128)(2,1)}, u32[]{:S(2)}) copy-start(bf16[1024,256]{1,0:T(8,128)(2,1)} %v_ref.3) | copy-start | bytes 1572868
  1.7 21.4 %copy-start.1 = (bf16[1024,256]{1,0:T(8,128)(2,1)S(1)}, bf16[1024,256]{1,0:T(8,128)(2,1)}, u32[]{:S(2)}) copy-start(bf16[1024,256]{1,0:T(8,128)(2,1)} %k_ref.3) | copy-start | bytes 1572868
  26.8 5.5 %copy-start = (bf16[64,1024]{1,0:T(8,128)(2,1)S(1)}, bf16[64,1024]{1,0:T(8,128)(2,1)}, u32[]{:S(2)}) copy-start(bf16[64,1024]{1,0:T(8,128)(2,1)} %q_ref.1) | copy-start | bytes 393220
  27.6 10.9 %collective-permute-start = (f16[64,1152]{1,0:T(8,128)(2,1)}, f16[64,1152]{1,0:T(8,128)(2,1)S(1)}, u32[]{:S(2)}, u32[]{:S(2)}) collective-permute-start(f16[64,1152]{1,0:T(8,128)(2,1)} %get-tuple-element.14), channel_id=1, source_target_pairs={{0,2},{1,3},{2,0},{3,1},{4,6},{5,7},{6,4},{7,5},{8,10},{9,11},{10,... | collective-permute-start | bytes 442376 | tf_op jit(solution)/shard_map/ppermute | solution.py:153
  28.4 10.1 %collective-permute-start.2 = (f16[64,1152]{1,0:T(8,128)(2,1)}, f16[64,1152]{1,0:T(8,128)(2,1)S(1)}, u32[]{:S(2)}, u32[]{:S(2)}) collective-permute-start(f16[64,1152]{1,0:T(8,128)(2,1)} %get-tuple-element.15), channel_id=1, source_target_pairs={{0,1},{1,2},{2,3},{3,0},{4,5},{5,6},{6,7},{7,4},{8,9},{9,10},{10,1... | collective-permute-start | bytes 442376 | tf_op jit(solution)/shard_map/ppermute | solution.py:153
  29.9 9.8 %collective-permute-start.1 = (f16[64,1152]{1,0:T(8,128)(2,1)}, f16[64,1152]{1,0:T(8,128)(2,1)}, u32[]{:S(2)}, u32[]{:S(2)}) collective-permute-start(f16[64,1152]{1,0:T(8,128)(2,1)} %get-tuple-element.16), channel_id=1, source_target_pairs={{0,3},{1,0},{2,1},{3,2},{4,7},{5,4},{6,5},{7,6},{8,11},{9,8},{10,9... | collective-permute-start | bytes 442376 | tf_op jit(solution)/shard_map/ppermute | solution.py:153
  33.1 0.9 %copy-start.3 = (bf16[64,2,4,128]{3,2,1,0:T(4,128)(2,1)S(1)}, bf16[64,2,4,128]{3,2,1,0:T(4,128)(2,1)}, u32[]{:S(2)}) copy-start(bf16[64,2,4,128]{3,2,1,0:T(4,128)(2,1)} %reshape.94) | copy-start | bytes 393220
  33.1 0.7 %copy-start.4 = (s32[256]{0:T(256)S(1)}, s32[256]{0:T(256)}, u32[]{:S(2)}) copy-start(s32[256]{0:T(256)} %param.12) | copy-start | bytes 3076
